TPU v7x, 768 devices: a whole 4x8x12 slice. The times are simulated.
768 devices in a mesh: dp: 24 (over x, z_hi, core), section: 8 (over y), mp: 4 (over z_lo).
Axes of the slice: x: 4, y: 8, z: 12 (z_hi: 3, z_lo: 4; z = z_hi * 4 + z_lo), core: 2. Of those that a mesh axis runs over, the one named last changes fastest.
Arguments:
- patch_features_window: bfloat16 [768, 729, 1152], P(('dp', 'section', 'mp')), may hold values from -2048 to 2048
- probe_request_heads: bfloat16 [1152], replicated, may hold values from -6 to 6
- lookup_projection: bfloat16 [1152, 1152], replicated, may hold values from -0.1875 to 0.1875
- content_projection: bfloat16 [1152, 1152], replicated, may hold values from -0.1875 to 0.1875
- final_projection: bfloat16 [1152, 1152], replicated, may hold values from -0.1875 to 0.1875
- prior_picture_entries: bfloat16 [23808, 1152], P(('dp', 'section', 'mp')), may hold values from -6 to 6
- caption_features: bfloat16 [24576, 1152], P(('dp', 'section', 'mp')), may hold values from -0.1875 to 0.1875
- partner_indices: int32 [24576], replicated, may hold values from 0 to 24575, each once
- score_scale_param: float32 [1], replicated, may hold values from 5 to 20
- score_shift: float32 [1], replicated, may hold values from -7.5 to -5.5
Outputs:
- losses: float32 [24576], P(('dp', 'section', 'mp'))
- text_grad: float32 [24576, 1152], P(('dp', 'section', 'mp'))
Inputs may be any that keep to these rules, and one draw needn't show every extreme that they name: `partner_indices`: every text is the positive partner of exactly one image.
All inputs are finite; a program needn't handle non-finite values.
Results may differ from a plain program's by a relative error of at most 0.0046.
Values may be sent and summed in bfloat16 or wider, within the bound.
No kernel may reach another device: no remote copies, remote signals or barrier semaphores. Data moves between devices by JAX's collectives and lax.ppermute only.
A program may use at most 64 MiB of HBM per device.

v0:
```python
import math

import jax
import jax.numpy as jnp
from jax import lax
from jax.sharding import PartitionSpec as P

HEADS = 16
HD = 72


def pool_image(
    patch_rows, probe_request_heads, lookup_projection, content_projection, final_projection
):
    width = lookup_projection.shape[0]
    key_probe = jnp.einsum(
        "dhe,he->dh",
        lookup_projection.reshape(width, HEADS, HD),
        probe_request_heads.reshape(HEADS, HD),
        preferred_element_type=jnp.float32,
    )
    key_probe = (key_probe / math.sqrt(HD)).astype(jnp.bfloat16)
    scores = jnp.dot(patch_rows, key_probe, preferred_element_type=jnp.float32)
    highest = jnp.max(scores, axis=0, keepdims=True)
    exponent = jnp.exp(scores - highest)
    weights = (exponent / jnp.sum(exponent, axis=0, keepdims=True)).astype(jnp.bfloat16)
    pooled_patch = lax.dot_general(
        weights, patch_rows, (((0,), (0,)), ((), ())), preferred_element_type=jnp.float32
    ).astype(jnp.bfloat16)
    values = jnp.einsum(
        "hd,dhe->he",
        pooled_patch,
        content_projection.reshape(width, HEADS, HD),
        preferred_element_type=jnp.float32,
    )
    values = values.astype(jnp.bfloat16).reshape(1, width)
    return jnp.dot(values, final_projection, preferred_element_type=jnp.float32).astype(
        jnp.bfloat16
    )


def normalize_rows(rows_in):
    widened = rows_in.astype(jnp.float32)
    inverse = lax.rsqrt(jnp.sum(widened * widened, axis=1, keepdims=True) + 1e-06)
    return (widened * inverse, inverse)


def block_contributions(
    picture_tile,
    target_tile,
    device_portion_count,
    overall_column_indices,
    score_scaling,
    starting_position,
):
    pair_scores = (
        score_scaling
        * lax.dot_general(
            picture_tile,
            device_portion_count,
            (((1,), (1,)), ((), ())),
            preferred_element_type=jnp.float32,
        )
        + starting_position
    )
    matching_flag = target_tile[:, None] == overall_column_indices[None, :]
    row_losses = jnp.sum(
        jax.nn.softplus(jnp.where(matching_flag, -pair_scores, pair_scores)), axis=1
    )
    sigmoid_derivatives = (
        (jax.nn.sigmoid(pair_scores) - matching_flag.astype(jnp.float32)) * score_scaling
    ).astype(jnp.bfloat16)
    grad_terms = lax.dot_general(
        sigmoid_derivatives,
        picture_tile,
        (((0,), (0,)), ((), ())),
        preferred_element_type=jnp.float32,
    )
    return (row_losses, grad_terms)


def local(
    patch_features_window,
    probe_request_heads,
    lookup_projection,
    content_projection,
    final_projection,
    prior_picture_entries,
    caption_features,
    partner_indices,
    score_scale_param,
    score_shift,
):
    row_count = caption_features.shape[0]
    inner_size = lax.axis_size(("section", "mp"))
    inner_pos = lax.axis_index(("section", "mp"))
    outer_pos = lax.axis_index("dp")
    score_scaling = score_scale_param[0]
    starting_position = score_shift[0]
    pooled = pool_image(
        patch_features_window[0],
        probe_request_heads,
        lookup_projection,
        content_projection,
        final_projection,
    )
    own_images = jnp.concatenate([pooled, prior_picture_entries], axis=0)
    image_norm = normalize_rows(own_images)[0].astype(jnp.bfloat16)
    text_unit, text_inverse = normalize_rows(caption_features)
    caption_magnitude = text_unit.astype(jnp.bfloat16)
    picture_tile = lax.all_gather(image_norm, ("section", "mp"), axis=0, tiled=True)
    target_tile = lax.dynamic_slice_in_dim(
        partner_indices, outer_pos * (inner_size * row_count), inner_size * row_count
    )
    device_portion_count = lax.all_gather(caption_magnitude, "dp", axis=0, tiled=True)
    text_cols = jnp.arange(device_portion_count.shape[0], dtype=jnp.int32)
    overall_column_indices = (
        text_cols // row_count * (inner_size * row_count)
        + inner_pos * row_count
        + text_cols % row_count
    )
    row_losses, grad_terms = block_contributions(
        picture_tile,
        target_tile,
        device_portion_count,
        overall_column_indices,
        score_scaling,
        starting_position,
    )
    own_losses = lax.psum_scatter(row_losses, ("section", "mp"), scatter_dimension=0, tiled=True)
    own_terms = lax.psum_scatter(grad_terms, "dp", scatter_dimension=0, tiled=True)
    along = jnp.sum(text_unit * own_terms, axis=1, keepdims=True)
    text_grad = (own_terms - text_unit * along) * text_inverse
    return (own_losses, text_grad)


def solution(mesh):
    placed = (
        P(("dp", "section", "mp"), None, None),
        P(),
        P(),
        P(),
        P(),
        P(("dp", "section", "mp"), None),
        P(("dp", "section", "mp"), None),
        P(),
        P(),
        P(),
    )
    return jax.shard_map(
        local,
        mesh=mesh,
        in_specs=placed,
        out_specs=(P(("dp", "section", "mp")), P(("dp", "section", "mp"), None)),
        check_vma=False,
    )
```

profile of v0, /device:TPU:1, one launch (start us, length us, event | category | flops | bytes accessed | tf_op | source)
XLA Modules:
  0.0 421.1 jit_solution(14262900369062743601)
XLA Ops:
  7.2 0.0 copy-start
  7.2 0.0 all-gather.5.cloned.1.call-start
  7.2 1.2 fusion.25
  8.4 1.6 fusion.19
  10.0 0.0 all-gather.5.cloned.1.call-update
  10.0 0.0 all-gather.3.cloned.1.call-start
  10.1 0.8 reshape.70
  10.8 5.2 %copy.14 = bf16[1152,1152]{0,1:T(8,128)(2,1)} copy(bf16[1152,1152]{1,0:T(8,128)(2,1)} %param.12) | data formatting | bytes 5308416 | tf_op args[2]
  16.1 5.2 %copy.15 = bf16[1152,1152]{0,1:T(8,128)(2,1)} copy(bf16[1152,1152]{1,0:T(8,128)(2,1)} %param.13) | data formatting | bytes 5308416 | tf_op args[3]
  21.3 0.0 copy-start.1
  21.3 0.0 copy-start.2
  21.3 2.4 fusion.47
  23.8 2.1 fusion.46
  25.9 0.2 fusion.29
  26.1 0.0 copy-done.1
  26.1 0.4 fusion.6
  26.5 0.0 copy-start.4
  26.5 0.0 copy-done.2
  26.5 0.9 fusion.27
  27.4 0.1 reshape.67
  27.5 0.0 copy-done
  27.5 0.5 convolution_reduce_fusion
  28.0 0.0 copy-done.4
  28.0 0.1 fusion.20
  28.2 0.7 fusion.21
  28.9 0.0 all-gather.3.cloned.1.call-update
  28.9 0.0 reduce-scatter.2.cloned.1.call-start
  30.3 0.7 dynamic_slice.3
  31.0 65.8 %all-gather.5.cloned.1.call-done = bf16[768,1152]{1,0:T(8,128)(2,1)} async-done(((bf16[32,1152]{1,0:T(8,128)(2,1)}), bf16[768,1152]{1,0:T(8,128)(2,1)}) %all-gather.5.cloned.1.call-update) | async-done | bytes 1769488 | tf_op jit(solution)/shard_map/all_gather | solution.py:115
  96.8 140.3 %all-gather.3.cloned.1.call-done = bf16[1024,1152]{1,0:T(8,128)(2,1)} async-done(((bf16[32,1152]{1,0:T(8,128)(2,1)}), bf16[1024,1152]{1,0:T(8,128)(2,1)}) %all-gather.3.cloned.1.call-update) | async-done | bytes 2359312 | tf_op jit(solution)/shard_map/all_gather | solution.py:111
  237.1 0.0 copy-start.5
  237.1 6.4 %fusion.5 = (f32[1024]{0:T(1024)S(1)}, f32[1024,768]{0,1:T(8,128)S(1)}) fusion(f32[]{:T(128)} %bitcast.34, f32[]{:T(128)} %bitcast.31, s32[1024]{0:T(1024)S(1)} %dynamic_slice.3, s32[768]{0:T(1024)S(1)} %fusion.42, bf16[1024,1152]{1,0:T(8,128)(2,1)} %all-gather.3.cloned.1.call-done, bf16[768,1152]{1,0:T(8,128)(2,1)} %all-gather.5.cloned.1.call-done), kind=kOutput, calls=%fused_computation.9 | convolution fusion | flops 1821375488 | bytes 7285768 | tf_op jit(solution)/shard_map/dot_general | solution.py:58
  243.5 0.0 copy-done.5
  243.5 4.7 %fusion.10 = f32[768,1152]{1,0:T(8,128)} fusion(bf16[1024,1152]{1,0:T(8,128)(2,1)S(1)} %copy-done.5, f32[1024,768]{0,1:T(8,128)S(1)} %get-tuple-element.5, f32[]{:T(128)} %bitcast.33, f32[]{:T(128)} %bitcast.32, s32[1024]{0:T(1024)S(1)} %dynamic_slice.3, s32[768]{0:T(1024)S(1)} %fusion.42), kind=kOutput, calls=%fused_computation.16 | convolution fusion | flops 1819803648 | bytes 9051144 | tf_op jit(solution)/shard_map/dot_general | solution.py:73
  248.2 0.0 copy-start.3
  248.2 0.0 reduce-scatter.2.cloned.1.call-update
  248.2 1.3 dynamic-slice
  250.1 65.4 %all-reduce = f32[1024]{0:T(1024)S(1)} all-reduce(f32[1024]{0:T(1024)S(1)} %get-tuple-element.4), channel_id=2, replica_groups=mesh['dp'=24,'section'=8,'mp'=4] {'section','mp'}, use_global_device_ids=true, to_apply=%region_5.6.clone | all-reduce | flops 1024 | bytes 8192
  315.6 0.6 dynamic-slice.1
  316.2 95.7 %reduce-scatter.2.cloned.1.call-done = f32[32,1152]{1,0:T(8,128)} async-done(((f32[768,1152]{1,0:T(8,128)}), f32[32,1152]{1,0:T(8,128)}) %reduce-scatter.2.cloned.1.call-update) | async-done | bytes 147472 | tf_op jit(solution)/shard_map/reduce_scatter | solution.py:131
  411.8 0.0 copy-done.3
  411.8 1.1 fusion.22
  412.9 1.7 fusion.24
  (5 shorter events, 0.0 us)
Async XLA Ops:
  7.2 20.4 %copy-start = (bf16[1152,1152]{1,0:T(8,128)(2,1)S(1)}, bf16[1152,1152]{1,0:T(8,128)(2,1)}, u32[]{:S(2)}) copy-start(bf16[1152,1152]{1,0:T(8,128)(2,1)} %param.14) | copy-start | bytes 7962628
  7.2 89.6 %all-gather.5.cloned.1.call-start = ((), (), s32[]{:S(2)}) async-start(), calls=%async_computation.2 | async-start | bytes 1843200 | tf_op jit(solution)/shard_map/all_gather | solution.py:115
  10.0 227.1 %all-gather.3.cloned.1.call-start = ((), (), s32[]{:S(2)}) async-start(), calls=%async_computation.1 | async-start | bytes 2433024 | tf_op jit(solution)/shard_map/all_gather | solution.py:111
  21.3 4.8 %copy-start.1 = (bf16[1,729,1152]{2,1,0:T(8,128)(2,1)S(1)}, bf16[1,729,1152]{2,1,0:T(8,128)(2,1)}, u32[]{:S(2)}) copy-start(bf16[1,729,1152]{2,1,0:T(8,128)(2,1)} %param.10) | copy-start | bytes 5038852
  21.3 5.2 %copy-start.2 = (bf16[1152,1152]{0,1:T(8,128)(2,1)S(1)}, bf16[1152,1152]{0,1:T(8,128)(2,1)}, u32[]{:S(2)}) copy-start(bf16[1152,1152]{0,1:T(8,128)(2,1)} %copy.15) | copy-start | bytes 7962628
  26.5 1.5 copy-start.4
  28.9 382.9 %reduce-scatter.2.cloned.1.call-start = ((), (), s32[]{:S(2)}) async-start(), calls=%async_computation.3 | async-start | bytes 3686400 | tf_op jit(solution)/shard_map/reduce_scatter | solution.py:131
  237.1 6.4 %copy-start.5 = (bf16[1024,1152]{1,0:T(8,128)(2,1)S(1)}, bf16[1024,1152]{1,0:T(8,128)(2,1)}, u32[]{:S(2)}) copy-start(bf16[1024,1152]{1,0:T(8,128)(2,1)} %all-gather.3.cloned.1.call-done) | copy-start | bytes 7077892
  248.2 163.7 %copy-start.3 = (bf16[32,1152]{1,0:T(8,128)(2,1)S(1)}, bf16[32,1152]{1,0:T(8,128)(2,1)}, u32[]{:S(2)}) copy-start(bf16[32,1152]{1,0:T(8,128)(2,1)} %param.16) | copy-start | bytes 221188
Sparse Core Ops, SparseCore 0:
  12.0 84.7 all-gather.4
  99.8 137.3 all-gather.2
  248.3 163.4 reduce-scatter.1
where the time goes:
time: 422 us; the launch traced here: 421 us
  waiting for transfers between devices  302 us (72%)
  blocking collectives  65.4 us (15%)
  matrix products  17.4 us (4%)
  between operations  15.8 us (4%)
  local copies, waits for them, and re-layouts  14 us (3%)
  other arithmetic  6.61 us (2%)
    all_gather x1, waiting for transfers between devices, local(): lax.all_gather(image_norm, ('section', 'mp'), axis=0, tiled=True)  140 us
    reduce_scatter x1, waiting for transfers between devices, local(): lax.psum_scatter(grad_terms, 'dp', scatter_dimension=0, tiled=True)  95.7 us
    all_gather x1, waiting for transfers between devices, local(): lax.all_gather(caption_magnitude, 'dp', axis=0, tiled=True)  65.8 us
    unnamed x1, blocking collectives  65.4 us
    unnamed x16, local copies, waits for them, and re-layouts  12.4 us
  transfers between devices with their start and end apart: 3, of which 3 were waited for; matrix products, arithmetic and copies ran while one was open for 5% of the time, Pallas kernels for 0%

commit v1 on v0

--- a/solution.py
+++ b/solution.py
@@ -79,6 +79,34 @@
     return (row_losses, grad_terms)
 
 
+def shift_ring(x, axis, size, step):
+    return lax.ppermute(x, axis, [(i, (i + step) % size) for i in range(size)])
+
+
+def ring_gather(x, axis, size):
+    forward, backward = x, x
+    arrived = {0: x}
+    forward_steps = size // 2
+    backward_steps = size - 1 - forward_steps
+    for step in range(1, forward_steps + 1):
+        forward = shift_ring(forward, axis, size, 1)
+        arrived[(size - step) % size] = forward
+        if step <= backward_steps:
+            backward = shift_ring(backward, axis, size, -1)
+            arrived[step] = backward
+    return jnp.concatenate([arrived[d] for d in range(size)], axis=0)
+
+
+def direct_scatter(x, axis, size):
+    pos = lax.axis_index(axis)
+    blocks = x.reshape(size, x.shape[0] // size, *x.shape[1:])
+    total = lax.dynamic_index_in_dim(blocks, pos, 0, keepdims=False)
+    for step in range(1, size):
+        outgoing = lax.dynamic_index_in_dim(blocks, (pos + step) % size, 0, keepdims=False)
+        total = total + shift_ring(outgoing, axis, size, step)
+    return total
+
+
 def local(
     patch_features_window,
     probe_request_heads,
@@ -92,11 +120,31 @@
     score_shift,
 ):
     row_count = caption_features.shape[0]
-    inner_size = lax.axis_size(("section", "mp"))
-    inner_pos = lax.axis_index(("section", "mp"))
-    outer_pos = lax.axis_index("dp")
+    prior_count = prior_picture_entries.shape[0]
+    section_size = lax.axis_size("section")
+    mp_size = lax.axis_size("mp")
+    inner_size = section_size * mp_size
+    section_pos = lax.axis_index("section")
+    mp_pos = lax.axis_index("mp")
+    inner_pos = section_pos * mp_size + mp_pos
+    outer_pos = lax.axis_index(("x", "zh", "core"))
+    x_size, zh_size, core_size = lax.axis_size("x"), lax.axis_size("zh"), lax.axis_size("core")
+    outer_size = x_size * zh_size * core_size
     score_scaling = score_scale_param[0]
     starting_position = score_shift[0]
+
+    text_unit, text_inverse = normalize_rows(caption_features)
+    caption_magnitude = text_unit.astype(jnp.bfloat16)
+    device_portion_count = lax.all_gather(caption_magnitude, ("x", "zh", "core"), axis=0, tiled=True)
+
+    prior_norm = normalize_rows(prior_picture_entries)[0].astype(jnp.bfloat16)
+    chunk_rows = row_count
+    prior_norm = jnp.concatenate(
+        [prior_norm, jnp.zeros((chunk_rows - prior_count, prior_norm.shape[1]), jnp.bfloat16)],
+        axis=0,
+    )
+    prior_tile = ring_gather(ring_gather(prior_norm, "mp", mp_size), "section", section_size)
+
     pooled = pool_image(
         patch_features_window[0],
         probe_request_heads,
@@ -104,21 +152,46 @@
         content_projection,
         final_projection,
     )
-    own_images = jnp.concatenate([pooled, prior_picture_entries], axis=0)
-    image_norm = normalize_rows(own_images)[0].astype(jnp.bfloat16)
-    text_unit, text_inverse = normalize_rows(caption_features)
-    caption_magnitude = text_unit.astype(jnp.bfloat16)
-    picture_tile = lax.all_gather(image_norm, ("section", "mp"), axis=0, tiled=True)
-    target_tile = lax.dynamic_slice_in_dim(
+    pooled_norm = normalize_rows(pooled)[0].astype(jnp.bfloat16)
+    pooled_tile = lax.all_to_all(
+        jnp.broadcast_to(pooled_norm, (inner_size, pooled_norm.shape[1])),
+        ("section", "mp"),
+        0,
+        0,
+        tiled=True,
+    )
+    picture_tile = jnp.concatenate([prior_tile, pooled_tile], axis=0)
+
+    group_labels = lax.dynamic_slice_in_dim(
         partner_indices, outer_pos * (inner_size * row_count), inner_size * row_count
-    )
-    device_portion_count = lax.all_gather(caption_magnitude, "dp", axis=0, tiled=True)
-    text_cols = jnp.arange(device_portion_count.shape[0], dtype=jnp.int32)
+    ).reshape(section_size, mp_size, row_count)
+    ring_labels = jnp.roll(jnp.roll(group_labels, -section_pos, axis=0), -mp_pos, axis=1)
+    prior_labels = jnp.concatenate(
+        [
+            ring_labels[:, :, 1 : 1 + prior_count],
+            jnp.full((section_size, mp_size, chunk_rows - prior_count), -1, jnp.int32),
+        ],
+        axis=2,
+    ).reshape(-1)
+    pooled_labels = group_labels[:, :, 0].reshape(-1)
+    target_tile = jnp.concatenate([prior_labels, pooled_labels])
+
+    width = device_portion_count.shape[1]
+    device_portion_count = (
+        device_portion_count.reshape(x_size, zh_size, core_size, row_count, width)
+        .transpose(2, 0, 1, 3, 4)
+        .reshape(outer_size * row_count, width)
+    )
+    blocks = jnp.arange(outer_size, dtype=jnp.int32)
+    block_core = blocks // (x_size * zh_size)
+    block_x = blocks // zh_size % x_size
+    block_zh = blocks % zh_size
+    block_dp = block_x * (zh_size * core_size) + block_zh * core_size + block_core
     overall_column_indices = (
-        text_cols // row_count * (inner_size * row_count)
-        + inner_pos * row_count
-        + text_cols % row_count
-    )
+        (block_dp * inner_size + inner_pos)[:, None] * row_count
+        + jnp.arange(row_count, dtype=jnp.int32)[None, :]
+    ).reshape(-1)
+
     row_losses, grad_terms = block_contributions(
         picture_tile,
         target_tile,
@@ -127,30 +200,50 @@
         score_scaling,
         starting_position,
     )
-    own_losses = lax.psum_scatter(row_losses, ("section", "mp"), scatter_dimension=0, tiled=True)
-    own_terms = lax.psum_scatter(grad_terms, "dp", scatter_dimension=0, tiled=True)
+    prior_losses = row_losses[: inner_size * chunk_rows].reshape(section_size, mp_size, chunk_rows)
+    prior_losses = jnp.roll(jnp.roll(prior_losses, section_pos, axis=0), mp_pos, axis=1)
+    pooled_losses = row_losses[inner_size * chunk_rows :]
+    loss_parts = jnp.concatenate(
+        [pooled_losses[:, None], prior_losses.reshape(inner_size, chunk_rows)[:, :prior_count]],
+        axis=1,
+    )
+    own_losses = jnp.sum(
+        lax.all_to_all(loss_parts, ("section", "mp"), 0, 0, tiled=True), axis=0
+    )
+
+    own_terms = direct_scatter(
+        direct_scatter(direct_scatter(grad_terms, "core", core_size), "x", x_size), "zh", zh_size
+    )
     along = jnp.sum(text_unit * own_terms, axis=1, keepdims=True)
     text_grad = (own_terms - text_unit * along) * text_inverse
     return (own_losses, text_grad)
 
 
 def solution(mesh):
+    outer = mesh.shape["dp"]
+    core_size = 2
+    x_size = outer // (core_size * 3)
+    fine_mesh = jax.sharding.Mesh(
+        mesh.devices.reshape(x_size, 3, core_size, mesh.shape["section"], mesh.shape["mp"]),
+        ("x", "zh", "core", "section", "mp"),
+    )
+    spread = ("x", "zh", "core", "section", "mp")
     placed = (
-        P(("dp", "section", "mp"), None, None),
-        P(),
-        P(),
-        P(),
-        P(),
-        P(("dp", "section", "mp"), None),
-        P(("dp", "section", "mp"), None),
+        P(spread, None, None),
+        P(),
+        P(),
+        P(),
+        P(),
+        P(spread, None),
+        P(spread, None),
         P(),
         P(),
         P(),
     )
     return jax.shard_map(
         local,
-        mesh=mesh,
+        mesh=fine_mesh,
         in_specs=placed,
-        out_specs=(P(("dp", "section", "mp")), P(("dp", "section", "mp"), None)),
+        out_specs=(P(spread), P(spread, None)),
         check_vma=False,
     )

time: 422 us -> 222 us (0.53)
  the two profiles are of different devices: /device:TPU:1 before, /device:TPU:64 now
where the time goes in v1:
time: 222 us; the launch traced here: 221 us
  starting transfers between devices  78.3 us (35%)
  local copies, waits for them, and re-layouts  50.3 us (23%)
  waiting for transfers between devices  47.7 us (21%)
  between operations  16.6 us (7%)
  other arithmetic  14.3 us (6%)
  matrix products  13.4 us (6%)
    ppermute x16, starting transfers between devices, shift_ring(): return lax.ppermute(x, axis, [(i, (i + step) % size) for i in range(size)])  59.9 us
    ppermute x16, waiting for transfers between devices, shift_ring(): return lax.ppermute(x, axis, [(i, (i + step) % size) for i in range(size)])  34.8 us
    concatenate x1, local copies, waits for them, and re-layouts, local(): picture_tile = jnp.concatenate([prior_tile, pooled_tile], axis=0)  22.5 us
    unnamed x33, local copies, waits for them, and re-layouts  15.4 us
    all_to_all x1, waiting for transfers between devices, local(): lax.all_to_all(loss_parts, ('section', 'mp'), 0, 0, tiled=True)  12.9 us
    all_to_all x1, starting transfers between devices, local(): lax.all_to_all(jnp.broadcast_to(pooled_norm, (inner_size, pooled_norm.sha...  10.3 us
    all_to_all x1, starting transfers between devices, local(): lax.all_to_all(loss_parts, ('section', 'mp'), 0, 0, tiled=True)  8.16 us
  transfers between devices with their start and end apart: 19, of which 10 were waited for; matrix products, arithmetic and copies ran while one was open for 24% of the time, Pallas kernels for 0%

profile of v1, /device:TPU:64, one launch (start us, length us, event | category | flops | bytes accessed | tf_op | source)
XLA Modules:
  0.0 220.6 jit_solution(13693367835362740587)
XLA Ops:
  7.2 1.2 fusion.24
  8.9 1.6 fusion.18
  10.6 1.0 fusion.19
  11.6 1.0 fusion.20
  12.6 10.6 %collective-permute-start = (bf16[32,1152]{1,0:T(8,128)(2,1)S(1)}, bf16[32,1152]{1,0:T(8,128)(2,1)S(1)}, u32[]{:S(2)}, u32[]{:S(2)}) collective-permute-start(bf16[32,1152]{1,0:T(8,128)(2,1)S(1)} %concatenate.40), channel_id=1, source_target_pairs={{0,3},{1,0},{2,1},{3,2},{4,7},{5,4},{6,5},{7,6},{8,11},{9,8},{10,9... | collective-permute-start | bytes 221192 | tf_op jit(solution)/shard_map/ppermute | solution.py:83
  23.2 1.9 collective-permute-start.1
  25.9 5.2 %copy.24 = bf16[1152,1152]{0,1:T(8,128)(2,1)} copy(bf16[1152,1152]{1,0:T(8,128)(2,1)} %param.12) | data formatting | bytes 5308416 | tf_op args[2]
  31.1 2.4 %fusion.52 = f32[16,1,1152]{2,1,0:T(1,128)S(1)} fusion(bf16[16,72,1]{1,2,0:T(2,128)(2,1)S(1)} %reshape.161, bf16[1152,16,72]{0,2,1:T(8,128)(2,1)} %bitcast.73), kind=kOutput, calls=%fused_computation.101 | convolution fusion | flops 2654208 | bytes 2730240 | tf_op jit(solution)/shard_map/dhe,he->dh/dot_general | solution.py:16
  34.8 5.3 %copy.25 = bf16[1152,1152]{0,1:T(8,128)(2,1)} copy(bf16[1152,1152]{1,0:T(8,128)(2,1)} %param.13) | data formatting | bytes 5308416 | tf_op args[3]
  40.1 1.9 collective-permute-start.2
  42.0 2.6 %fusion.27 = f32[16,1,72]{2,1,0:T(1,128)S(1)} fusion(bf16[1152,16,72]{0,2,1:T(8,128)(2,1)} %bitcast.78, bf16[16,1152,1]{1,0,2:T(8,128)(2,1)S(1)} %fusion.7), kind=kOutput, calls=%fused_computation.48 | convolution fusion | flops 2654208 | bytes 2695680 | tf_op jit(solution)/shard_map/hd,dhe->he/dot_general | solution.py:30
  44.8 1.8 collective-permute-done.2
  46.5 3.9 %concatenate.41 = bf16[128,1152]{1,0:T(8,128)(2,1)} concatenate(bf16[31,1152]{1,0:T(8,128)(2,1)S(1)} %fusion.20, bf16[1,1152]{1,0:T(2,128)(2,1)S(1)} %broadcast_in_dim.6, bf16[32,1152]{1,0:T(8,128)(2,1)S(1)} %collective-permute-done, bf16[32,1152]{1,0:T(8,128)(2,1)S(1)} %collective-permute-done.2, bf16[32,1152]{1,0:T(8,128)(2,1)S(1)} %collective-permute-done.1), dimensions={0} | concatenate | bytes 589824 | tf_op jit(solution)/shard_map/concatenate | solution.py:97
  50.5 1.9 collective-permute-start.6
  54.2 5.1 %collective-permute-start.3 = (bf16[128,1152]{1,0:T(8,128)(2,1)}, bf16[128,1152]{1,0:T(8,128)(2,1)S(1)}, u32[]{:S(2)}, u32[]{:S(2)}) collective-permute-start(bf16[128,1152]{1,0:T(8,128)(2,1)} %concatenate.41), channel_id=1, source_target_pairs={{0,28},{4,0},{8,4},{12,8},{16,12},{20,16},{24,20},{28,24},{1,29},{... | collective-permute-start | bytes 884744 | tf_op jit(solution)/shard_map/ppermute | solution.py:83
  59.3 2.0 collective-permute-done.6
  61.3 1.9 collective-permute-start.7
  63.8 1.1 reduce.9
  65.7 10.3 %all-to-all-start = ((bf16[32,2,576]{2,1,0:T(2,128)(2,1)}), bf16[32,2,576]{2,1,0:T(2,128)(2,1)S(1)}, u32[]{:S(2)}, u32[]{:S(2)}) async-start(bf16[32,2,576]{2,1,0:T(2,128)(2,1)} %reshape.165), calls=%async_computation | async-start | bytes 163840 | tf_op jit(solution)/shard_map/all_to_all | solution.py:156
  76.0 4.7 %collective-permute-start.4 = (bf16[128,1152]{1,0:T(8,128)(2,1)S(1)}, bf16[128,1152]{1,0:T(8,128)(2,1)}, u32[]{:S(2)}, u32[]{:S(2)}) collective-permute-start(bf16[128,1152]{1,0:T(8,128)(2,1)S(1)} %collective-permute-done.3), channel_id=1, source_target_pairs={{0,28},{4,0},{8,4},{12,8},{16,12},{20,16},{24,20},{28,24},{1,29},{... | collective-permute-start | bytes 884744 | tf_op jit(solution)/shard_map/ppermute | solution.py:83
  80.7 1.9 collective-permute-start.8
  84.4 1.9 collective-permute-done.4
  86.4 4.4 %collective-permute-start.5 = (bf16[128,1152]{1,0:T(8,128)(2,1)}, bf16[128,1152]{1,0:T(8,128)(2,1)}, u32[]{:S(2)}, u32[]{:S(2)}) collective-permute-start(bf16[128,1152]{1,0:T(8,128)(2,1)} %collective-permute-done.4), channel_id=1, source_target_pairs={{0,28},{4,0},{8,4},{12,8},{16,12},{20,16},{24,20},{28,24},{1,29},{... | collective-permute-start | bytes 884744 | tf_op jit(solution)/shard_map/ppermute | solution.py:83
  90.8 2.1 collective-permute-start.9
  95.3 5.6 %collective-permute-done.9 = bf16[128,1152]{1,0:T(8,128)(2,1)} collective-permute-done((bf16[128,1152]{1,0:T(8,128)(2,1)}, bf16[128,1152]{1,0:T(8,128)(2,1)}, u32[]{:S(2)}, u32[]{:S(2)}) %collective-permute-start.9) | collective-permute-done | bytes 294944 | tf_op jit(solution)/shard_map/ppermute | solution.py:83
  101.0 22.5 %concatenate.42 = bf16[1056,1152]{1,0:T(8,128)(2,1)} concatenate(bf16[31,1152]{1,0:T(8,128)(2,1)S(1)} %fusion.20, bf16[1,1152]{1,0:T(2,128)(2,1)S(1)} %broadcast_in_dim.6, bf16[32,1152]{1,0:T(8,128)(2,1)} %copy-done.7, bf16[32,1152]{1,0:T(8,128)(2,1)} %copy-done.9, bf16[32,1152]{1,0:T(8,128)(2,1)} %copy-done.8, bf16[128,1152]{1,0:T(8,128)(2,1)S(1)} %collective-permute-done.3, ...), dimensions={0} | concatenate | bytes 4866048 | tf_op jit(solution)/shard_map/concatenate | solution.py:163
  123.5 1.8 copy.26
  125.7 3.8 %fusion.6 = (f32[1056]{0:T(1024)S(1)}, f32[1056,768]{1,0:T(8,128)S(1)}) fusion(s32[768]{0:T(1024)S(1)} %copy-done.13, s32[1056]{0:T(1024)S(1)} %copy-done.10, f32[]{:T(128)} %bitcast.72, bf16[1056,1152]{1,0:T(8,128)(2,1)S(1)} %copy-done.4, bf16[768,1152]{1,0:T(8,128)(2,1)S(1)} %bitcast.80, f32[]{:T(128)} %bitcast.70), kind=kOutput, calls=%fused_computation.11 | convolution fusion | flops 1878293504 | bytes 7458056 | tf_op jit(solution)/shard_map/dot_general | solution.py:58
  129.6 3.0 %fusion.11 = f32[768,1152]{1,0:T(8,128)S(1)} fusion(bf16[1056,1152]{1,0:T(8,128)(2,1)S(1)} %copy-done.4, f32[1056,768]{1,0:T(8,128)S(1)} %get-tuple-element.12, f32[]{:T(128)} %bitcast.71, s32[768]{0:T(1024)S(1)} %copy-done.13, s32[1056]{0:T(1024)S(1)} %copy-done.10), kind=kOutput, calls=%fused_computation.19 | convolution fusion | flops 1875050496 | bytes 9223300 | tf_op jit(solution)/shard_map/dot_general | solution.py:73
  132.6 1.7 copy-done.3
  134.3 1.4 dynamic-slice_bitcast_fusion
  135.7 1.9 collective-permute-start.10
  137.7 4.0 %collective-permute-done.10 = f32[384,1152]{1,0:T(8,128)} collective-permute-done((f32[384,1152]{1,0:T(8,128)}, f32[384,1152]{1,0:T(8,128)}, u32[]{:S(2)}, u32[]{:S(2)}) %collective-permute-start.10) | collective-permute-done | bytes 1769504 | tf_op jit(solution)/shard_map/ppermute | solution.py:83
  141.6 2.2 bitcast_add_fusion
  143.8 1.2 copy-done.1
  145.0 1.1 dynamic-slice_bitcast_fusion.3
  146.1 2.3 %collective-permute-start.13 = (f32[96,1152]{1,0:T(8,128)}, f32[96,1152]{1,0:T(8,128)S(1)}, u32[]{:S(2)}, u32[]{:S(2)}) collective-permute-start(f32[96,1152]{1,0:T(8,128)} %get-tuple-element.5), channel_id=1, source_target_pairs={{0,576},{192,0},{384,192},{576,384},{1,577},{193,1},{385,193},{577... | collective-permute-start | bytes 1327112 | tf_op jit(solution)/shard_map/ppermute | solution.py:83
  148.4 2.7 %collective-permute-start.12 = (f32[96,1152]{1,0:T(8,128)}, f32[96,1152]{1,0:T(8,128)}, u32[]{:S(2)}, u32[]{:S(2)}) collective-permute-start(f32[96,1152]{1,0:T(8,128)} %get-tuple-element.6), channel_id=1, source_target_pairs={{0,384},{192,576},{384,0},{576,192},{1,385},{193,577},{385,1},{577... | collective-permute-start | bytes 1327112 | tf_op jit(solution)/shard_map/ppermute | solution.py:83
  151.1 2.8 %collective-permute-start.11 = (f32[96,1152]{1,0:T(8,128)}, f32[96,1152]{1,0:T(8,128)}, u32[]{:S(2)}, u32[]{:S(2)}) collective-permute-start(f32[96,1152]{1,0:T(8,128)} %get-tuple-element.4), channel_id=1, source_target_pairs={{0,192},{192,384},{384,576},{576,0},{1,193},{193,385},{385,577},{5... | collective-permute-start | bytes 1327112 | tf_op jit(solution)/shard_map/ppermute | solution.py:83
  154.1 7.1 %collective-permute-done.13 = f32[96,1152]{1,0:T(8,128)S(1)} collective-permute-done((f32[96,1152]{1,0:T(8,128)}, f32[96,1152]{1,0:T(8,128)S(1)}, u32[]{:S(2)}, u32[]{:S(2)}) %collective-permute-start.13) | collective-permute-done | bytes 442400 | tf_op jit(solution)/shard_map/ppermute | solution.py:83
  161.2 4.0 %collective-permute-done.12 = f32[96,1152]{1,0:T(8,128)} collective-permute-done((f32[96,1152]{1,0:T(8,128)}, f32[96,1152]{1,0:T(8,128)}, u32[]{:S(2)}, u32[]{:S(2)}) %collective-permute-start.12) | collective-permute-done | bytes 442400 | tf_op jit(solution)/shard_map/ppermute | solution.py:83
  165.2 8.3 %collective-permute-done.11 = f32[96,1152]{1,0:T(8,128)} collective-permute-done((f32[96,1152]{1,0:T(8,128)}, f32[96,1152]{1,0:T(8,128)}, u32[]{:S(2)}, u32[]{:S(2)}) %collective-permute-start.11) | collective-permute-done | bytes 442400 | tf_op jit(solution)/shard_map/ppermute | solution.py:83
  173.5 1.5 fusion.15
  175.7 11.8 %collective-permute-start.15 = (f32[32,1152]{1,0:T(8,128)}, f32[32,1152]{1,0:T(8,128)S(1)}, u32[]{:S(2)}, u32[]{:S(2)}) collective-permute-start(f32[32,1152]{1,0:T(8,128)} %get-tuple-element.8), channel_id=1, source_target_pairs={{0,128},{64,0},{128,64},{1,129},{65,1},{129,65},{2,130},{66,2},{13... | collective-permute-start | bytes 442376 | tf_op jit(solution)/shard_map/ppermute | solution.py:83
  187.5 1.9 collective-permute-start.14
  190.3 8.2 %all-to-all-start.1 = ((f32[32,1,32]{2,1,0:T(1,128)}), f32[32,1,32]{2,1,0:T(1,128)S(1)}, u32[]{:S(2)}, u32[]{:S(2)}) async-start(f32[32,1,32]{2,1,0:T(1,128)} %bitcast.14), calls=%async_computation.1 | async-start | bytes 32768 | tf_op jit(solution)/shard_map/all_to_all | solution.py:211
  198.4 12.9 %all-to-all-done.1 = f32[32,1,32]{2,1,0:T(1,128)S(1)} async-done(((f32[32,1,32]{2,1,0:T(1,128)}), f32[32,1,32]{2,1,0:T(1,128)S(1)}, u32[]{:S(2)}, u32[]{:S(2)}) %all-to-all-start.1) | async-done | bytes 4128 | tf_op jit(solution)/shard_map/all_to_all | solution.py:211
  211.9 1.1 fusion.21
  (78 shorter events, 11.6 us)
Async XLA Ops:
  7.2 45.2 %copy-start = (bf16[1152,1152]{1,0:T(8,128)(2,1)S(1)}, bf16[1152,1152]{1,0:T(8,128)(2,1)}, u32[]{:S(2)}) copy-start(bf16[1152,1152]{1,0:T(8,128)(2,1)} %param.14) | copy-start | bytes 7962628
  7.2 116.3 %all-gather.2.cloned.1.call-start = ((), (), s32[]{:S(2)}) async-start(), calls=%async_computation.2 | async-start | bytes 1843200 | tf_op jit(solution)/shard_map/all_gather | solution.py:138
  8.4 0.6 copy-start.11
  12.6 32.2 %collective-permute-start = (bf16[32,1152]{1,0:T(8,128)(2,1)S(1)}, bf16[32,1152]{1,0:T(8,128)(2,1)S(1)}, u32[]{:S(2)}, u32[]{:S(2)}) collective-permute-start(bf16[32,1152]{1,0:T(8,128)(2,1)S(1)} %concatenate.40), channel_id=1, source_target_pairs={{0,3},{1,0},{2,1},{3,2},{4,7},{5,4},{6,5},{7,6},{8,11},{9,8},{10,9... | collective-permute-start | bytes 221192 | tf_op jit(solution)/shard_map/ppermute | solution.py:83
  23.2 16.9 %collective-permute-start.1 = (bf16[32,1152]{1,0:T(8,128)(2,1)S(1)}, bf16[32,1152]{1,0:T(8,128)(2,1)S(1)}, u32[]{:S(2)}, u32[]{:S(2)}) collective-permute-start(bf16[32,1152]{1,0:T(8,128)(2,1)S(1)} %concatenate.40), channel_id=1, source_target_pairs={{0,1},{1,2},{2,3},{3,0},{4,5},{5,6},{6,7},{7,4},{8,9},{9,10},{10,1... | collective-permute-start | bytes 221192 | tf_op jit(solution)/shard_map/ppermute | solution.py:83
  31.1 2.4 %copy-start.2 = (bf16[1,729,1152]{2,1,0:T(8,128)(2,1)S(1)}, bf16[1,729,1152]{2,1,0:T(8,128)(2,1)}, u32[]{:S(2)}) copy-start(bf16[1,729,1152]{2,1,0:T(8,128)(2,1)} %param.10) | copy-start | bytes 5038852
  40.1 12.8 %copy-start.8 = (bf16[32,1152]{1,0:T(8,128)(2,1)}, bf16[32,1152]{1,0:T(8,128)(2,1)S(1)}, u32[]{:S(2)}) copy-start(bf16[32,1152]{1,0:T(8,128)(2,1)S(1)} %collective-permute-done.1) | copy-start | bytes 221188
  40.1 6.4 %collective-permute-start.2 = (bf16[32,1152]{1,0:T(8,128)(2,1)S(1)}, bf16[32,1152]{1,0:T(8,128)(2,1)S(1)}, u32[]{:S(2)}, u32[]{:S(2)}) collective-permute-start(bf16[32,1152]{1,0:T(8,128)(2,1)S(1)} %collective-permute-done.1), channel_id=1, source_target_pairs={{0,1},{1,2},{2,3},{3,0},{4,5},{5,6},{6,7},{7,4},{8,9},{9,10},{10,1... | collective-permute-start | bytes 221192 | tf_op jit(solution)/shard_map/ppermute | solution.py:83
  44.8 18.4 %copy-start.7 = (bf16[32,1152]{1,0:T(8,128)(2,1)}, bf16[32,1152]{1,0:T(8,128)(2,1)S(1)}, u32[]{:S(2)}) copy-start(bf16[32,1152]{1,0:T(8,128)(2,1)S(1)} %collective-permute-done) | copy-start | bytes 221188
  46.5 16.8 %copy-start.9 = (bf16[32,1152]{1,0:T(8,128)(2,1)}, bf16[32,1152]{1,0:T(8,128)(2,1)S(1)}, u32[]{:S(2)}) copy-start(bf16[32,1152]{1,0:T(8,128)(2,1)S(1)} %collective-permute-done.2) | copy-start | bytes 221188
  50.5 10.8 %collective-permute-start.6 = (bf16[128,1152]{1,0:T(8,128)(2,1)}, bf16[128,1152]{1,0:T(8,128)(2,1)S(1)}, u32[]{:S(2)}, u32[]{:S(2)}) collective-permute-start(bf16[128,1152]{1,0:T(8,128)(2,1)} %concatenate.41), channel_id=1, source_target_pairs={{0,4},{4,8},{8,12},{12,16},{16,20},{20,24},{24,28},{28,0},{1,5},{5... | collective-permute-start | bytes 884744 | tf_op jit(solution)/shard_map/ppermute | solution.py:83
  54.2 21.8 %collective-permute-start.3 = (bf16[128,1152]{1,0:T(8,128)(2,1)}, bf16[128,1152]{1,0:T(8,128)(2,1)S(1)}, u32[]{:S(2)}, u32[]{:S(2)}) collective-permute-start(bf16[128,1152]{1,0:T(8,128)(2,1)} %concatenate.41), channel_id=1, source_target_pairs={{0,28},{4,0},{8,4},{12,8},{16,12},{20,16},{24,20},{28,24},{1,29},{... | collective-permute-start | bytes 884744 | tf_op jit(solution)/shard_map/ppermute | solution.py:83
  61.3 19.4 %collective-permute-start.7 = (bf16[128,1152]{1,0:T(8,128)(2,1)S(1)}, bf16[128,1152]{1,0:T(8,128)(2,1)}, u32[]{:S(2)}, u32[]{:S(2)}) collective-permute-start(bf16[128,1152]{1,0:T(8,128)(2,1)S(1)} %collective-permute-done.6), channel_id=1, source_target_pairs={{0,4},{4,8},{8,12},{12,16},{16,20},{20,24},{24,28},{28,0},{1,5},{5... | collective-permute-start | bytes 884744 | tf_op jit(solution)/shard_map/ppermute | solution.py:83
  65.7 29.4 %all-to-all-start = ((bf16[32,2,576]{2,1,0:T(2,128)(2,1)}), bf16[32,2,576]{2,1,0:T(2,128)(2,1)S(1)}, u32[]{:S(2)}, u32[]{:S(2)}) async-start(bf16[32,2,576]{2,1,0:T(2,128)(2,1)} %reshape.165), calls=%async_computation | async-start | bytes 163840 | tf_op jit(solution)/shard_map/all_to_all | solution.py:156
  76.0 10.4 %collective-permute-start.4 = (bf16[128,1152]{1,0:T(8,128)(2,1)S(1)}, bf16[128,1152]{1,0:T(8,128)(2,1)}, u32[]{:S(2)}, u32[]{:S(2)}) collective-permute-start(bf16[128,1152]{1,0:T(8,128)(2,1)S(1)} %collective-permute-done.3), channel_id=1, source_target_pairs={{0,28},{4,0},{8,4},{12,8},{16,12},{20,16},{24,20},{28,24},{1,29},{... | collective-permute-start | bytes 884744 | tf_op jit(solution)/shard_map/ppermute | solution.py:83
  80.7 10.1 %collective-permute-start.8 = (bf16[128,1152]{1,0:T(8,128)(2,1)}, bf16[128,1152]{1,0:T(8,128)(2,1)}, u32[]{:S(2)}, u32[]{:S(2)}) collective-permute-start(bf16[128,1152]{1,0:T(8,128)(2,1)} %collective-permute-done.7), channel_id=1, source_target_pairs={{0,4},{4,8},{8,12},{12,16},{16,20},{20,24},{24,28},{28,0},{1,5},{5... | collective-permute-start | bytes 884744 | tf_op jit(solution)/shard_map/ppermute | solution.py:83
  86.4 9.0 %collective-permute-start.5 = (bf16[128,1152]{1,0:T(8,128)(2,1)}, bf16[128,1152]{1,0:T(8,128)(2,1)}, u32[]{:S(2)}, u32[]{:S(2)}) collective-permute-start(bf16[128,1152]{1,0:T(8,128)(2,1)} %collective-permute-done.4), channel_id=1, source_target_pairs={{0,28},{4,0},{8,4},{12,8},{16,12},{20,16},{24,20},{28,24},{1,29},{... | collective-permute-start | bytes 884744 | tf_op jit(solution)/shard_map/ppermute | solution.py:83
  90.8 10.1 %collective-permute-start.9 = (bf16[128,1152]{1,0:T(8,128)(2,1)}, bf16[128,1152]{1,0:T(8,128)(2,1)}, u32[]{:S(2)}, u32[]{:S(2)}) collective-permute-start(bf16[128,1152]{1,0:T(8,128)(2,1)} %collective-permute-done.8), channel_id=1, source_target_pairs={{0,4},{4,8},{8,12},{12,16},{16,20},{20,24},{24,28},{28,0},{1,5},{5... | collective-permute-start | bytes 884744 | tf_op jit(solution)/shard_map/ppermute | solution.py:83
  123.5 1.8 copy-start.10
  123.5 1.8 copy-start.13
  123.5 2.2 %copy-start.4 = (bf16[1056,1152]{1,0:T(8,128)(2,1)S(1)}, bf16[1056,1152]{1,0:T(8,128)(2,1)}, u32[]{:S(2)}) copy-start(bf16[1056,1152]{1,0:T(8,128)(2,1)} %concatenate.42) | copy-start | bytes 7299076
  132.6 1.7 copy-start.3
  135.7 5.9 %collective-permute-start.10 = (f32[384,1152]{1,0:T(8,128)}, f32[384,1152]{1,0:T(8,128)}, u32[]{:S(2)}, u32[]{:S(2)}) collective-permute-start(f32[384,1152]{1,0:T(8,128)} %dynamic-slice_bitcast_fusion), channel_id=1, source_target_pairs={{0,32},{32,0},{1,33},{33,1},{2,34},{34,2},{3,35},{35,3},{4,36},{36... | collective-permute-start | bytes 5308424 | tf_op jit(solution)/shard_map/ppermute | solution.py:83
  143.8 1.2 copy-start.1
  145.0 66.8 %copy-start.5 = (bf16[32,1152]{1,0:T(8,128)(2,1)S(1)}, bf16[32,1152]{1,0:T(8,128)(2,1)}, u32[]{:S(2)}) copy-start(bf16[32,1152]{1,0:T(8,128)(2,1)} %param.16) | copy-start | bytes 221188
  145.0 66.8 %copy-start.12 = (f32[32]{0:T(128)S(1)}, f32[32]{0:T(128)}, u32[]{:S(2)}) copy-start(f32[32]{0:T(128)} %copy-done.11) | copy-start | bytes 388
  146.1 15.1 %collective-permute-start.13 = (f32[96,1152]{1,0:T(8,128)}, f32[96,1152]{1,0:T(8,128)S(1)}, u32[]{:S(2)}, u32[]{:S(2)}) collective-permute-start(f32[96,1152]{1,0:T(8,128)} %get-tuple-element.5), channel_id=1, source_target_pairs={{0,576},{192,0},{384,192},{576,384},{1,577},{193,1},{385,193},{577... | collective-permute-start | bytes 1327112 | tf_op jit(solution)/shard_map/ppermute | solution.py:83
  148.4 16.8 %collective-permute-start.12 = (f32[96,1152]{1,0:T(8,128)}, f32[96,1152]{1,0:T(8,128)}, u32[]{:S(2)}, u32[]{:S(2)}) collective-permute-start(f32[96,1152]{1,0:T(8,128)} %get-tuple-element.6), channel_id=1, source_target_pairs={{0,384},{192,576},{384,0},{576,192},{1,385},{193,577},{385,1},{577... | collective-permute-start | bytes 1327112 | tf_op jit(solution)/shard_map/ppermute | solution.py:83
  151.1 22.4 %collective-permute-start.11 = (f32[96,1152]{1,0:T(8,128)}, f32[96,1152]{1,0:T(8,128)}, u32[]{:S(2)}, u32[]{:S(2)}) collective-permute-start(f32[96,1152]{1,0:T(8,128)} %get-tuple-element.4), channel_id=1, source_target_pairs={{0,192},{192,384},{384,576},{576,0},{1,193},{193,385},{385,577},{5... | collective-permute-start | bytes 1327112 | tf_op jit(solution)/shard_map/ppermute | solution.py:83
  161.2 4.0 %copy-start.6 = (f32[96,1152]{1,0:T(8,128)}, f32[96,1152]{1,0:T(8,128)S(1)}, u32[]{:S(2)}) copy-start(f32[96,1152]{1,0:T(8,128)S(1)} %collective-permute-done.13) | copy-start | bytes 1327108
  175.7 36.2 %collective-permute-start.15 = (f32[32,1152]{1,0:T(8,128)}, f32[32,1152]{1,0:T(8,128)S(1)}, u32[]{:S(2)}, u32[]{:S(2)}) collective-permute-start(f32[32,1152]{1,0:T(8,128)} %get-tuple-element.8), channel_id=1, source_target_pairs={{0,128},{64,0},{128,64},{1,129},{65,1},{129,65},{2,130},{66,2},{13... | collective-permute-start | bytes 442376 | tf_op jit(solution)/shard_map/ppermute | solution.py:83
  187.5 24.3 %collective-permute-start.14 = (f32[32,1152]{1,0:T(8,128)S(1)}, f32[32,1152]{1,0:T(8,128)}, u32[]{:S(2)}, u32[]{:S(2)}) collective-permute-start(f32[32,1152]{1,0:T(8,128)S(1)} %get-tuple-element.7), channel_id=1, source_target_pairs={{0,64},{64,128},{128,0},{1,65},{65,129},{129,1},{2,66},{66,130},{1... | collective-permute-start | bytes 442376 | tf_op jit(solution)/shard_map/ppermute | solution.py:83
  190.3 21.0 %all-to-all-start.1 = ((f32[32,1,32]{2,1,0:T(1,128)}), f32[32,1,32]{2,1,0:T(1,128)S(1)}, u32[]{:S(2)}, u32[]{:S(2)}) async-start(f32[32,1,32]{2,1,0:T(1,128)} %bitcast.14), calls=%async_computation.1 | async-start | bytes 32768 | tf_op jit(solution)/shard_map/all_to_all | solution.py:211
Sparse Core Ops, SparseCore 0:
  12.0 83.4 all-gather.1

commit v2 on v1

--- a/solution.py
+++ b/solution.py
@@ -13,12 +13,13 @@
     patch_rows, probe_request_heads, lookup_projection, content_projection, final_projection
 ):
     width = lookup_projection.shape[0]
-    key_probe = jnp.einsum(
-        "dhe,he->dh",
-        lookup_projection.reshape(width, HEADS, HD),
-        probe_request_heads.reshape(HEADS, HD),
-        preferred_element_type=jnp.float32,
-    )
+    head_of_column = jnp.arange(width, dtype=jnp.int32) // HD
+    probe_blocks = jnp.where(
+        head_of_column[:, None] == jnp.arange(HEADS, dtype=jnp.int32)[None, :],
+        probe_request_heads[:, None],
+        jnp.zeros((), probe_request_heads.dtype),
+    )
+    key_probe = jnp.dot(lookup_projection, probe_blocks, preferred_element_type=jnp.float32)
     key_probe = (key_probe / math.sqrt(HD)).astype(jnp.bfloat16)
     scores = jnp.dot(patch_rows, key_probe, preferred_element_type=jnp.float32)
     highest = jnp.max(scores, axis=0, keepdims=True)
@@ -27,11 +28,11 @@
     pooled_patch = lax.dot_general(
         weights, patch_rows, (((0,), (0,)), ((), ())), preferred_element_type=jnp.float32
     ).astype(jnp.bfloat16)
-    values = jnp.einsum(
-        "hd,dhe->he",
-        pooled_patch,
-        content_projection.reshape(width, HEADS, HD),
-        preferred_element_type=jnp.float32,
+    every_head = jnp.dot(pooled_patch, content_projection, preferred_element_type=jnp.float32)
+    values = jnp.sum(
+        every_head.reshape(HEADS, HEADS, HD)
+        * jnp.eye(HEADS, dtype=jnp.float32)[:, :, None],
+        axis=1,
     )
     values = values.astype(jnp.bfloat16).reshape(1, width)
     return jnp.dot(values, final_projection, preferred_element_type=jnp.float32).astype(
@@ -137,12 +138,10 @@
     caption_magnitude = text_unit.astype(jnp.bfloat16)
     device_portion_count = lax.all_gather(caption_magnitude, ("x", "zh", "core"), axis=0, tiled=True)
 
-    prior_norm = normalize_rows(prior_picture_entries)[0].astype(jnp.bfloat16)
     chunk_rows = row_count
-    prior_norm = jnp.concatenate(
-        [prior_norm, jnp.zeros((chunk_rows - prior_count, prior_norm.shape[1]), jnp.bfloat16)],
-        axis=0,
-    )
+    prior_norm = normalize_rows(
+        jnp.pad(prior_picture_entries, ((0, chunk_rows - prior_count), (0, 0)))
+    )[0].astype(jnp.bfloat16)
     prior_tile = ring_gather(ring_gather(prior_norm, "mp", mp_size), "section", section_size)
 
     pooled = pool_image(

time: 222 us -> 223 us (level)
  the two profiles are of different devices: /device:TPU:64 before, /device:TPU:1 now
where the time goes in v2:
time: 223 us; the launch traced here: 222 us
  waiting for transfers between devices  78.2 us (35%)
  starting transfers between devices  75.4 us (34%)
  local copies, waits for them, and re-layouts  23 us (10%)
  between operations  16.6 us (7%)
  matrix products  15.4 us (7%)
  other arithmetic  13.5 us (6%)
    ppermute x16, starting transfers between devices, shift_ring(): return lax.ppermute(x, axis, [(i, (i + step) % size) for i in range(size)])  55.1 us
    all_gather x1, waiting for transfers between devices, local(): lax.all_gather(caption_magnitude, ('x', 'zh', 'core'), axis=0, tiled=True)  34.9 us
    ppermute x16, waiting for transfers between devices, shift_ring(): return lax.ppermute(x, axis, [(i, (i + step) % size) for i in range(size)])  34.3 us
    unnamed x24, local copies, waits for them, and re-layouts  15.3 us
    all_to_all x1, starting transfers between devices, local(): lax.all_to_all(jnp.broadcast_to(pooled_norm, (inner_size, pooled_norm.sha...  10.2 us
    all_to_all x1, starting transfers between devices, local(): lax.all_to_all(loss_parts, ('section', 'mp'), 0, 0, tiled=True)  10.1 us
    all_to_all x1, waiting for transfers between devices, local(): lax.all_to_all(loss_parts, ('section', 'mp'), 0, 0, tiled=True)  8.97 us
  transfers between devices with their start and end apart: 19, of which 12 were waited for; matrix products, arithmetic and copies ran while one was open for 13% of the time, Pallas kernels for 0%

profile of v2, /device:TPU:1, one launch (start us, length us, event | category | flops | bytes accessed | tf_op | source)
XLA Modules:
  0.0 222.0 jit_solution(18074795325174298103)
XLA Ops:
  7.2 1.2 fusion.27
  8.3 1.6 constant_dynamic-update-slice_fusion.10
  9.9 8.4 %collective-permute-start = (bf16[32,1152]{1,0:T(8,128)(2,1)S(1)}, bf16[32,1152]{1,0:T(8,128)(2,1)S(1)}, u32[]{:S(2)}, u32[]{:S(2)}) collective-permute-start(bf16[32,1152]{1,0:T(8,128)(2,1)S(1)} %get-tuple-element.5), channel_id=1, source_target_pairs={{0,3},{1,0},{2,1},{3,2},{4,7},{5,4},{6,5},{7,6},{8,11},{9,8},{10,9... | collective-permute-start | bytes 221192 | tf_op jit(solution)/shard_map/ppermute | solution.py:84
  18.4 1.9 collective-permute-start.1
  20.3 4.1 %fusion.68 = (f32[16]{0:T(128)S(1)}, f32[16,729]{1,0:T(8,128)S(1)}) fusion(bf16[1,729,1152]{2,1,0:T(8,128)(2,1)} %param.10, bf16[1152,1152]{1,0:T(8,128)(2,1)} %param.12, s32[1152]{0:T(1024)S(1)} %add_select_fusion, bf16[1152]{0:T(1024)(128)(2,1)} %param.11), kind=kOutput, calls=%fused_computation.126 | convolution fusion | flops 69426560 | bytes 4387456 | tf_op jit(solution)/shard_map/dot_general | solution.py:24
  24.7 2.2 fusion.15
  27.3 2.2 %convolution_reduce_fusion = bf16[1152]{0:T(1024)(128)(2,1)S(1)} fusion(bf16[1152,1]{0,1:T(2,128)(2,1)S(1)} %reshape.167, bf16[1152,1152]{1,0:T(8,128)(2,1)} %param.14), kind=kOutput, calls=%fused_computation.23 | convolution fusion | flops 2654208 | bytes 2658816 | tf_op jit(solution)/shard_map/dot_general | solution.py:38
  31.4 1.1 reduce.9
  32.5 0.8 reshape.172
  33.3 10.2 %all-to-all-start = ((bf16[32,2,576]{2,1,0:T(2,128)(2,1)}), bf16[32,2,576]{2,1,0:T(2,128)(2,1)S(1)}, u32[]{:S(2)}, u32[]{:S(2)}) async-start(bf16[32,2,576]{2,1,0:T(2,128)(2,1)} %reshape.172), calls=%async_computation | async-start | bytes 163840 | tf_op jit(solution)/shard_map/all_to_all | solution.py:155
  45.3 3.1 %collective-permute-start.2 = (bf16[32,1152]{1,0:T(8,128)(2,1)S(1)}, bf16[32,1152]{1,0:T(8,128)(2,1)S(1)}, u32[]{:S(2)}, u32[]{:S(2)}) collective-permute-start(bf16[32,1152]{1,0:T(8,128)(2,1)S(1)} %collective-permute-done.1), channel_id=1, source_target_pairs={{0,1},{1,2},{2,3},{3,0},{4,5},{5,6},{6,7},{7,4},{8,9},{9,10},{10,1... | collective-permute-start | bytes 221192 | tf_op jit(solution)/shard_map/ppermute | solution.py:84
  48.8 3.6 %collective-permute-done.2 = bf16[32,1152]{1,0:T(8,128)(2,1)S(1)} collective-permute-done((bf16[32,1152]{1,0:T(8,128)(2,1)S(1)}, bf16[32,1152]{1,0:T(8,128)(2,1)S(1)}, u32[]{:S(2)}, u32[]{:S(2)}) %collective-permute-start.2) | collective-permute-done | bytes 73760 | tf_op jit(solution)/shard_map/ppermute | solution.py:84
  53.2 3.1 %collective-permute-start.6 = (bf16[128,1152]{1,0:T(8,128)(2,1)}, bf16[128,1152]{1,0:T(8,128)(2,1)S(1)}, u32[]{:S(2)}, u32[]{:S(2)}) collective-permute-start(bf16[128,1152]{1,0:T(8,128)(2,1)} %pad_maximum_fusion), channel_id=1, source_target_pairs={{0,4},{4,8},{8,12},{12,16},{16,20},{20,24},{24,28},{28,0},{1,5},{5... | collective-permute-start | bytes 884744 | tf_op jit(solution)/shard_map/ppermute | solution.py:84
  57.9 3.4 %collective-permute-start.3 = (bf16[128,1152]{1,0:T(8,128)(2,1)}, bf16[128,1152]{1,0:T(8,128)(2,1)}, u32[]{:S(2)}, u32[]{:S(2)}) collective-permute-start(bf16[128,1152]{1,0:T(8,128)(2,1)} %pad_maximum_fusion), channel_id=1, source_target_pairs={{0,28},{4,0},{8,4},{12,8},{16,12},{20,16},{24,20},{28,24},{1,29},{... | collective-permute-start | bytes 884744 | tf_op jit(solution)/shard_map/ppermute | solution.py:84
  61.3 1.4 collective-permute-done.6
  62.6 1.9 collective-permute-start.7
  65.7 4.6 %collective-permute-start.4 = (bf16[128,1152]{1,0:T(8,128)(2,1)}, bf16[128,1152]{1,0:T(8,128)(2,1)}, u32[]{:S(2)}, u32[]{:S(2)}) collective-permute-start(bf16[128,1152]{1,0:T(8,128)(2,1)} %collective-permute-done.3), channel_id=1, source_target_pairs={{0,28},{4,0},{8,4},{12,8},{16,12},{20,16},{24,20},{28,24},{1,29},{... | collective-permute-start | bytes 884744 | tf_op jit(solution)/shard_map/ppermute | solution.py:84
  71.4 1.9 collective-permute-start.8
  74.2 5.0 %collective-permute-start.5 = (bf16[128,1152]{1,0:T(8,128)(2,1)}, bf16[128,1152]{1,0:T(8,128)(2,1)S(1)}, u32[]{:S(2)}, u32[]{:S(2)}) collective-permute-start(bf16[128,1152]{1,0:T(8,128)(2,1)} %collective-permute-done.4), channel_id=1, source_target_pairs={{0,28},{4,0},{8,4},{12,8},{16,12},{20,16},{24,20},{28,24},{1,29},{... | collective-permute-start | bytes 884744 | tf_op jit(solution)/shard_map/ppermute | solution.py:84
  79.2 1.7 constant_dynamic-update-slice_fusion.6
  80.9 2.1 collective-permute-start.9
  83.0 1.7 constant_dynamic-update-slice_fusion.5
  85.4 4.4 %collective-permute-done.9 = bf16[128,1152]{1,0:T(8,128)(2,1)S(1)} collective-permute-done((bf16[128,1152]{1,0:T(8,128)(2,1)}, bf16[128,1152]{1,0:T(8,128)(2,1)S(1)}, u32[]{:S(2)}, u32[]{:S(2)}) %collective-permute-start.9) | collective-permute-done | bytes 294944 | tf_op jit(solution)/shard_map/ppermute | solution.py:84
  90.5 1.7 constant_dynamic-update-slice_fusion.2
  92.2 1.7 constant_dynamic-update-slice_fusion.1
  95.3 34.9 %all-gather.2.cloned.1.call-done = bf16[768,1152]{1,0:T(8,128)(2,1)} async-done(((bf16[32,1152]{1,0:T(8,128)(2,1)}), bf16[768,1152]{1,0:T(8,128)(2,1)}) %all-gather.2.cloned.1.call-update) | async-done | bytes 1769488 | tf_op jit(solution)/shard_map/all_gather | solution.py:139
  130.3 1.8 copy.18
  132.5 3.9 %fusion.6 = (f32[1056]{0:T(1024)S(1)}, f32[1056,768]{1,0:T(8,128)S(1)}) fusion(s32[768]{0:T(1024)S(1)} %add.265, s32[1056]{0:T(1024)S(1)} %pad_add_fusion, f32[]{:T(128)} %bitcast.59, bf16[1056,1152]{1,0:T(8,128)(2,1)S(1)} %copy-done.5, bf16[768,1152]{1,0:T(8,128)(2,1)S(1)} %bitcast.65, f32[]{:T(128)} %bitcast.57), kind=kOutput, calls=%fused_computation.11 | convolution fusion | flops 1878293504 | bytes 7458056 | tf_op jit(solution)/shard_map/dot_general | solution.py:59
  136.3 3.0 %fusion.11 = f32[768,1152]{1,0:T(8,128)S(1)} fusion(bf16[1056,1152]{1,0:T(8,128)(2,1)S(1)} %copy-done.5, f32[1056,768]{1,0:T(8,128)S(1)} %get-tuple-element.14, f32[]{:T(128)} %bitcast.58, s32[768]{0:T(1024)S(1)} %add.265, s32[1056]{0:T(1024)S(1)} %pad_add_fusion), kind=kOutput, calls=%fused_computation.20 | convolution fusion | flops 1875050496 | bytes 9223300 | tf_op jit(solution)/shard_map/dot_general | solution.py:74
  139.3 1.7 copy-done.2
  141.1 1.4 dynamic-slice_bitcast_fusion
  142.4 2.1 collective-permute-start.10
  144.6 3.7 %collective-permute-done.10 = f32[384,1152]{1,0:T(8,128)} collective-permute-done((f32[384,1152]{1,0:T(8,128)}, f32[384,1152]{1,0:T(8,128)}, u32[]{:S(2)}, u32[]{:S(2)}) %collective-permute-start.10) | collective-permute-done | bytes 1769504 | tf_op jit(solution)/shard_map/ppermute | solution.py:84
  148.4 2.2 bitcast_add_fusion
  150.6 1.2 copy-done.1
  151.8 1.1 dynamic-slice_bitcast_fusion.3
  152.9 3.4 %collective-permute-start.13 = (f32[96,1152]{1,0:T(8,128)}, f32[96,1152]{1,0:T(8,128)S(1)}, u32[]{:S(2)}, u32[]{:S(2)}) collective-permute-start(f32[96,1152]{1,0:T(8,128)} %get-tuple-element.7), channel_id=1, source_target_pairs={{0,576},{192,0},{384,192},{576,384},{1,577},{193,1},{385,193},{577... | collective-permute-start | bytes 1327112 | tf_op jit(solution)/shard_map/ppermute | solution.py:84
  156.2 2.5 %collective-permute-start.12 = (f32[96,1152]{1,0:T(8,128)}, f32[96,1152]{1,0:T(8,128)}, u32[]{:S(2)}, u32[]{:S(2)}) collective-permute-start(f32[96,1152]{1,0:T(8,128)} %get-tuple-element.8), channel_id=1, source_target_pairs={{0,384},{192,576},{384,0},{576,192},{1,385},{193,577},{385,1},{577... | collective-permute-start | bytes 1327112 | tf_op jit(solution)/shard_map/ppermute | solution.py:84
  158.7 2.5 %collective-permute-start.11 = (f32[96,1152]{1,0:T(8,128)}, f32[96,1152]{1,0:T(8,128)}, u32[]{:S(2)}, u32[]{:S(2)}) collective-permute-start(f32[96,1152]{1,0:T(8,128)} %get-tuple-element.6), channel_id=1, source_target_pairs={{0,192},{192,384},{384,576},{576,0},{1,193},{193,385},{385,577},{5... | collective-permute-start | bytes 1327112 | tf_op jit(solution)/shard_map/ppermute | solution.py:84
  161.4 5.2 %collective-permute-done.13 = f32[96,1152]{1,0:T(8,128)S(1)} collective-permute-done((f32[96,1152]{1,0:T(8,128)}, f32[96,1152]{1,0:T(8,128)S(1)}, u32[]{:S(2)}, u32[]{:S(2)}) %collective-permute-start.13) | collective-permute-done | bytes 442400 | tf_op jit(solution)/shard_map/ppermute | solution.py:84
  166.6 4.6 %collective-permute-done.12 = f32[96,1152]{1,0:T(8,128)} collective-permute-done((f32[96,1152]{1,0:T(8,128)}, f32[96,1152]{1,0:T(8,128)}, u32[]{:S(2)}, u32[]{:S(2)}) %collective-permute-start.12) | collective-permute-done | bytes 442400 | tf_op jit(solution)/shard_map/ppermute | solution.py:84
  171.2 10.3 %collective-permute-done.11 = f32[96,1152]{1,0:T(8,128)} collective-permute-done((f32[96,1152]{1,0:T(8,128)}, f32[96,1152]{1,0:T(8,128)}, u32[]{:S(2)}, u32[]{:S(2)}) %collective-permute-start.11) | collective-permute-done | bytes 442400 | tf_op jit(solution)/shard_map/ppermute | solution.py:84
  181.5 1.5 fusion.19
  183.7 5.5 %collective-permute-start.15 = (f32[32,1152]{1,0:T(8,128)}, f32[32,1152]{1,0:T(8,128)S(1)}, u32[]{:S(2)}, u32[]{:S(2)}) collective-permute-start(f32[32,1152]{1,0:T(8,128)} %get-tuple-element.10), channel_id=1, source_target_pairs={{0,128},{64,0},{128,64},{1,129},{65,1},{129,65},{2,130},{66,2},{13... | collective-permute-start | bytes 442376 | tf_op jit(solution)/shard_map/ppermute | solution.py:84
  189.2 3.7 %collective-permute-start.14 = (f32[32,1152]{1,0:T(8,128)S(1)}, f32[32,1152]{1,0:T(8,128)}, u32[]{:S(2)}, u32[]{:S(2)}) collective-permute-start(f32[32,1152]{1,0:T(8,128)S(1)} %get-tuple-element.9), channel_id=1, source_target_pairs={{0,64},{64,128},{128,0},{1,65},{65,129},{129,1},{2,66},{66,130},{1... | collective-permute-start | bytes 442376 | tf_op jit(solution)/shard_map/ppermute | solution.py:84
  193.7 10.1 %all-to-all-start.1 = ((f32[32,1,32]{2,1,0:T(1,128)}), f32[32,1,32]{2,1,0:T(1,128)S(1)}, u32[]{:S(2)}, u32[]{:S(2)}) async-start(f32[32,1,32]{2,1,0:T(1,128)} %bitcast.8), calls=%async_computation.1 | async-start | bytes 32768 | tf_op jit(solution)/shard_map/all_to_all | solution.py:210
  203.8 9.0 %all-to-all-done.1 = f32[32,1,32]{2,1,0:T(1,128)S(1)} async-done(((f32[32,1,32]{2,1,0:T(1,128)}), f32[32,1,32]{2,1,0:T(1,128)S(1)}, u32[]{:S(2)}, u32[]{:S(2)}) %all-to-all-start.1) | async-done | bytes 4128 | tf_op jit(solution)/shard_map/all_to_all | solution.py:210
  213.3 1.1 fusion.29
  (67 shorter events, 14.3 us)
Async XLA Ops:
  7.2 17.5 %copy-start = (bf16[1152,1152]{1,0:T(8,128)(2,1)S(1)}, bf16[1152,1152]{1,0:T(8,128)(2,1)}, u32[]{:S(2)}) copy-start(bf16[1152,1152]{1,0:T(8,128)(2,1)} %param.13) | copy-start | bytes 7962628
  9.9 38.9 %collective-permute-start = (bf16[32,1152]{1,0:T(8,128)(2,1)S(1)}, bf16[32,1152]{1,0:T(8,128)(2,1)S(1)}, u32[]{:S(2)}, u32[]{:S(2)}) collective-permute-start(bf16[32,1152]{1,0:T(8,128)(2,1)S(1)} %get-tuple-element.5), channel_id=1, source_target_pairs={{0,3},{1,0},{2,1},{3,2},{4,7},{5,4},{6,5},{7,6},{8,11},{9,8},{10,9... | collective-permute-start | bytes 221192 | tf_op jit(solution)/shard_map/ppermute | solution.py:84
  18.4 26.9 %collective-permute-start.1 = (bf16[32,1152]{1,0:T(8,128)(2,1)S(1)}, bf16[32,1152]{1,0:T(8,128)(2,1)S(1)}, u32[]{:S(2)}, u32[]{:S(2)}) collective-permute-start(bf16[32,1152]{1,0:T(8,128)(2,1)S(1)} %get-tuple-element.5), channel_id=1, source_target_pairs={{0,1},{1,2},{2,3},{3,0},{4,5},{5,6},{6,7},{7,4},{8,9},{9,10},{10,1... | collective-permute-start | bytes 221192 | tf_op jit(solution)/shard_map/ppermute | solution.py:84
  26.9 16.6 %copy-start.3 = (bf16[32,1152]{1,0:T(8,128)(2,1)S(1)}, bf16[32,1152]{1,0:T(8,128)(2,1)}, u32[]{:S(2)}) copy-start(bf16[32,1152]{1,0:T(8,128)(2,1)} %param.16) | copy-start | bytes 221188
  33.3 40.7 %all-to-all-start = ((bf16[32,2,576]{2,1,0:T(2,128)(2,1)}), bf16[32,2,576]{2,1,0:T(2,128)(2,1)S(1)}, u32[]{:S(2)}, u32[]{:S(2)}) async-start(bf16[32,2,576]{2,1,0:T(2,128)(2,1)} %reshape.172), calls=%async_computation | async-start | bytes 163840 | tf_op jit(solution)/shard_map/all_to_all | solution.py:155
  43.4 86.8 %all-gather.2.cloned.1.call-start = ((), (), s32[]{:S(2)}) async-start(), calls=%async_computation.2 | async-start | bytes 1843200 | tf_op jit(solution)/shard_map/all_gather | solution.py:139
  45.3 7.2 %collective-permute-start.2 = (bf16[32,1152]{1,0:T(8,128)(2,1)S(1)}, bf16[32,1152]{1,0:T(8,128)(2,1)S(1)}, u32[]{:S(2)}, u32[]{:S(2)}) collective-permute-start(bf16[32,1152]{1,0:T(8,128)(2,1)S(1)} %collective-permute-done.1), channel_id=1, source_target_pairs={{0,1},{1,2},{2,3},{3,0},{4,5},{5,6},{6,7},{7,4},{8,9},{9,10},{10,1... | collective-permute-start | bytes 221192 | tf_op jit(solution)/shard_map/ppermute | solution.py:84
  53.2 9.4 %collective-permute-start.6 = (bf16[128,1152]{1,0:T(8,128)(2,1)}, bf16[128,1152]{1,0:T(8,128)(2,1)S(1)}, u32[]{:S(2)}, u32[]{:S(2)}) collective-permute-start(bf16[128,1152]{1,0:T(8,128)(2,1)} %pad_maximum_fusion), channel_id=1, source_target_pairs={{0,4},{4,8},{8,12},{12,16},{16,20},{20,24},{24,28},{28,0},{1,5},{5... | collective-permute-start | bytes 884744 | tf_op jit(solution)/shard_map/ppermute | solution.py:84
  57.9 7.8 %collective-permute-start.3 = (bf16[128,1152]{1,0:T(8,128)(2,1)}, bf16[128,1152]{1,0:T(8,128)(2,1)}, u32[]{:S(2)}, u32[]{:S(2)}) collective-permute-start(bf16[128,1152]{1,0:T(8,128)(2,1)} %pad_maximum_fusion), channel_id=1, source_target_pairs={{0,28},{4,0},{8,4},{12,8},{16,12},{20,16},{24,20},{28,24},{1,29},{... | collective-permute-start | bytes 884744 | tf_op jit(solution)/shard_map/ppermute | solution.py:84
  62.6 8.8 %collective-permute-start.7 = (bf16[128,1152]{1,0:T(8,128)(2,1)S(1)}, bf16[128,1152]{1,0:T(8,128)(2,1)}, u32[]{:S(2)}, u32[]{:S(2)}) collective-permute-start(bf16[128,1152]{1,0:T(8,128)(2,1)S(1)} %collective-permute-done.6), channel_id=1, source_target_pairs={{0,4},{4,8},{8,12},{12,16},{16,20},{20,24},{24,28},{28,0},{1,5},{5... | collective-permute-start | bytes 884744 | tf_op jit(solution)/shard_map/ppermute | solution.py:84
  65.7 8.5 %collective-permute-start.4 = (bf16[128,1152]{1,0:T(8,128)(2,1)}, bf16[128,1152]{1,0:T(8,128)(2,1)}, u32[]{:S(2)}, u32[]{:S(2)}) collective-permute-start(bf16[128,1152]{1,0:T(8,128)(2,1)} %collective-permute-done.3), channel_id=1, source_target_pairs={{0,28},{4,0},{8,4},{12,8},{16,12},{20,16},{24,20},{28,24},{1,29},{... | collective-permute-start | bytes 884744 | tf_op jit(solution)/shard_map/ppermute | solution.py:84
  71.4 9.5 %collective-permute-start.8 = (bf16[128,1152]{1,0:T(8,128)(2,1)}, bf16[128,1152]{1,0:T(8,128)(2,1)}, u32[]{:S(2)}, u32[]{:S(2)}) collective-permute-start(bf16[128,1152]{1,0:T(8,128)(2,1)} %collective-permute-done.7), channel_id=1, source_target_pairs={{0,4},{4,8},{8,12},{12,16},{16,20},{20,24},{24,28},{28,0},{1,5},{5... | collective-permute-start | bytes 884744 | tf_op jit(solution)/shard_map/ppermute | solution.py:84
  74.2 10.5 %collective-permute-start.5 = (bf16[128,1152]{1,0:T(8,128)(2,1)}, bf16[128,1152]{1,0:T(8,128)(2,1)S(1)}, u32[]{:S(2)}, u32[]{:S(2)}) collective-permute-start(bf16[128,1152]{1,0:T(8,128)(2,1)} %collective-permute-done.4), channel_id=1, source_target_pairs={{0,28},{4,0},{8,4},{12,8},{16,12},{20,16},{24,20},{28,24},{1,29},{... | collective-permute-start | bytes 884744 | tf_op jit(solution)/shard_map/ppermute | solution.py:84
  80.9 8.9 %collective-permute-start.9 = (bf16[128,1152]{1,0:T(8,128)(2,1)}, bf16[128,1152]{1,0:T(8,128)(2,1)S(1)}, u32[]{:S(2)}, u32[]{:S(2)}) collective-permute-start(bf16[128,1152]{1,0:T(8,128)(2,1)} %collective-permute-done.8), channel_id=1, source_target_pairs={{0,4},{4,8},{8,12},{12,16},{16,20},{20,24},{24,28},{28,0},{1,5},{5... | collective-permute-start | bytes 884744 | tf_op jit(solution)/shard_map/ppermute | solution.py:84
  130.3 2.2 copy-start.5
  139.3 1.8 copy-start.2
  142.4 5.9 %collective-permute-start.10 = (f32[384,1152]{1,0:T(8,128)}, f32[384,1152]{1,0:T(8,128)}, u32[]{:S(2)}, u32[]{:S(2)}) collective-permute-start(f32[384,1152]{1,0:T(8,128)} %dynamic-slice_bitcast_fusion), channel_id=1, source_target_pairs={{0,32},{32,0},{1,33},{33,1},{2,34},{34,2},{3,35},{35,3},{4,36},{36... | collective-permute-start | bytes 5308424 | tf_op jit(solution)/shard_map/ppermute | solution.py:84
  150.6 1.2 copy-start.1
  152.9 13.7 %collective-permute-start.13 = (f32[96,1152]{1,0:T(8,128)}, f32[96,1152]{1,0:T(8,128)S(1)}, u32[]{:S(2)}, u32[]{:S(2)}) collective-permute-start(f32[96,1152]{1,0:T(8,128)} %get-tuple-element.7), channel_id=1, source_target_pairs={{0,576},{192,0},{384,192},{576,384},{1,577},{193,1},{385,193},{577... | collective-permute-start | bytes 1327112 | tf_op jit(solution)/shard_map/ppermute | solution.py:84
  156.2 15.0 %collective-permute-start.12 = (f32[96,1152]{1,0:T(8,128)}, f32[96,1152]{1,0:T(8,128)}, u32[]{:S(2)}, u32[]{:S(2)}) collective-permute-start(f32[96,1152]{1,0:T(8,128)} %get-tuple-element.8), channel_id=1, source_target_pairs={{0,384},{192,576},{384,0},{576,192},{1,385},{193,577},{385,1},{577... | collective-permute-start | bytes 1327112 | tf_op jit(solution)/shard_map/ppermute | solution.py:84
  158.7 22.8 %collective-permute-start.11 = (f32[96,1152]{1,0:T(8,128)}, f32[96,1152]{1,0:T(8,128)}, u32[]{:S(2)}, u32[]{:S(2)}) collective-permute-start(f32[96,1152]{1,0:T(8,128)} %get-tuple-element.6), channel_id=1, source_target_pairs={{0,192},{192,384},{384,576},{576,0},{1,193},{193,385},{385,577},{5... | collective-permute-start | bytes 1327112 | tf_op jit(solution)/shard_map/ppermute | solution.py:84
  166.6 4.6 %copy-start.4 = (f32[96,1152]{1,0:T(8,128)}, f32[96,1152]{1,0:T(8,128)S(1)}, u32[]{:S(2)}) copy-start(f32[96,1152]{1,0:T(8,128)S(1)} %collective-permute-done.13) | copy-start | bytes 1327108
  183.7 29.6 %collective-permute-start.15 = (f32[32,1152]{1,0:T(8,128)}, f32[32,1152]{1,0:T(8,128)S(1)}, u32[]{:S(2)}, u32[]{:S(2)}) collective-permute-start(f32[32,1152]{1,0:T(8,128)} %get-tuple-element.10), channel_id=1, source_target_pairs={{0,128},{64,0},{128,64},{1,129},{65,1},{129,65},{2,130},{66,2},{13... | collective-permute-start | bytes 442376 | tf_op jit(solution)/shard_map/ppermute | solution.py:84
  189.2 24.1 %collective-permute-start.14 = (f32[32,1152]{1,0:T(8,128)S(1)}, f32[32,1152]{1,0:T(8,128)}, u32[]{:S(2)}, u32[]{:S(2)}) collective-permute-start(f32[32,1152]{1,0:T(8,128)S(1)} %get-tuple-element.9), channel_id=1, source_target_pairs={{0,64},{64,128},{128,0},{1,65},{65,129},{129,1},{2,66},{66,130},{1... | collective-permute-start | bytes 442376 | tf_op jit(solution)/shard_map/ppermute | solution.py:84
  193.7 19.0 %all-to-all-start.1 = ((f32[32,1,32]{2,1,0:T(1,128)}), f32[32,1,32]{2,1,0:T(1,128)S(1)}, u32[]{:S(2)}, u32[]{:S(2)}) async-start(f32[32,1,32]{2,1,0:T(1,128)} %bitcast.8), calls=%async_computation.1 | async-start | bytes 32768 | tf_op jit(solution)/shard_map/all_to_all | solution.py:210
Sparse Core Ops, SparseCore 0:
  48.3 81.9 all-gather.1

commit v3 on v2

--- a/solution.py
+++ b/solution.py
@@ -84,18 +84,21 @@
     return lax.ppermute(x, axis, [(i, (i + step) % size) for i in range(size)])
 
 
-def ring_gather(x, axis, size):
+def ring_gather(x, axis, size, held=None, held_step=0):
     forward, backward = x, x
     arrived = {0: x}
     forward_steps = size // 2
     backward_steps = size - 1 - forward_steps
     for step in range(1, forward_steps + 1):
+        if held is not None and step == held_step:
+            forward, held = lax.optimization_barrier((forward, held))
         forward = shift_ring(forward, axis, size, 1)
         arrived[(size - step) % size] = forward
         if step <= backward_steps:
             backward = shift_ring(backward, axis, size, -1)
             arrived[step] = backward
-    return jnp.concatenate([arrived[d] for d in range(size)], axis=0)
+    tile = jnp.concatenate([arrived[d] for d in range(size)], axis=0)
+    return tile if held is None else (tile, held)
 
 
 def direct_scatter(x, axis, size):
@@ -142,7 +145,13 @@
     prior_norm = normalize_rows(
         jnp.pad(prior_picture_entries, ((0, chunk_rows - prior_count), (0, 0)))
     )[0].astype(jnp.bfloat16)
-    prior_tile = ring_gather(ring_gather(prior_norm, "mp", mp_size), "section", section_size)
+    prior_tile, device_portion_count = ring_gather(
+        ring_gather(prior_norm, "mp", mp_size),
+        "section",
+        section_size,
+        held=device_portion_count,
+        held_step=section_size // 2,
+    )
 
     pooled = pool_image(
         patch_features_window[0],

time: 223 us -> 211 us (0.946)
  waiting for transfers between devices: 78.2 us -> 66.4 us
  local copies, waits for them, and re-layouts: 23 us -> 19.1 us
    all_gather x1, waiting for transfers between devices: 34.9 us -> 21.9 us  [local(): lax.all_gather(caption_magnitude, ('x', 'zh', 'core'), axis=0, tiled=True)]
    unnamed x24, local copies, waits for them, and re-layouts: 15.3 us -> 12 us
where the time goes in v3:
time: 211 us; the launch traced here: 209 us
  starting transfers between devices  76.8 us (36%)
  waiting for transfers between devices  66.4 us (31%)
  local copies, waits for them, and re-layouts  19.1 us (9%)
  between operations  16.5 us (8%)
  matrix products  15.4 us (7%)
  other arithmetic  15.2 us (7%)
    ppermute x16, starting transfers between devices, shift_ring(): return lax.ppermute(x, axis, [(i, (i + step) % size) for i in range(size)])  56.5 us
    ppermute x16, waiting for transfers between devices, shift_ring(): return lax.ppermute(x, axis, [(i, (i + step) % size) for i in range(size)])  35.5 us
    all_gather x1, waiting for transfers between devices, local(): lax.all_gather(caption_magnitude, ('x', 'zh', 'core'), axis=0, tiled=True)  21.9 us
    unnamed x24, local copies, waits for them, and re-layouts  12 us
    all_to_all x1, starting transfers between devices, local(): lax.all_to_all(jnp.broadcast_to(pooled_norm, (inner_size, pooled_norm.sha...  10.2 us
    all_to_all x1, starting transfers between devices, local(): lax.all_to_all(loss_parts, ('section', 'mp'), 0, 0, tiled=True)  10.1 us
    all_to_all x1, waiting for transfers between devices, local(): lax.all_to_all(loss_parts, ('section', 'mp'), 0, 0, tiled=True)  8.97 us
  transfers between devices with their start and end apart: 19, of which 12 were waited for; matrix products, arithmetic and copies ran while one was open for 13% of the time, Pallas kernels for 0%

profile of v3, /device:TPU:1, one launch (start us, length us, event | category | flops | bytes accessed | tf_op | source)
XLA Modules:
  0.0 209.5 jit_solution(13177465785089554211)
XLA Ops:
  7.2 1.2 fusion.27
  8.4 1.6 constant_dynamic-update-slice_fusion.10
  10.0 8.4 %collective-permute-start = (bf16[32,1152]{1,0:T(8,128)(2,1)S(1)}, bf16[32,1152]{1,0:T(8,128)(2,1)S(1)}, u32[]{:S(2)}, u32[]{:S(2)}) collective-permute-start(bf16[32,1152]{1,0:T(8,128)(2,1)S(1)} %get-tuple-element.9), channel_id=1, source_target_pairs={{0,3},{1,0},{2,1},{3,2},{4,7},{5,4},{6,5},{7,6},{8,11},{9,8},{10,9... | collective-permute-start | bytes 221192 | tf_op jit(solution)/shard_map/ppermute | solution.py:84
  18.4 1.9 collective-permute-start.1
  20.4 1.0 fusion.32
  21.4 1.6 fusion.26
  23.0 4.1 %fusion.68 = (f32[16]{0:T(128)S(1)}, f32[16,729]{1,0:T(8,128)S(1)}) fusion(bf16[1,729,1152]{2,1,0:T(8,128)(2,1)} %param.10, bf16[1152,1152]{1,0:T(8,128)(2,1)} %param.12, s32[1152]{0:T(1024)S(1)} %add_select_fusion, bf16[1152]{0:T(1024)(128)(2,1)} %param.11), kind=kOutput, calls=%fused_computation.126 | convolution fusion | flops 69426560 | bytes 4387456 | tf_op jit(solution)/shard_map/dot_general | solution.py:24
  27.4 2.2 %fusion.15 = f32[16,1152]{1,0:T(8,128)S(1)} fusion(bf16[1152,1152]{1,0:T(8,128)(2,1)S(1)} %copy-done, bf16[1,729,1152]{2,1,0:T(8,128)(2,1)} %param.10, f32[16,729]{1,0:T(8,128)S(1)} %get-tuple-element.16, f32[16]{0:T(128)S(1)} %fusion.38, f32[16]{0:T(128)S(1)} %get-tuple-element.15), kind=kOutput, calls=%fused_computation.22 | convolution fusion | flops 69394608 | bytes 4454336 | tf_op jit(solution)/shard_map/dot_general | solution.py:31
  30.0 2.2 %convolution_reduce_fusion = bf16[1152]{0:T(1024)(128)(2,1)S(1)} fusion(bf16[1152,1]{0,1:T(2,128)(2,1)S(1)} %reshape.167, bf16[1152,1152]{1,0:T(8,128)(2,1)} %param.14), kind=kOutput, calls=%fused_computation.23 | convolution fusion | flops 2654208 | bytes 2658816 | tf_op jit(solution)/shard_map/dot_general | solution.py:38
  34.1 1.1 reduce.9
  35.9 10.2 %all-to-all-start = ((bf16[32,2,576]{2,1,0:T(2,128)(2,1)}), bf16[32,2,576]{2,1,0:T(2,128)(2,1)S(1)}, u32[]{:S(2)}, u32[]{:S(2)}) async-start(bf16[32,2,576]{2,1,0:T(2,128)(2,1)} %reshape.172), calls=%async_computation | async-start | bytes 163840 | tf_op jit(solution)/shard_map/all_to_all | solution.py:164
  47.1 3.1 %collective-permute-start.2 = (bf16[32,1152]{1,0:T(8,128)(2,1)S(1)}, bf16[32,1152]{1,0:T(8,128)(2,1)S(1)}, u32[]{:S(2)}, u32[]{:S(2)}) collective-permute-start(bf16[32,1152]{1,0:T(8,128)(2,1)S(1)} %collective-permute-done.1), channel_id=1, source_target_pairs={{0,1},{1,2},{2,3},{3,0},{4,5},{5,6},{6,7},{7,4},{8,9},{9,10},{10,1... | collective-permute-start | bytes 221192 | tf_op jit(solution)/shard_map/ppermute | solution.py:84
  50.5 4.2 %collective-permute-done.2 = bf16[32,1152]{1,0:T(8,128)(2,1)S(1)} collective-permute-done((bf16[32,1152]{1,0:T(8,128)(2,1)S(1)}, bf16[32,1152]{1,0:T(8,128)(2,1)S(1)}, u32[]{:S(2)}, u32[]{:S(2)}) %collective-permute-start.2) | collective-permute-done | bytes 73760 | tf_op jit(solution)/shard_map/ppermute | solution.py:84
  55.5 3.1 %collective-permute-start.6 = (bf16[128,1152]{1,0:T(8,128)(2,1)}, bf16[128,1152]{1,0:T(8,128)(2,1)S(1)}, u32[]{:S(2)}, u32[]{:S(2)}) collective-permute-start(bf16[128,1152]{1,0:T(8,128)(2,1)} %pad_maximum_fusion), channel_id=1, source_target_pairs={{0,4},{4,8},{8,12},{12,16},{16,20},{20,24},{24,28},{28,0},{1,5},{5... | collective-permute-start | bytes 884744 | tf_op jit(solution)/shard_map/ppermute | solution.py:84
  60.2 3.4 %collective-permute-start.3 = (bf16[128,1152]{1,0:T(8,128)(2,1)}, bf16[128,1152]{1,0:T(8,128)(2,1)}, u32[]{:S(2)}, u32[]{:S(2)}) collective-permute-start(bf16[128,1152]{1,0:T(8,128)(2,1)} %pad_maximum_fusion), channel_id=1, source_target_pairs={{0,28},{4,0},{8,4},{12,8},{16,12},{20,16},{24,20},{28,24},{1,29},{... | collective-permute-start | bytes 884744 | tf_op jit(solution)/shard_map/ppermute | solution.py:84
  63.6 1.5 collective-permute-done.6
  65.0 1.9 collective-permute-start.7
  68.0 4.9 %collective-permute-start.4 = (bf16[128,1152]{1,0:T(8,128)(2,1)}, bf16[128,1152]{1,0:T(8,128)(2,1)}, u32[]{:S(2)}, u32[]{:S(2)}) collective-permute-start(bf16[128,1152]{1,0:T(8,128)(2,1)} %collective-permute-done.3), channel_id=1, source_target_pairs={{0,28},{4,0},{8,4},{12,8},{16,12},{20,16},{24,20},{28,24},{1,29},{... | collective-permute-start | bytes 884744 | tf_op jit(solution)/shard_map/ppermute | solution.py:84
  73.8 1.9 collective-permute-start.8
  76.9 5.0 %collective-permute-start.5 = (bf16[128,1152]{1,0:T(8,128)(2,1)}, bf16[128,1152]{1,0:T(8,128)(2,1)S(1)}, u32[]{:S(2)}, u32[]{:S(2)}) collective-permute-start(bf16[128,1152]{1,0:T(8,128)(2,1)} %collective-permute-done.4), channel_id=1, source_target_pairs={{0,28},{4,0},{8,4},{12,8},{16,12},{20,16},{24,20},{28,24},{1,29},{... | collective-permute-start | bytes 884744 | tf_op jit(solution)/shard_map/ppermute | solution.py:84
  81.9 1.7 constant_dynamic-update-slice_fusion.6
  83.6 21.9 %all-gather.2.cloned.1.call-done = bf16[768,1152]{1,0:T(8,128)(2,1)} async-done(((bf16[32,1152]{1,0:T(8,128)(2,1)}), bf16[768,1152]{1,0:T(8,128)(2,1)}) %all-gather.2.cloned.1.call-update) | async-done | bytes 1769488 | tf_op jit(solution)/shard_map/all_gather | solution.py:142
  105.5 2.3 %collective-permute-start.9 = (bf16[128,1152]{1,0:T(8,128)(2,1)}, bf16[128,1152]{1,0:T(8,128)(2,1)S(1)}, u32[]{:S(2)}, u32[]{:S(2)}) collective-permute-start(bf16[128,1152]{1,0:T(8,128)(2,1)} %collective-permute-done.8), channel_id=1, source_target_pairs={{0,4},{4,8},{8,12},{12,16},{16,20},{20,24},{24,28},{28,0},{1,5},{5... | collective-permute-start | bytes 884744 | tf_op jit(solution)/shard_map/ppermute | solution.py:84
  107.8 1.7 constant_dynamic-update-slice_fusion.5
  110.2 1.8 copy.18
  112.0 5.1 %collective-permute-done.9 = bf16[128,1152]{1,0:T(8,128)(2,1)S(1)} collective-permute-done((bf16[128,1152]{1,0:T(8,128)(2,1)}, bf16[128,1152]{1,0:T(8,128)(2,1)S(1)}, u32[]{:S(2)}, u32[]{:S(2)}) %collective-permute-start.9) | collective-permute-done | bytes 294944 | tf_op jit(solution)/shard_map/ppermute | solution.py:84
  117.2 1.0 constant_dynamic-update-slice_fusion.2
  119.2 3.8 %fusion.6 = (f32[1056]{0:T(1024)S(1)}, f32[1056,768]{1,0:T(8,128)S(1)}) fusion(s32[768]{0:T(1024)S(1)} %add.265, s32[1056]{0:T(1024)S(1)} %pad_add_fusion, f32[]{:T(128)} %bitcast.59, bf16[1056,1152]{1,0:T(8,128)(2,1)S(1)} %bitcast_dynamic-update-slice_fusion, bf16[768,1152]{1,0:T(8,128)(2,1)S(1)} %bitcast.65, f32[]{:T(128)} %bitcast.57), kind=kOutput, calls=%fused_computation.11 | convolution fusion | flops 1878293504 | bytes 7458056 | tf_op jit(solution)/shard_map/dot_general | solution.py:59
  123.1 3.0 %fusion.11 = f32[768,1152]{1,0:T(8,128)S(1)} fusion(bf16[1056,1152]{1,0:T(8,128)(2,1)S(1)} %bitcast_dynamic-update-slice_fusion, f32[1056,768]{1,0:T(8,128)S(1)} %get-tuple-element.18, f32[]{:T(128)} %bitcast.58, s32[768]{0:T(1024)S(1)} %add.265, s32[1056]{0:T(1024)S(1)} %pad_add_fusion), kind=kOutput, calls=%fused_computation.20 | convolution fusion | flops 1875050496 | bytes 9223300 | tf_op jit(solution)/shard_map/dot_general | solution.py:74
  126.1 1.7 copy-done.2
  127.8 1.4 dynamic-slice_bitcast_fusion
  129.2 2.9 %collective-permute-start.10 = (f32[384,1152]{1,0:T(8,128)}, f32[384,1152]{1,0:T(8,128)}, u32[]{:S(2)}, u32[]{:S(2)}) collective-permute-start(f32[384,1152]{1,0:T(8,128)} %dynamic-slice_bitcast_fusion), channel_id=1, source_target_pairs={{0,32},{32,0},{1,33},{33,1},{2,34},{34,2},{3,35},{35,3},{4,36},{36... | collective-permute-start | bytes 5308424 | tf_op jit(solution)/shard_map/ppermute | solution.py:84
  132.2 3.6 %collective-permute-done.10 = f32[384,1152]{1,0:T(8,128)} collective-permute-done((f32[384,1152]{1,0:T(8,128)}, f32[384,1152]{1,0:T(8,128)}, u32[]{:S(2)}, u32[]{:S(2)}) %collective-permute-start.10) | collective-permute-done | bytes 1769504 | tf_op jit(solution)/shard_map/ppermute | solution.py:84
  135.8 2.2 %bitcast_add_fusion = f32[384,1152]{1,0:T(8,128)S(1)} fusion(f32[384,1152]{1,0:T(8,128)} %collective-permute-done.10, f32[2,384,1152]{2,1,0:T(8,128)} %bitcast.63, s32[]{:T(128)S(6)} %select_n.174), kind=kLoop, calls=%fused_computation.15 | loop fusion | flops 442368 | bytes 5308420 | tf_op jit(solution)/shard_map/add | solution.py:110
  138.0 1.2 copy-done.1
  139.2 1.1 dynamic-slice_bitcast_fusion.3
  140.3 3.4 %collective-permute-start.13 = (f32[96,1152]{1,0:T(8,128)}, f32[96,1152]{1,0:T(8,128)S(1)}, u32[]{:S(2)}, u32[]{:S(2)}) collective-permute-start(f32[96,1152]{1,0:T(8,128)} %get-tuple-element.11), channel_id=1, source_target_pairs={{0,576},{192,0},{384,192},{576,384},{1,577},{193,1},{385,193},{577... | collective-permute-start | bytes 1327112 | tf_op jit(solution)/shard_map/ppermute | solution.py:84
  143.7 2.5 %collective-permute-start.12 = (f32[96,1152]{1,0:T(8,128)}, f32[96,1152]{1,0:T(8,128)}, u32[]{:S(2)}, u32[]{:S(2)}) collective-permute-start(f32[96,1152]{1,0:T(8,128)} %get-tuple-element.12), channel_id=1, source_target_pairs={{0,384},{192,576},{384,0},{576,192},{1,385},{193,577},{385,1},{577... | collective-permute-start | bytes 1327112 | tf_op jit(solution)/shard_map/ppermute | solution.py:84
  146.1 2.5 %collective-permute-start.11 = (f32[96,1152]{1,0:T(8,128)}, f32[96,1152]{1,0:T(8,128)}, u32[]{:S(2)}, u32[]{:S(2)}) collective-permute-start(f32[96,1152]{1,0:T(8,128)} %get-tuple-element.10), channel_id=1, source_target_pairs={{0,192},{192,384},{384,576},{576,0},{1,193},{193,385},{385,577},{5... | collective-permute-start | bytes 1327112 | tf_op jit(solution)/shard_map/ppermute | solution.py:84
  148.9 5.0 %collective-permute-done.13 = f32[96,1152]{1,0:T(8,128)S(1)} collective-permute-done((f32[96,1152]{1,0:T(8,128)}, f32[96,1152]{1,0:T(8,128)S(1)}, u32[]{:S(2)}, u32[]{:S(2)}) %collective-permute-start.13) | collective-permute-done | bytes 442400 | tf_op jit(solution)/shard_map/ppermute | solution.py:84
  153.9 4.6 %collective-permute-done.12 = f32[96,1152]{1,0:T(8,128)} collective-permute-done((f32[96,1152]{1,0:T(8,128)}, f32[96,1152]{1,0:T(8,128)}, u32[]{:S(2)}, u32[]{:S(2)}) %collective-permute-start.12) | collective-permute-done | bytes 442400 | tf_op jit(solution)/shard_map/ppermute | solution.py:84
  158.5 10.5 %collective-permute-done.11 = f32[96,1152]{1,0:T(8,128)} collective-permute-done((f32[96,1152]{1,0:T(8,128)}, f32[96,1152]{1,0:T(8,128)}, u32[]{:S(2)}, u32[]{:S(2)}) %collective-permute-start.11) | collective-permute-done | bytes 442400 | tf_op jit(solution)/shard_map/ppermute | solution.py:84
  168.9 1.5 fusion.19
  171.1 5.5 %collective-permute-start.15 = (f32[32,1152]{1,0:T(8,128)}, f32[32,1152]{1,0:T(8,128)S(1)}, u32[]{:S(2)}, u32[]{:S(2)}) collective-permute-start(f32[32,1152]{1,0:T(8,128)} %get-tuple-element.14), channel_id=1, source_target_pairs={{0,128},{64,0},{128,64},{1,129},{65,1},{129,65},{2,130},{66,2},{13... | collective-permute-start | bytes 442376 | tf_op jit(solution)/shard_map/ppermute | solution.py:84
  176.6 3.7 %collective-permute-start.14 = (f32[32,1152]{1,0:T(8,128)S(1)}, f32[32,1152]{1,0:T(8,128)}, u32[]{:S(2)}, u32[]{:S(2)}) collective-permute-start(f32[32,1152]{1,0:T(8,128)S(1)} %get-tuple-element.13), channel_id=1, source_target_pairs={{0,64},{64,128},{128,0},{1,65},{65,129},{129,1},{2,66},{66,130},{1... | collective-permute-start | bytes 442376 | tf_op jit(solution)/shard_map/ppermute | solution.py:84
  181.1 10.1 %all-to-all-start.1 = ((f32[32,1,32]{2,1,0:T(1,128)}), f32[32,1,32]{2,1,0:T(1,128)S(1)}, u32[]{:S(2)}, u32[]{:S(2)}) async-start(f32[32,1,32]{2,1,0:T(1,128)} %bitcast.8), calls=%async_computation.1 | async-start | bytes 32768 | tf_op jit(solution)/shard_map/all_to_all | solution.py:219
  191.2 9.0 %all-to-all-done.1 = f32[32,1,32]{2,1,0:T(1,128)S(1)} async-done(((f32[32,1,32]{2,1,0:T(1,128)}), f32[32,1,32]{2,1,0:T(1,128)S(1)}, u32[]{:S(2)}, u32[]{:S(2)}) %all-to-all-start.1) | async-done | bytes 4128 | tf_op jit(solution)/shard_map/all_to_all | solution.py:219
  200.7 1.1 fusion.29
  (67 shorter events, 12.7 us)
Async XLA Ops:
  7.2 20.2 %copy-start = (bf16[1152,1152]{1,0:T(8,128)(2,1)S(1)}, bf16[1152,1152]{1,0:T(8,128)(2,1)}, u32[]{:S(2)}) copy-start(bf16[1152,1152]{1,0:T(8,128)(2,1)} %param.13) | copy-start | bytes 7962628
  7.2 98.3 %all-gather.2.cloned.1.call-start = ((), (), s32[]{:S(2)}) async-start(), calls=%async_computation.2 | async-start | bytes 1843200 | tf_op jit(solution)/shard_map/all_gather | solution.py:142
  10.0 40.5 %collective-permute-start = (bf16[32,1152]{1,0:T(8,128)(2,1)S(1)}, bf16[32,1152]{1,0:T(8,128)(2,1)S(1)}, u32[]{:S(2)}, u32[]{:S(2)}) collective-permute-start(bf16[32,1152]{1,0:T(8,128)(2,1)S(1)} %get-tuple-element.9), channel_id=1, source_target_pairs={{0,3},{1,0},{2,1},{3,2},{4,7},{5,4},{6,5},{7,6},{8,11},{9,8},{10,9... | collective-permute-start | bytes 221192 | tf_op jit(solution)/shard_map/ppermute | solution.py:84
  18.4 28.7 %collective-permute-start.1 = (bf16[32,1152]{1,0:T(8,128)(2,1)S(1)}, bf16[32,1152]{1,0:T(8,128)(2,1)S(1)}, u32[]{:S(2)}, u32[]{:S(2)}) collective-permute-start(bf16[32,1152]{1,0:T(8,128)(2,1)S(1)} %get-tuple-element.9), channel_id=1, source_target_pairs={{0,1},{1,2},{2,3},{3,0},{4,5},{5,6},{6,7},{7,4},{8,9},{9,10},{10,1... | collective-permute-start | bytes 221192 | tf_op jit(solution)/shard_map/ppermute | solution.py:84
  35.9 40.4 %all-to-all-start = ((bf16[32,2,576]{2,1,0:T(2,128)(2,1)}), bf16[32,2,576]{2,1,0:T(2,128)(2,1)S(1)}, u32[]{:S(2)}, u32[]{:S(2)}) async-start(bf16[32,2,576]{2,1,0:T(2,128)(2,1)} %reshape.172), calls=%async_computation | async-start | bytes 163840 | tf_op jit(solution)/shard_map/all_to_all | solution.py:164
  47.1 7.7 %collective-permute-start.2 = (bf16[32,1152]{1,0:T(8,128)(2,1)S(1)}, bf16[32,1152]{1,0:T(8,128)(2,1)S(1)}, u32[]{:S(2)}, u32[]{:S(2)}) collective-permute-start(bf16[32,1152]{1,0:T(8,128)(2,1)S(1)} %collective-permute-done.1), channel_id=1, source_target_pairs={{0,1},{1,2},{2,3},{3,0},{4,5},{5,6},{6,7},{7,4},{8,9},{9,10},{10,1... | collective-permute-start | bytes 221192 | tf_op jit(solution)/shard_map/ppermute | solution.py:84
  55.5 9.5 %collective-permute-start.6 = (bf16[128,1152]{1,0:T(8,128)(2,1)}, bf16[128,1152]{1,0:T(8,128)(2,1)S(1)}, u32[]{:S(2)}, u32[]{:S(2)}) collective-permute-start(bf16[128,1152]{1,0:T(8,128)(2,1)} %pad_maximum_fusion), channel_id=1, source_target_pairs={{0,4},{4,8},{8,12},{12,16},{16,20},{20,24},{24,28},{28,0},{1,5},{5... | collective-permute-start | bytes 884744 | tf_op jit(solution)/shard_map/ppermute | solution.py:84
  60.2 7.8 %collective-permute-start.3 = (bf16[128,1152]{1,0:T(8,128)(2,1)}, bf16[128,1152]{1,0:T(8,128)(2,1)}, u32[]{:S(2)}, u32[]{:S(2)}) collective-permute-start(bf16[128,1152]{1,0:T(8,128)(2,1)} %pad_maximum_fusion), channel_id=1, source_target_pairs={{0,28},{4,0},{8,4},{12,8},{16,12},{20,16},{24,20},{28,24},{1,29},{... | collective-permute-start | bytes 884744 | tf_op jit(solution)/shard_map/ppermute | solution.py:84
  65.0 8.8 %collective-permute-start.7 = (bf16[128,1152]{1,0:T(8,128)(2,1)S(1)}, bf16[128,1152]{1,0:T(8,128)(2,1)}, u32[]{:S(2)}, u32[]{:S(2)}) collective-permute-start(bf16[128,1152]{1,0:T(8,128)(2,1)S(1)} %collective-permute-done.6), channel_id=1, source_target_pairs={{0,4},{4,8},{8,12},{12,16},{16,20},{20,24},{24,28},{28,0},{1,5},{5... | collective-permute-start | bytes 884744 | tf_op jit(solution)/shard_map/ppermute | solution.py:84
  68.0 8.9 %collective-permute-start.4 = (bf16[128,1152]{1,0:T(8,128)(2,1)}, bf16[128,1152]{1,0:T(8,128)(2,1)}, u32[]{:S(2)}, u32[]{:S(2)}) collective-permute-start(bf16[128,1152]{1,0:T(8,128)(2,1)} %collective-permute-done.3), channel_id=1, source_target_pairs={{0,28},{4,0},{8,4},{12,8},{16,12},{20,16},{24,20},{28,24},{1,29},{... | collective-permute-start | bytes 884744 | tf_op jit(solution)/shard_map/ppermute | solution.py:84
  73.8 9.8 %collective-permute-start.8 = (bf16[128,1152]{1,0:T(8,128)(2,1)}, bf16[128,1152]{1,0:T(8,128)(2,1)}, u32[]{:S(2)}, u32[]{:S(2)}) collective-permute-start(bf16[128,1152]{1,0:T(8,128)(2,1)} %collective-permute-done.7), channel_id=1, source_target_pairs={{0,4},{4,8},{8,12},{12,16},{16,20},{20,24},{24,28},{28,0},{1,5},{5... | collective-permute-start | bytes 884744 | tf_op jit(solution)/shard_map/ppermute | solution.py:84
  76.9 32.6 %collective-permute-start.5 = (bf16[128,1152]{1,0:T(8,128)(2,1)}, bf16[128,1152]{1,0:T(8,128)(2,1)S(1)}, u32[]{:S(2)}, u32[]{:S(2)}) collective-permute-start(bf16[128,1152]{1,0:T(8,128)(2,1)} %collective-permute-done.4), channel_id=1, source_target_pairs={{0,28},{4,0},{8,4},{12,8},{16,12},{20,16},{24,20},{28,24},{1,29},{... | collective-permute-start | bytes 884744 | tf_op jit(solution)/shard_map/ppermute | solution.py:84
  105.5 11.7 %collective-permute-start.9 = (bf16[128,1152]{1,0:T(8,128)(2,1)}, bf16[128,1152]{1,0:T(8,128)(2,1)S(1)}, u32[]{:S(2)}, u32[]{:S(2)}) collective-permute-start(bf16[128,1152]{1,0:T(8,128)(2,1)} %collective-permute-done.8), channel_id=1, source_target_pairs={{0,4},{4,8},{8,12},{12,16},{16,20},{20,24},{24,28},{28,0},{1,5},{5... | collective-permute-start | bytes 884744 | tf_op jit(solution)/shard_map/ppermute | solution.py:84
  110.2 6.9 %copy-start.5 = (bf16[1056,1152]{1,0:T(8,128)(2,1)S(1)}, bf16[1056,1152]{1,0:T(8,128)(2,1)}, u32[]{:S(2)}) copy-start(bf16[1056,1152]{1,0:T(8,128)(2,1)} %constant_dynamic-update-slice_fusion.4) | copy-start | bytes 7299076
  126.1 1.8 copy-start.2
  129.2 6.6 %collective-permute-start.10 = (f32[384,1152]{1,0:T(8,128)}, f32[384,1152]{1,0:T(8,128)}, u32[]{:S(2)}, u32[]{:S(2)}) collective-permute-start(f32[384,1152]{1,0:T(8,128)} %dynamic-slice_bitcast_fusion), channel_id=1, source_target_pairs={{0,32},{32,0},{1,33},{33,1},{2,34},{34,2},{3,35},{35,3},{4,36},{36... | collective-permute-start | bytes 5308424 | tf_op jit(solution)/shard_map/ppermute | solution.py:84
  138.0 1.2 copy-start.1
  139.2 61.6 %copy-start.3 = (bf16[32,1152]{1,0:T(8,128)(2,1)S(1)}, bf16[32,1152]{1,0:T(8,128)(2,1)}, u32[]{:S(2)}) copy-start(bf16[32,1152]{1,0:T(8,128)(2,1)} %param.16) | copy-start | bytes 221188
  140.3 13.6 %collective-permute-start.13 = (f32[96,1152]{1,0:T(8,128)}, f32[96,1152]{1,0:T(8,128)S(1)}, u32[]{:S(2)}, u32[]{:S(2)}) collective-permute-start(f32[96,1152]{1,0:T(8,128)} %get-tuple-element.11), channel_id=1, source_target_pairs={{0,576},{192,0},{384,192},{576,384},{1,577},{193,1},{385,193},{577... | collective-permute-start | bytes 1327112 | tf_op jit(solution)/shard_map/ppermute | solution.py:84
  143.7 14.8 %collective-permute-start.12 = (f32[96,1152]{1,0:T(8,128)}, f32[96,1152]{1,0:T(8,128)}, u32[]{:S(2)}, u32[]{:S(2)}) collective-permute-start(f32[96,1152]{1,0:T(8,128)} %get-tuple-element.12), channel_id=1, source_target_pairs={{0,384},{192,576},{384,0},{576,192},{1,385},{193,577},{385,1},{577... | collective-permute-start | bytes 1327112 | tf_op jit(solution)/shard_map/ppermute | solution.py:84
  146.1 22.8 %collective-permute-start.11 = (f32[96,1152]{1,0:T(8,128)}, f32[96,1152]{1,0:T(8,128)}, u32[]{:S(2)}, u32[]{:S(2)}) collective-permute-start(f32[96,1152]{1,0:T(8,128)} %get-tuple-element.10), channel_id=1, source_target_pairs={{0,192},{192,384},{384,576},{576,0},{1,193},{193,385},{385,577},{5... | collective-permute-start | bytes 1327112 | tf_op jit(solution)/shard_map/ppermute | solution.py:84
  153.9 4.6 %copy-start.4 = (f32[96,1152]{1,0:T(8,128)}, f32[96,1152]{1,0:T(8,128)S(1)}, u32[]{:S(2)}) copy-start(f32[96,1152]{1,0:T(8,128)S(1)} %collective-permute-done.13) | copy-start | bytes 1327108
  171.1 29.6 %collective-permute-start.15 = (f32[32,1152]{1,0:T(8,128)}, f32[32,1152]{1,0:T(8,128)S(1)}, u32[]{:S(2)}, u32[]{:S(2)}) collective-permute-start(f32[32,1152]{1,0:T(8,128)} %get-tuple-element.14), channel_id=1, source_target_pairs={{0,128},{64,0},{128,64},{1,129},{65,1},{129,65},{2,130},{66,2},{13... | collective-permute-start | bytes 442376 | tf_op jit(solution)/shard_map/ppermute | solution.py:84
  176.6 24.1 %collective-permute-start.14 = (f32[32,1152]{1,0:T(8,128)S(1)}, f32[32,1152]{1,0:T(8,128)}, u32[]{:S(2)}, u32[]{:S(2)}) collective-permute-start(f32[32,1152]{1,0:T(8,128)S(1)} %get-tuple-element.13), channel_id=1, source_target_pairs={{0,64},{64,128},{128,0},{1,65},{65,129},{129,1},{2,66},{66,130},{1... | collective-permute-start | bytes 442376 | tf_op jit(solution)/shard_map/ppermute | solution.py:84
  181.1 19.0 %all-to-all-start.1 = ((f32[32,1,32]{2,1,0:T(1,128)}), f32[32,1,32]{2,1,0:T(1,128)S(1)}, u32[]{:S(2)}, u32[]{:S(2)}) async-start(f32[32,1,32]{2,1,0:T(1,128)} %bitcast.8), calls=%async_computation.1 | async-start | bytes 32768 | tf_op jit(solution)/shard_map/all_to_all | solution.py:219
Sparse Core Ops, SparseCore 0:
  23.1 82.2 all-gather.1

commit v4 on v3

--- a/solution.py
+++ b/solution.py
@@ -215,13 +215,14 @@
         [pooled_losses[:, None], prior_losses.reshape(inner_size, chunk_rows)[:, :prior_count]],
         axis=1,
     )
+    core_terms = direct_scatter(grad_terms, "core", core_size)
+    loss_parts, core_terms = lax.optimization_barrier((loss_parts, core_terms))
     own_losses = jnp.sum(
         lax.all_to_all(loss_parts, ("section", "mp"), 0, 0, tiled=True), axis=0
     )
-
-    own_terms = direct_scatter(
-        direct_scatter(direct_scatter(grad_terms, "core", core_size), "x", x_size), "zh", zh_size
-    )
+    x_terms = direct_scatter(core_terms, "x", x_size)
+    own_losses, x_terms = lax.optimization_barrier((own_losses, x_terms))
+    own_terms = direct_scatter(x_terms, "zh", zh_size)
     along = jnp.sum(text_unit * own_terms, axis=1, keepdims=True)
     text_grad = (own_terms - text_unit * along) * text_inverse
     return (own_losses, text_grad)

time: 211 us -> 204 us (0.967)
  waiting for transfers between devices: 66.4 us -> 60.1 us
    ppermute x16, waiting for transfers between devices: 35.5 us -> 30 us  [shift_ring(): return lax.ppermute(x, axis, [(i, (i + step) % size) for i in range(size)])]
  transfers between devices with their start and end apart: 19 -> 19, of which waited for: 12 -> 11; matrix products, arithmetic and copies ran while one was open for 13% -> 13% of each run, Pallas kernels for 0% -> 0%
where the time goes in v4:
time: 204 us; the launch traced here: 203 us
  starting transfers between devices  75.7 us (37%)
  waiting for transfers between devices  60.1 us (29%)
  local copies, waits for them, and re-layouts  19.9 us (10%)
  between operations  16.6 us (8%)
  matrix products  15.4 us (8%)
  other arithmetic  15.2 us (7%)
    ppermute x16, starting transfers between devices, shift_ring(): return lax.ppermute(x, axis, [(i, (i + step) % size) for i in range(size)])  57.2 us
    ppermute x16, waiting for transfers between devices, shift_ring(): return lax.ppermute(x, axis, [(i, (i + step) % size) for i in range(size)])  30 us
    all_gather x1, waiting for transfers between devices, local(): lax.all_gather(caption_magnitude, ('x', 'zh', 'core'), axis=0, tiled=True)  21.3 us
    unnamed x24, local copies, waits for them, and re-layouts  12.7 us
    all_to_all x1, starting transfers between devices, local(): lax.all_to_all(loss_parts, ('section', 'mp'), 0, 0, tiled=True)  10.1 us
    all_to_all x1, waiting for transfers between devices, local(): lax.all_to_all(loss_parts, ('section', 'mp'), 0, 0, tiled=True)  8.86 us
    all_to_all x1, starting transfers between devices, local(): lax.all_to_all(jnp.broadcast_to(pooled_norm, (inner_size, pooled_norm.sha...  8.38 us
    dot_general x1, matrix products, pool_image(): scores = jnp.dot(patch_rows, key_probe, preferred_element_type=jnp.float32)  4.15 us
  transfers between devices with their start and end apart: 19, of which 11 were waited for; matrix products, arithmetic and copies ran while one was open for 13% of the time, Pallas kernels for 0%

profile of v4, /device:TPU:1, one launch (start us, length us, event | category | flops | bytes accessed | tf_op | source)
XLA Modules:
  0.0 202.9 jit_solution(9084287959298284421)
XLA Ops:
  7.2 1.2 fusion.27
  8.4 1.6 constant_dynamic-update-slice_fusion.10
  10.0 4.8 %collective-permute-start.1 = (bf16[32,1152]{1,0:T(8,128)(2,1)S(1)}, bf16[32,1152]{1,0:T(8,128)(2,1)S(1)}, u32[]{:S(2)}, u32[]{:S(2)}) collective-permute-start(bf16[32,1152]{1,0:T(8,128)(2,1)S(1)} %get-tuple-element.17), channel_id=1, source_target_pairs={{0,1},{1,2},{2,3},{3,0},{4,5},{5,6},{6,7},{7,4},{8,9},{9,10},{10,1... | collective-permute-start | bytes 221192 | tf_op jit(solution)/shard_map/ppermute | solution.py:84
  14.8 5.5 %collective-permute-start = (bf16[32,1152]{1,0:T(8,128)(2,1)S(1)}, bf16[32,1152]{1,0:T(8,128)(2,1)S(1)}, u32[]{:S(2)}, u32[]{:S(2)}) collective-permute-start(bf16[32,1152]{1,0:T(8,128)(2,1)S(1)} %get-tuple-element.17), channel_id=1, source_target_pairs={{0,3},{1,0},{2,1},{3,2},{4,7},{5,4},{6,5},{7,6},{8,11},{9,8},{10,9... | collective-permute-start | bytes 221192 | tf_op jit(solution)/shard_map/ppermute | solution.py:84
  20.4 1.0 fusion.32
  21.4 1.6 fusion.26
  23.0 4.1 %fusion.68 = (f32[16]{0:T(128)S(1)}, f32[16,729]{1,0:T(8,128)S(1)}) fusion(bf16[1,729,1152]{2,1,0:T(8,128)(2,1)} %param.10, bf16[1152,1152]{1,0:T(8,128)(2,1)} %param.12, s32[1152]{0:T(1024)S(1)} %add_select_fusion, bf16[1152]{0:T(1024)(128)(2,1)} %param.11), kind=kOutput, calls=%fused_computation.126 | convolution fusion | flops 69426560 | bytes 4387456 | tf_op jit(solution)/shard_map/dot_general | solution.py:24
  27.4 2.2 %fusion.15 = f32[16,1152]{1,0:T(8,128)S(1)} fusion(bf16[1152,1152]{1,0:T(8,128)(2,1)S(1)} %copy-done, bf16[1,729,1152]{2,1,0:T(8,128)(2,1)} %param.10, f32[16,729]{1,0:T(8,128)S(1)} %get-tuple-element.24, f32[16]{0:T(128)S(1)} %fusion.38, f32[16]{0:T(128)S(1)} %get-tuple-element.23), kind=kOutput, calls=%fused_computation.22 | convolution fusion | flops 69394608 | bytes 4454336 | tf_op jit(solution)/shard_map/dot_general | solution.py:31
  30.0 2.2 %convolution_reduce_fusion = bf16[1152]{0:T(1024)(128)(2,1)S(1)} fusion(bf16[1152,1]{0,1:T(2,128)(2,1)S(1)} %reshape.167, bf16[1152,1152]{1,0:T(8,128)(2,1)} %param.14), kind=kOutput, calls=%fused_computation.23 | convolution fusion | flops 2654208 | bytes 2658816 | tf_op jit(solution)/shard_map/dot_general | solution.py:38
  34.1 1.1 reduce.9
  35.9 8.4 %all-to-all-start = ((bf16[32,2,576]{2,1,0:T(2,128)(2,1)}), bf16[32,2,576]{2,1,0:T(2,128)(2,1)S(1)}, u32[]{:S(2)}, u32[]{:S(2)}) async-start(bf16[32,2,576]{2,1,0:T(2,128)(2,1)} %reshape.172), calls=%async_computation | async-start | bytes 163840 | tf_op jit(solution)/shard_map/all_to_all | solution.py:164
  45.7 3.1 %collective-permute-start.2 = (bf16[32,1152]{1,0:T(8,128)(2,1)S(1)}, bf16[32,1152]{1,0:T(8,128)(2,1)S(1)}, u32[]{:S(2)}, u32[]{:S(2)}) collective-permute-start(bf16[32,1152]{1,0:T(8,128)(2,1)S(1)} %collective-permute-done.1), channel_id=1, source_target_pairs={{0,1},{1,2},{2,3},{3,0},{4,5},{5,6},{6,7},{7,4},{8,9},{9,10},{10,1... | collective-permute-start | bytes 221192 | tf_op jit(solution)/shard_map/ppermute | solution.py:84
  48.9 5.4 %collective-permute-done.2 = bf16[32,1152]{1,0:T(8,128)(2,1)S(1)} collective-permute-done((bf16[32,1152]{1,0:T(8,128)(2,1)S(1)}, bf16[32,1152]{1,0:T(8,128)(2,1)S(1)}, u32[]{:S(2)}, u32[]{:S(2)}) %collective-permute-start.2) | collective-permute-done | bytes 73760 | tf_op jit(solution)/shard_map/ppermute | solution.py:84
  55.0 3.1 %collective-permute-start.6 = (bf16[128,1152]{1,0:T(8,128)(2,1)}, bf16[128,1152]{1,0:T(8,128)(2,1)S(1)}, u32[]{:S(2)}, u32[]{:S(2)}) collective-permute-start(bf16[128,1152]{1,0:T(8,128)(2,1)} %pad_maximum_fusion), channel_id=1, source_target_pairs={{0,4},{4,8},{8,12},{12,16},{16,20},{20,24},{24,28},{28,0},{1,5},{5... | collective-permute-start | bytes 884744 | tf_op jit(solution)/shard_map/ppermute | solution.py:84
  59.6 3.4 %collective-permute-start.3 = (bf16[128,1152]{1,0:T(8,128)(2,1)}, bf16[128,1152]{1,0:T(8,128)(2,1)}, u32[]{:S(2)}, u32[]{:S(2)}) collective-permute-start(bf16[128,1152]{1,0:T(8,128)(2,1)} %pad_maximum_fusion), channel_id=1, source_target_pairs={{0,28},{4,0},{8,4},{12,8},{16,12},{20,16},{24,20},{28,24},{1,29},{... | collective-permute-start | bytes 884744 | tf_op jit(solution)/shard_map/ppermute | solution.py:84
  63.9 1.9 collective-permute-start.7
  66.5 1.1 collective-permute-done.3
  67.5 4.4 %collective-permute-start.4 = (bf16[128,1152]{1,0:T(8,128)(2,1)}, bf16[128,1152]{1,0:T(8,128)(2,1)}, u32[]{:S(2)}, u32[]{:S(2)}) collective-permute-start(bf16[128,1152]{1,0:T(8,128)(2,1)} %collective-permute-done.3), channel_id=1, source_target_pairs={{0,28},{4,0},{8,4},{12,8},{16,12},{20,16},{24,20},{28,24},{1,29},{... | collective-permute-start | bytes 884744 | tf_op jit(solution)/shard_map/ppermute | solution.py:84
  72.7 1.9 collective-permute-start.8
  75.9 5.0 %collective-permute-start.5 = (bf16[128,1152]{1,0:T(8,128)(2,1)}, bf16[128,1152]{1,0:T(8,128)(2,1)S(1)}, u32[]{:S(2)}, u32[]{:S(2)}) collective-permute-start(bf16[128,1152]{1,0:T(8,128)(2,1)} %collective-permute-done.4), channel_id=1, source_target_pairs={{0,28},{4,0},{8,4},{12,8},{16,12},{20,16},{24,20},{28,24},{1,29},{... | collective-permute-start | bytes 884744 | tf_op jit(solution)/shard_map/ppermute | solution.py:84
  81.0 1.7 constant_dynamic-update-slice_fusion.6
  82.6 21.3 %all-gather.2.cloned.1.call-done = bf16[768,1152]{1,0:T(8,128)(2,1)} async-done(((bf16[32,1152]{1,0:T(8,128)(2,1)}), bf16[768,1152]{1,0:T(8,128)(2,1)}) %all-gather.2.cloned.1.call-update) | async-done | bytes 1769488 | tf_op jit(solution)/shard_map/all_gather | solution.py:142
  103.9 2.3 %collective-permute-start.9 = (bf16[128,1152]{1,0:T(8,128)(2,1)}, bf16[128,1152]{1,0:T(8,128)(2,1)S(1)}, u32[]{:S(2)}, u32[]{:S(2)}) collective-permute-start(bf16[128,1152]{1,0:T(8,128)(2,1)} %collective-permute-done.8), channel_id=1, source_target_pairs={{0,4},{4,8},{8,12},{12,16},{16,20},{20,24},{24,28},{28,0},{1,5},{5... | collective-permute-start | bytes 884744 | tf_op jit(solution)/shard_map/ppermute | solution.py:84
  106.2 1.7 constant_dynamic-update-slice_fusion.5
  108.7 1.8 copy.18
  110.4 5.2 %collective-permute-done.9 = bf16[128,1152]{1,0:T(8,128)(2,1)S(1)} collective-permute-done((bf16[128,1152]{1,0:T(8,128)(2,1)}, bf16[128,1152]{1,0:T(8,128)(2,1)S(1)}, u32[]{:S(2)}, u32[]{:S(2)}) %collective-permute-start.9) | collective-permute-done | bytes 294944 | tf_op jit(solution)/shard_map/ppermute | solution.py:84
  115.7 1.0 constant_dynamic-update-slice_fusion.2
  116.7 1.0 constant_dynamic-update-slice_fusion.1
  117.7 3.8 %fusion.6 = (f32[1056]{0:T(1024)S(1)}, f32[1056,768]{1,0:T(8,128)S(1)}) fusion(s32[768]{0:T(1024)S(1)} %add.265, s32[1056]{0:T(1024)S(1)} %pad_add_fusion, f32[]{:T(128)} %bitcast.59, bf16[1056,1152]{1,0:T(8,128)(2,1)S(1)} %bitcast_dynamic-update-slice_fusion, bf16[768,1152]{1,0:T(8,128)(2,1)S(1)} %bitcast.65, f32[]{:T(128)} %bitcast.57), kind=kOutput, calls=%fused_computation.11 | convolution fusion | flops 1878293504 | bytes 7458056 | tf_op jit(solution)/shard_map/dot_general | solution.py:59
  121.6 3.0 %fusion.11 = f32[768,1152]{1,0:T(8,128)S(1)} fusion(bf16[1056,1152]{1,0:T(8,128)(2,1)S(1)} %bitcast_dynamic-update-slice_fusion, f32[1056,768]{1,0:T(8,128)S(1)} %get-tuple-element.26, f32[]{:T(128)} %bitcast.58, s32[768]{0:T(1024)S(1)} %add.265, s32[1056]{0:T(1024)S(1)} %pad_add_fusion), kind=kOutput, calls=%fused_computation.20 | convolution fusion | flops 1875050496 | bytes 9223300 | tf_op jit(solution)/shard_map/dot_general | solution.py:74
  124.6 1.7 copy-done.2
  126.3 1.4 dynamic-slice_bitcast_fusion
  127.7 3.0 %collective-permute-start.10 = (f32[384,1152]{1,0:T(8,128)}, f32[384,1152]{1,0:T(8,128)}, u32[]{:S(2)}, u32[]{:S(2)}) collective-permute-start(f32[384,1152]{1,0:T(8,128)} %dynamic-slice_bitcast_fusion), channel_id=1, source_target_pairs={{0,32},{32,0},{1,33},{33,1},{2,34},{34,2},{3,35},{35,3},{4,36},{36... | collective-permute-start | bytes 5308424 | tf_op jit(solution)/shard_map/ppermute | solution.py:84
  131.6 2.6 %collective-permute-done.10 = f32[384,1152]{1,0:T(8,128)} collective-permute-done((f32[384,1152]{1,0:T(8,128)}, f32[384,1152]{1,0:T(8,128)}, u32[]{:S(2)}, u32[]{:S(2)}) %collective-permute-start.10) | collective-permute-done | bytes 1769504 | tf_op jit(solution)/shard_map/ppermute | solution.py:84
  134.3 2.2 %bitcast_add_fusion = f32[384,1152]{1,0:T(8,128)S(1)} fusion(f32[384,1152]{1,0:T(8,128)} %collective-permute-done.10, f32[2,384,1152]{2,1,0:T(8,128)} %bitcast.63, s32[]{:T(128)S(6)} %select_n.174), kind=kLoop, calls=%fused_computation.15 | loop fusion | flops 442368 | bytes 5308420 | tf_op jit(solution)/shard_map/add | solution.py:110
  136.5 1.2 copy-done.1
  137.7 1.1 dynamic-slice_bitcast_fusion.3
  138.8 2.1 %collective-permute-start.11 = (f32[96,1152]{1,0:T(8,128)}, f32[96,1152]{1,0:T(8,128)S(1)}, u32[]{:S(2)}, u32[]{:S(2)}) collective-permute-start(f32[96,1152]{1,0:T(8,128)} %get-tuple-element.18), channel_id=1, source_target_pairs={{0,192},{192,384},{384,576},{576,0},{1,193},{193,385},{385,577},{5... | collective-permute-start | bytes 1327112 | tf_op jit(solution)/shard_map/ppermute | solution.py:84
  140.9 4.3 %collective-permute-start.12 = (f32[96,1152]{1,0:T(8,128)}, f32[96,1152]{1,0:T(8,128)}, u32[]{:S(2)}, u32[]{:S(2)}) collective-permute-start(f32[96,1152]{1,0:T(8,128)} %get-tuple-element.20), channel_id=1, source_target_pairs={{0,384},{192,576},{384,0},{576,192},{1,385},{193,577},{385,1},{577... | collective-permute-start | bytes 1327112 | tf_op jit(solution)/shard_map/ppermute | solution.py:84
  145.3 3.1 %collective-permute-start.13 = (f32[96,1152]{1,0:T(8,128)}, f32[96,1152]{1,0:T(8,128)}, u32[]{:S(2)}, u32[]{:S(2)}) collective-permute-start(f32[96,1152]{1,0:T(8,128)} %get-tuple-element.19), channel_id=1, source_target_pairs={{0,576},{192,0},{384,192},{576,384},{1,577},{193,1},{385,193},{577... | collective-permute-start | bytes 1327112 | tf_op jit(solution)/shard_map/ppermute | solution.py:84
  148.4 10.1 %all-to-all-start.1 = ((f32[32,1,32]{2,1,0:T(1,128)}), f32[32,1,32]{2,1,0:T(1,128)S(1)}, u32[]{:S(2)}, u32[]{:S(2)}) async-start(f32[32,1,32]{2,1,0:T(1,128)} %bitcast.11), calls=%async_computation.1 | async-start | bytes 32768 | tf_op jit(solution)/shard_map/all_to_all | solution.py:221
  158.5 8.9 %all-to-all-done.1 = f32[32,1,32]{2,1,0:T(1,128)S(1)} async-done(((f32[32,1,32]{2,1,0:T(1,128)}), f32[32,1,32]{2,1,0:T(1,128)S(1)}, u32[]{:S(2)}, u32[]{:S(2)}) %all-to-all-start.1) | async-done | bytes 4128 | tf_op jit(solution)/shard_map/all_to_all | solution.py:221
  168.7 1.5 fusion.19
  170.8 2.3 %collective-permute-start.14 = (f32[32,1152]{1,0:T(8,128)}, f32[32,1152]{1,0:T(8,128)S(1)}, u32[]{:S(2)}, u32[]{:S(2)}) collective-permute-start(f32[32,1152]{1,0:T(8,128)} %get-tuple-element.21), channel_id=1, source_target_pairs={{0,64},{64,128},{128,0},{1,65},{65,129},{129,1},{2,66},{66,130},{1... | collective-permute-start | bytes 442376 | tf_op jit(solution)/shard_map/ppermute | solution.py:84
  173.1 6.9 %collective-permute-start.15 = (f32[32,1152]{1,0:T(8,128)S(1)}, f32[32,1152]{1,0:T(8,128)}, u32[]{:S(2)}, u32[]{:S(2)}) collective-permute-start(f32[32,1152]{1,0:T(8,128)S(1)} %get-tuple-element.22), channel_id=1, source_target_pairs={{0,128},{64,0},{128,64},{1,129},{65,1},{129,65},{2,130},{66,2},{13... | collective-permute-start | bytes 442376 | tf_op jit(solution)/shard_map/ppermute | solution.py:84
  180.0 8.8 %collective-permute-done.14 = f32[32,1152]{1,0:T(8,128)S(1)} collective-permute-done((f32[32,1152]{1,0:T(8,128)}, f32[32,1152]{1,0:T(8,128)S(1)}, u32[]{:S(2)}, u32[]{:S(2)}) %collective-permute-start.14) | collective-permute-done | bytes 147488 | tf_op jit(solution)/shard_map/ppermute | solution.py:84
  188.8 5.4 %collective-permute-done.15 = f32[32,1152]{1,0:T(8,128)} collective-permute-done((f32[32,1152]{1,0:T(8,128)S(1)}, f32[32,1152]{1,0:T(8,128)}, u32[]{:S(2)}, u32[]{:S(2)}) %collective-permute-start.15) | collective-permute-done | bytes 147488 | tf_op jit(solution)/shard_map/ppermute | solution.py:84
  194.2 1.1 fusion.29
  (67 shorter events, 13.0 us)
Async XLA Ops:
  7.2 20.2 %copy-start = (bf16[1152,1152]{1,0:T(8,128)(2,1)S(1)}, bf16[1152,1152]{1,0:T(8,128)(2,1)}, u32[]{:S(2)}) copy-start(bf16[1152,1152]{1,0:T(8,128)(2,1)} %param.13) | copy-start | bytes 7962628
  7.2 96.8 %all-gather.2.cloned.1.call-start = ((), (), s32[]{:S(2)}) async-start(), calls=%async_computation.2 | async-start | bytes 1843200 | tf_op jit(solution)/shard_map/all_gather | solution.py:142
  10.0 35.7 %collective-permute-start.1 = (bf16[32,1152]{1,0:T(8,128)(2,1)S(1)}, bf16[32,1152]{1,0:T(8,128)(2,1)S(1)}, u32[]{:S(2)}, u32[]{:S(2)}) collective-permute-start(bf16[32,1152]{1,0:T(8,128)(2,1)S(1)} %get-tuple-element.17), channel_id=1, source_target_pairs={{0,1},{1,2},{2,3},{3,0},{4,5},{5,6},{6,7},{7,4},{8,9},{9,10},{10,1... | collective-permute-start | bytes 221192 | tf_op jit(solution)/shard_map/ppermute | solution.py:84
  14.8 34.1 %collective-permute-start = (bf16[32,1152]{1,0:T(8,128)(2,1)S(1)}, bf16[32,1152]{1,0:T(8,128)(2,1)S(1)}, u32[]{:S(2)}, u32[]{:S(2)}) collective-permute-start(bf16[32,1152]{1,0:T(8,128)(2,1)S(1)} %get-tuple-element.17), channel_id=1, source_target_pairs={{0,3},{1,0},{2,1},{3,2},{4,7},{5,4},{6,5},{7,6},{8,11},{9,8},{10,9... | collective-permute-start | bytes 221192 | tf_op jit(solution)/shard_map/ppermute | solution.py:84
  35.9 39.3 %all-to-all-start = ((bf16[32,2,576]{2,1,0:T(2,128)(2,1)}), bf16[32,2,576]{2,1,0:T(2,128)(2,1)S(1)}, u32[]{:S(2)}, u32[]{:S(2)}) async-start(bf16[32,2,576]{2,1,0:T(2,128)(2,1)} %reshape.172), calls=%async_computation | async-start | bytes 163840 | tf_op jit(solution)/shard_map/all_to_all | solution.py:164
  45.7 8.6 %collective-permute-start.2 = (bf16[32,1152]{1,0:T(8,128)(2,1)S(1)}, bf16[32,1152]{1,0:T(8,128)(2,1)S(1)}, u32[]{:S(2)}, u32[]{:S(2)}) collective-permute-start(bf16[32,1152]{1,0:T(8,128)(2,1)S(1)} %collective-permute-done.1), channel_id=1, source_target_pairs={{0,1},{1,2},{2,3},{3,0},{4,5},{5,6},{6,7},{7,4},{8,9},{9,10},{10,1... | collective-permute-start | bytes 221192 | tf_op jit(solution)/shard_map/ppermute | solution.py:84
  55.0 8.9 %collective-permute-start.6 = (bf16[128,1152]{1,0:T(8,128)(2,1)}, bf16[128,1152]{1,0:T(8,128)(2,1)S(1)}, u32[]{:S(2)}, u32[]{:S(2)}) collective-permute-start(bf16[128,1152]{1,0:T(8,128)(2,1)} %pad_maximum_fusion), channel_id=1, source_target_pairs={{0,4},{4,8},{8,12},{12,16},{16,20},{20,24},{24,28},{28,0},{1,5},{5... | collective-permute-start | bytes 884744 | tf_op jit(solution)/shard_map/ppermute | solution.py:84
  59.6 7.9 %collective-permute-start.3 = (bf16[128,1152]{1,0:T(8,128)(2,1)}, bf16[128,1152]{1,0:T(8,128)(2,1)}, u32[]{:S(2)}, u32[]{:S(2)}) collective-permute-start(bf16[128,1152]{1,0:T(8,128)(2,1)} %pad_maximum_fusion), channel_id=1, source_target_pairs={{0,28},{4,0},{8,4},{12,8},{16,12},{20,16},{24,20},{28,24},{1,29},{... | collective-permute-start | bytes 884744 | tf_op jit(solution)/shard_map/ppermute | solution.py:84
  63.9 8.8 %collective-permute-start.7 = (bf16[128,1152]{1,0:T(8,128)(2,1)S(1)}, bf16[128,1152]{1,0:T(8,128)(2,1)}, u32[]{:S(2)}, u32[]{:S(2)}) collective-permute-start(bf16[128,1152]{1,0:T(8,128)(2,1)S(1)} %collective-permute-done.6), channel_id=1, source_target_pairs={{0,4},{4,8},{8,12},{12,16},{16,20},{20,24},{24,28},{28,0},{1,5},{5... | collective-permute-start | bytes 884744 | tf_op jit(solution)/shard_map/ppermute | solution.py:84
  67.5 8.4 %collective-permute-start.4 = (bf16[128,1152]{1,0:T(8,128)(2,1)}, bf16[128,1152]{1,0:T(8,128)(2,1)}, u32[]{:S(2)}, u32[]{:S(2)}) collective-permute-start(bf16[128,1152]{1,0:T(8,128)(2,1)} %collective-permute-done.3), channel_id=1, source_target_pairs={{0,28},{4,0},{8,4},{12,8},{16,12},{20,16},{24,20},{28,24},{1,29},{... | collective-permute-start | bytes 884744 | tf_op jit(solution)/shard_map/ppermute | solution.py:84
  72.7 10.0 %collective-permute-start.8 = (bf16[128,1152]{1,0:T(8,128)(2,1)}, bf16[128,1152]{1,0:T(8,128)(2,1)}, u32[]{:S(2)}, u32[]{:S(2)}) collective-permute-start(bf16[128,1152]{1,0:T(8,128)(2,1)} %collective-permute-done.7), channel_id=1, source_target_pairs={{0,4},{4,8},{8,12},{12,16},{16,20},{20,24},{24,28},{28,0},{1,5},{5... | collective-permute-start | bytes 884744 | tf_op jit(solution)/shard_map/ppermute | solution.py:84
  75.9 32.0 %collective-permute-start.5 = (bf16[128,1152]{1,0:T(8,128)(2,1)}, bf16[128,1152]{1,0:T(8,128)(2,1)S(1)}, u32[]{:S(2)}, u32[]{:S(2)}) collective-permute-start(bf16[128,1152]{1,0:T(8,128)(2,1)} %collective-permute-done.4), channel_id=1, source_target_pairs={{0,28},{4,0},{8,4},{12,8},{16,12},{20,16},{24,20},{28,24},{1,29},{... | collective-permute-start | bytes 884744 | tf_op jit(solution)/shard_map/ppermute | solution.py:84
  103.9 11.7 %collective-permute-start.9 = (bf16[128,1152]{1,0:T(8,128)(2,1)}, bf16[128,1152]{1,0:T(8,128)(2,1)S(1)}, u32[]{:S(2)}, u32[]{:S(2)}) collective-permute-start(bf16[128,1152]{1,0:T(8,128)(2,1)} %collective-permute-done.8), channel_id=1, source_target_pairs={{0,4},{4,8},{8,12},{12,16},{16,20},{20,24},{24,28},{28,0},{1,5},{5... | collective-permute-start | bytes 884744 | tf_op jit(solution)/shard_map/ppermute | solution.py:84
  108.7 7.0 %copy-start.5 = (bf16[1056,1152]{1,0:T(8,128)(2,1)S(1)}, bf16[1056,1152]{1,0:T(8,128)(2,1)}, u32[]{:S(2)}) copy-start(bf16[1056,1152]{1,0:T(8,128)(2,1)} %constant_dynamic-update-slice_fusion.4) | copy-start | bytes 7299076
  124.5 1.8 copy-start.2
  127.7 6.6 %collective-permute-start.10 = (f32[384,1152]{1,0:T(8,128)}, f32[384,1152]{1,0:T(8,128)}, u32[]{:S(2)}, u32[]{:S(2)}) collective-permute-start(f32[384,1152]{1,0:T(8,128)} %dynamic-slice_bitcast_fusion), channel_id=1, source_target_pairs={{0,32},{32,0},{1,33},{33,1},{2,34},{34,2},{3,35},{35,3},{4,36},{36... | collective-permute-start | bytes 5308424 | tf_op jit(solution)/shard_map/ppermute | solution.py:84
  136.5 1.2 copy-start.1
  137.7 56.5 %copy-start.3 = (bf16[32,1152]{1,0:T(8,128)(2,1)S(1)}, bf16[32,1152]{1,0:T(8,128)(2,1)}, u32[]{:S(2)}) copy-start(bf16[32,1152]{1,0:T(8,128)(2,1)} %param.16) | copy-start | bytes 221188
  138.8 29.1 %collective-permute-start.11 = (f32[96,1152]{1,0:T(8,128)}, f32[96,1152]{1,0:T(8,128)S(1)}, u32[]{:S(2)}, u32[]{:S(2)}) collective-permute-start(f32[96,1152]{1,0:T(8,128)} %get-tuple-element.18), channel_id=1, source_target_pairs={{0,192},{192,384},{384,576},{576,0},{1,193},{193,385},{385,577},{5... | collective-permute-start | bytes 1327112 | tf_op jit(solution)/shard_map/ppermute | solution.py:84
  140.9 27.0 %collective-permute-start.12 = (f32[96,1152]{1,0:T(8,128)}, f32[96,1152]{1,0:T(8,128)}, u32[]{:S(2)}, u32[]{:S(2)}) collective-permute-start(f32[96,1152]{1,0:T(8,128)} %get-tuple-element.20), channel_id=1, source_target_pairs={{0,384},{192,576},{384,0},{576,192},{1,385},{193,577},{385,1},{577... | collective-permute-start | bytes 1327112 | tf_op jit(solution)/shard_map/ppermute | solution.py:84
  145.3 23.4 %collective-permute-start.13 = (f32[96,1152]{1,0:T(8,128)}, f32[96,1152]{1,0:T(8,128)}, u32[]{:S(2)}, u32[]{:S(2)}) collective-permute-start(f32[96,1152]{1,0:T(8,128)} %get-tuple-element.19), channel_id=1, source_target_pairs={{0,576},{192,0},{384,192},{576,384},{1,577},{193,1},{385,193},{577... | collective-permute-start | bytes 1327112 | tf_op jit(solution)/shard_map/ppermute | solution.py:84
  148.4 19.0 %all-to-all-start.1 = ((f32[32,1,32]{2,1,0:T(1,128)}), f32[32,1,32]{2,1,0:T(1,128)S(1)}, u32[]{:S(2)}, u32[]{:S(2)}) async-start(f32[32,1,32]{2,1,0:T(1,128)} %bitcast.11), calls=%async_computation.1 | async-start | bytes 32768 | tf_op jit(solution)/shard_map/all_to_all | solution.py:221
  167.9 0.8 copy-start.4
  170.8 17.9 %collective-permute-start.14 = (f32[32,1152]{1,0:T(8,128)}, f32[32,1152]{1,0:T(8,128)S(1)}, u32[]{:S(2)}, u32[]{:S(2)}) collective-permute-start(f32[32,1152]{1,0:T(8,128)} %get-tuple-element.21), channel_id=1, source_target_pairs={{0,64},{64,128},{128,0},{1,65},{65,129},{129,1},{2,66},{66,130},{1... | collective-permute-start | bytes 442376 | tf_op jit(solution)/shard_map/ppermute | solution.py:84
  173.1 21.1 %collective-permute-start.15 = (f32[32,1152]{1,0:T(8,128)S(1)}, f32[32,1152]{1,0:T(8,128)}, u32[]{:S(2)}, u32[]{:S(2)}) collective-permute-start(f32[32,1152]{1,0:T(8,128)S(1)} %get-tuple-element.22), channel_id=1, source_target_pairs={{0,128},{64,0},{128,64},{1,129},{65,1},{129,65},{2,130},{66,2},{13... | collective-permute-start | bytes 442376 | tf_op jit(solution)/shard_map/ppermute | solution.py:84
Sparse Core Ops, SparseCore 0:
  23.1 80.7 all-gather.1

commit v5 on v4

--- a/solution.py
+++ b/solution.py
@@ -71,13 +71,16 @@
     sigmoid_derivatives = (
         (jax.nn.sigmoid(pair_scores) - matching_flag.astype(jnp.float32)) * score_scaling
     ).astype(jnp.bfloat16)
-    grad_terms = lax.dot_general(
-        sigmoid_derivatives,
+    return (row_losses, sigmoid_derivatives)
+
+
+def column_terms(sigmoid_derivatives, picture_tile, start, count):
+    return lax.dot_general(
+        lax.dynamic_slice_in_dim(sigmoid_derivatives, start, count, axis=1),
         picture_tile,
         (((0,), (0,)), ((), ())),
         preferred_element_type=jnp.float32,
     )
-    return (row_losses, grad_terms)
 
 
 def shift_ring(x, axis, size, step):
@@ -99,6 +102,12 @@
             arrived[step] = backward
     tile = jnp.concatenate([arrived[d] for d in range(size)], axis=0)
     return tile if held is None else (tile, held)
+
+
+def direct_gather(x, axis, size):
+    return jnp.concatenate(
+        [x] + [shift_ring(x, axis, size, -step) for step in range(1, size)], axis=0
+    )
 
 
 def direct_scatter(x, axis, size):
@@ -146,7 +155,7 @@
         jnp.pad(prior_picture_entries, ((0, chunk_rows - prior_count), (0, 0)))
     )[0].astype(jnp.bfloat16)
     prior_tile, device_portion_count = ring_gather(
-        ring_gather(prior_norm, "mp", mp_size),
+        direct_gather(prior_norm, "mp", mp_size),
         "section",
         section_size,
         held=device_portion_count,
@@ -200,7 +209,7 @@
         + jnp.arange(row_count, dtype=jnp.int32)[None, :]
     ).reshape(-1)
 
-    row_losses, grad_terms = block_contributions(
+    row_losses, sigmoid_derivatives = block_contributions(
         picture_tile,
         target_tile,
         device_portion_count,
@@ -215,7 +224,14 @@
         [pooled_losses[:, None], prior_losses.reshape(inner_size, chunk_rows)[:, :prior_count]],
         axis=1,
     )
-    core_terms = direct_scatter(grad_terms, "core", core_size)
+    core_pos = lax.axis_index("core")
+    core_cols = device_portion_count.shape[0] // core_size
+    core_terms = column_terms(sigmoid_derivatives, picture_tile, core_pos * core_cols, core_cols)
+    for step in range(1, core_size):
+        outgoing = column_terms(
+            sigmoid_derivatives, picture_tile, (core_pos + step) % core_size * core_cols, core_cols
+        )
+        core_terms = core_terms + shift_ring(outgoing, "core", core_size, step)
     loss_parts, core_terms = lax.optimization_barrier((loss_parts, core_terms))
     own_losses = jnp.sum(
         lax.all_to_all(loss_parts, ("section", "mp"), 0, 0, tiled=True), axis=0

time: 204 us -> 207 us (1.015)
  matrix products: 15.4 us -> 19.8 us
  waiting for transfers between devices: 60.1 us -> 63.5 us
  local copies, waits for them, and re-layouts: 19.9 us -> 16.8 us
  other arithmetic: 15.2 us -> 13 us
    all_gather x1, waiting for transfers between devices: 21.3 us -> 27.3 us  [local(): lax.all_gather(caption_magnitude, ('x', 'zh', 'core'), axis=0, tiled=True)]
    dot_general x1 -> x2, matrix products: 2.98 us -> 6.62 us  [column_terms(): lax.dot_general(lax.dynamic_slice_in_dim(sigmoid_derivatives, start, coun...]
    ppermute x16, waiting for transfers between devices: 30 us -> 27.4 us  [shift_ring(): return lax.ppermute(x, axis, [(i, (i + step) % size) for i in range(size)])]
    add x2 -> x1, other arithmetic: 3.68 us -> 1.49 us  [direct_scatter(): total = total + shift_ring(outgoing, axis, size, step)]
    unnamed x24 -> x26, local copies, waits for them, and re-layouts: 12.7 us -> 11 us
  transfers between devices with their start and end apart: 19 -> 19, of which waited for: 11 -> 8; matrix products, arithmetic and copies ran while one was open for 13% -> 13% of each run, Pallas kernels for 0% -> 0%
where the time goes in v5:
time: 207 us; the launch traced here: 206 us
  starting transfers between devices  76 us (37%)
  waiting for transfers between devices  63.5 us (31%)
  matrix products  19.8 us (10%)
  local copies, waits for them, and re-layouts  16.8 us (8%)
  between operations  16.6 us (8%)
  other arithmetic  13 us (6%)
    ppermute x16, starting transfers between devices, shift_ring(): return lax.ppermute(x, axis, [(i, (i + step) % size) for i in range(size)])  56 us
    ppermute x16, waiting for transfers between devices, shift_ring(): return lax.ppermute(x, axis, [(i, (i + step) % size) for i in range(size)])  27.4 us
    all_gather x1, waiting for transfers between devices, local(): lax.all_gather(caption_magnitude, ('x', 'zh', 'core'), axis=0, tiled=True)  27.3 us
    unnamed x26, local copies, waits for them, and re-layouts  11 us
    all_to_all x1, starting transfers between devices, local(): lax.all_to_all(loss_parts, ('section', 'mp'), 0, 0, tiled=True)  10.1 us
    all_to_all x1, starting transfers between devices, local(): lax.all_to_all(jnp.broadcast_to(pooled_norm, (inner_size, pooled_norm.sha...  9.91 us
    all_to_all x1, waiting for transfers between devices, local(): lax.all_to_all(loss_parts, ('section', 'mp'), 0, 0, tiled=True)  8.86 us
    dot_general x2, matrix products, column_terms(): lax.dot_general(lax.dynamic_slice_in_dim(sigmoid_derivatives, start, coun...  6.62 us
  transfers between devices with their start and end apart: 19, of which 8 were waited for; matrix products, arithmetic and copies ran while one was open for 13% of the time, Pallas kernels for 0%

profile of v5, /device:TPU:1, one launch (start us, length us, event | category | flops | bytes accessed | tf_op | source)
XLA Modules:
  0.0 205.7 jit_solution(7605690223758499561)
XLA Ops:
  7.2 1.2 fusion.27
  8.4 1.6 constant_dynamic-update-slice_fusion.10
  10.0 8.4 %collective-permute-start = (bf16[32,1152]{1,0:T(8,128)(2,1)S(1)}, bf16[32,1152]{1,0:T(8,128)(2,1)S(1)}, u32[]{:S(2)}, u32[]{:S(2)}) collective-permute-start(bf16[32,1152]{1,0:T(8,128)(2,1)S(1)} %get-tuple-element.17), channel_id=1, source_target_pairs={{0,3},{1,0},{2,1},{3,2},{4,7},{5,4},{6,5},{7,6},{8,11},{9,8},{10,9... | collective-permute-start | bytes 221192 | tf_op jit(solution)/shard_map/ppermute | solution.py:87
  18.4 1.9 collective-permute-start.1
  20.4 2.2 %collective-permute-start.2 = (bf16[32,1152]{1,0:T(8,128)(2,1)S(1)}, bf16[32,1152]{1,0:T(8,128)(2,1)S(1)}, u32[]{:S(2)}, u32[]{:S(2)}) collective-permute-start(bf16[32,1152]{1,0:T(8,128)(2,1)S(1)} %get-tuple-element.17), channel_id=1, source_target_pairs={{0,1},{1,2},{2,3},{3,0},{4,5},{5,6},{6,7},{7,4},{8,9},{9,10},{10,1... | collective-permute-start | bytes 221192 | tf_op jit(solution)/shard_map/ppermute | solution.py:87
  22.6 1.0 fusion.32
  23.6 1.6 fusion.26
  25.2 4.1 %fusion.69 = (f32[16]{0:T(128)S(1)}, f32[16,729]{1,0:T(8,128)S(1)}) fusion(bf16[1,729,1152]{2,1,0:T(8,128)(2,1)} %param.10, bf16[1152,1152]{1,0:T(8,128)(2,1)} %param.12, s32[1152]{0:T(1024)S(1)} %add_select_fusion, bf16[1152]{0:T(1024)(128)(2,1)} %param.11), kind=kOutput, calls=%fused_computation.127 | convolution fusion | flops 69426560 | bytes 4387456 | tf_op jit(solution)/shard_map/dot_general | solution.py:24
  29.6 2.2 %fusion.12 = f32[16,1152]{1,0:T(8,128)S(1)} fusion(bf16[1152,1152]{1,0:T(8,128)(2,1)S(1)} %copy-done, bf16[1,729,1152]{2,1,0:T(8,128)(2,1)} %param.10, f32[16,729]{1,0:T(8,128)S(1)} %get-tuple-element.26, f32[16]{0:T(128)S(1)} %fusion.38, f32[16]{0:T(128)S(1)} %get-tuple-element.25), kind=kOutput, calls=%fused_computation.19 | convolution fusion | flops 69394608 | bytes 4454336 | tf_op jit(solution)/shard_map/dot_general | solution.py:31
  32.2 2.2 %convolution_reduce_fusion = bf16[1152]{0:T(1024)(128)(2,1)S(1)} fusion(bf16[1152,1]{0,1:T(2,128)(2,1)S(1)} %reshape.163, bf16[1152,1152]{1,0:T(8,128)(2,1)} %param.14), kind=kOutput, calls=%fused_computation.20 | convolution fusion | flops 2654208 | bytes 2658816 | tf_op jit(solution)/shard_map/dot_general | solution.py:38
  36.3 1.1 reduce.9
  37.4 0.8 reshape.168
  38.1 9.9 %all-to-all-start = ((bf16[32,2,576]{2,1,0:T(2,128)(2,1)}), bf16[32,2,576]{2,1,0:T(2,128)(2,1)S(1)}, u32[]{:S(2)}, u32[]{:S(2)}) async-start(bf16[32,2,576]{2,1,0:T(2,128)(2,1)} %reshape.168), calls=%async_computation | async-start | bytes 163840 | tf_op jit(solution)/shard_map/all_to_all | solution.py:173
  50.2 3.1 %collective-permute-start.6 = (bf16[128,1152]{1,0:T(8,128)(2,1)}, bf16[128,1152]{1,0:T(8,128)(2,1)S(1)}, u32[]{:S(2)}, u32[]{:S(2)}) collective-permute-start(bf16[128,1152]{1,0:T(8,128)(2,1)} %pad_maximum_fusion), channel_id=1, source_target_pairs={{0,4},{4,8},{8,12},{12,16},{16,20},{20,24},{24,28},{28,0},{1,5},{5... | collective-permute-start | bytes 884744 | tf_op jit(solution)/shard_map/ppermute | solution.py:87
  54.8 3.4 %collective-permute-start.3 = (bf16[128,1152]{1,0:T(8,128)(2,1)}, bf16[128,1152]{1,0:T(8,128)(2,1)}, u32[]{:S(2)}, u32[]{:S(2)}) collective-permute-start(bf16[128,1152]{1,0:T(8,128)(2,1)} %pad_maximum_fusion), channel_id=1, source_target_pairs={{0,28},{4,0},{8,4},{12,8},{16,12},{20,16},{24,20},{28,24},{1,29},{... | collective-permute-start | bytes 884744 | tf_op jit(solution)/shard_map/ppermute | solution.py:87
  58.2 3.4 %collective-permute-done.6 = bf16[128,1152]{1,0:T(8,128)(2,1)S(1)} collective-permute-done((bf16[128,1152]{1,0:T(8,128)(2,1)}, bf16[128,1152]{1,0:T(8,128)(2,1)S(1)}, u32[]{:S(2)}, u32[]{:S(2)}) %collective-permute-start.6) | collective-permute-done | bytes 294944 | tf_op jit(solution)/shard_map/ppermute | solution.py:87
  61.6 1.9 collective-permute-start.7
  64.1 4.6 %collective-permute-start.4 = (bf16[128,1152]{1,0:T(8,128)(2,1)}, bf16[128,1152]{1,0:T(8,128)(2,1)}, u32[]{:S(2)}, u32[]{:S(2)}) collective-permute-start(bf16[128,1152]{1,0:T(8,128)(2,1)} %collective-permute-done.3), channel_id=1, source_target_pairs={{0,28},{4,0},{8,4},{12,8},{16,12},{20,16},{24,20},{28,24},{1,29},{... | collective-permute-start | bytes 884744 | tf_op jit(solution)/shard_map/ppermute | solution.py:87
  69.3 2.1 %collective-permute-done.7 = bf16[128,1152]{1,0:T(8,128)(2,1)} collective-permute-done((bf16[128,1152]{1,0:T(8,128)(2,1)S(1)}, bf16[128,1152]{1,0:T(8,128)(2,1)}, u32[]{:S(2)}, u32[]{:S(2)}) %collective-permute-start.7) | collective-permute-done | bytes 294944 | tf_op jit(solution)/shard_map/ppermute | solution.py:87
  71.4 1.9 collective-permute-start.8
  74.1 4.6 %collective-permute-start.5 = (bf16[128,1152]{1,0:T(8,128)(2,1)}, bf16[128,1152]{1,0:T(8,128)(2,1)S(1)}, u32[]{:S(2)}, u32[]{:S(2)}) collective-permute-start(bf16[128,1152]{1,0:T(8,128)(2,1)} %collective-permute-done.4), channel_id=1, source_target_pairs={{0,28},{4,0},{8,4},{12,8},{16,12},{20,16},{24,20},{28,24},{1,29},{... | collective-permute-start | bytes 884744 | tf_op jit(solution)/shard_map/ppermute | solution.py:87
  78.7 1.7 constant_dynamic-update-slice_fusion.6
  80.4 27.3 %all-gather.2.cloned.1.call-done = bf16[768,1152]{1,0:T(8,128)(2,1)} async-done(((bf16[32,1152]{1,0:T(8,128)(2,1)}), bf16[768,1152]{1,0:T(8,128)(2,1)}) %all-gather.2.cloned.1.call-update) | async-done | bytes 1769488 | tf_op jit(solution)/shard_map/all_gather | solution.py:151
  107.6 2.2 %collective-permute-start.9 = (bf16[128,1152]{1,0:T(8,128)(2,1)}, bf16[128,1152]{1,0:T(8,128)(2,1)S(1)}, u32[]{:S(2)}, u32[]{:S(2)}) collective-permute-start(bf16[128,1152]{1,0:T(8,128)(2,1)} %collective-permute-done.8), channel_id=1, source_target_pairs={{0,4},{4,8},{8,12},{12,16},{16,20},{20,24},{24,28},{28,0},{1,5},{5... | collective-permute-start | bytes 884744 | tf_op jit(solution)/shard_map/ppermute | solution.py:87
  109.8 1.7 constant_dynamic-update-slice_fusion.5
  112.3 1.8 copy.18
  114.0 5.3 %collective-permute-done.9 = bf16[128,1152]{1,0:T(8,128)(2,1)S(1)} collective-permute-done((bf16[128,1152]{1,0:T(8,128)(2,1)}, bf16[128,1152]{1,0:T(8,128)(2,1)S(1)}, u32[]{:S(2)}, u32[]{:S(2)}) %collective-permute-start.9) | collective-permute-done | bytes 294944 | tf_op jit(solution)/shard_map/ppermute | solution.py:87
  119.4 1.0 constant_dynamic-update-slice_fusion.2
  120.4 1.0 constant_dynamic-update-slice_fusion.1
  121.4 4.6 %fusion.3 = (bf16[1056,768]{1,0:T(8,128)(2,1)S(1)}, f32[1056]{0:T(1024)S(1)}) fusion(f32[]{:T(128)} %bitcast.53, s32[768]{0:T(1024)S(1)} %add.264, s32[1056]{0:T(1024)S(1)} %pad_add_fusion, f32[]{:T(128)} %bitcast.54, bf16[1056,1152]{1,0:T(8,128)(2,1)S(1)} %bitcast_dynamic-update-slice_fusion, bf16[768,1152]{1,0:T(8,128)(2,1)S(1)} %bitcast.58), kind=kOutput, calls=%fused_computation.8 | convolution fusion | flops 1883159552 | bytes 5836040 | tf_op jit(solution)/shard_map/dot_general | solution.py:59
  126.0 2.7 %fusion.14 = f32[384,1152]{1,0:T(8,128)} fusion(bf16[1056,1152]{1,0:T(8,128)(2,1)S(1)} %bitcast_dynamic-update-slice_fusion, bf16[1056,768]{1,0:T(8,128)(2,1)S(1)} %get-tuple-element.18, s32[]{:T(128)S(6)} %select_n.175), kind=kOutput, calls=%fused_computation.21 | convolution fusion | flops 934281216 | bytes 5013508 | tf_op jit(solution)/shard_map/dot_general | solution.py:78
  128.7 3.1 %collective-permute-start.10 = (f32[384,1152]{1,0:T(8,128)}, f32[384,1152]{1,0:T(8,128)}, u32[]{:S(2)}, u32[]{:S(2)}) collective-permute-start(f32[384,1152]{1,0:T(8,128)} %fusion.14), channel_id=1, source_target_pairs={{0,32},{32,0},{1,33},{33,1},{2,34},{34,2},{3,35},{35,3},{4,36},{36... | collective-permute-start | bytes 5308424 | tf_op jit(solution)/shard_map/ppermute | solution.py:87
  132.9 2.4 %collective-permute-done.10 = f32[384,1152]{1,0:T(8,128)} collective-permute-done((f32[384,1152]{1,0:T(8,128)}, f32[384,1152]{1,0:T(8,128)}, u32[]{:S(2)}, u32[]{:S(2)}) %collective-permute-start.10) | collective-permute-done | bytes 1769504 | tf_op jit(solution)/shard_map/ppermute | solution.py:87
  135.3 3.9 %convolution_add_fusion = f32[384,1152]{1,0:T(8,128)S(1)} fusion(f32[384,1152]{1,0:T(8,128)} %collective-permute-done.10, bf16[1056,1152]{1,0:T(8,128)(2,1)} %copy-done.2, bf16[1056,768]{1,0:T(8,128)(2,1)} %copy-done.4, s32[]{:T(128)S(6)} %select_n.173), kind=kOutput, calls=%fused_computation.12 | convolution fusion | flops 934723584 | bytes 6782980 | tf_op jit(solution)/shard_map/dot_general | solution.py:78
  139.3 1.2 copy-done.3
  140.5 1.1 dynamic-slice_bitcast_fusion.2
  141.6 2.1 %collective-permute-start.11 = (f32[96,1152]{1,0:T(8,128)}, f32[96,1152]{1,0:T(8,128)S(1)}, u32[]{:S(2)}, u32[]{:S(2)}) collective-permute-start(f32[96,1152]{1,0:T(8,128)} %get-tuple-element.20), channel_id=1, source_target_pairs={{0,192},{192,384},{384,576},{576,0},{1,193},{193,385},{385,577},{5... | collective-permute-start | bytes 1327112 | tf_op jit(solution)/shard_map/ppermute | solution.py:87
  143.8 4.3 %collective-permute-start.12 = (f32[96,1152]{1,0:T(8,128)}, f32[96,1152]{1,0:T(8,128)}, u32[]{:S(2)}, u32[]{:S(2)}) collective-permute-start(f32[96,1152]{1,0:T(8,128)} %get-tuple-element.22), channel_id=1, source_target_pairs={{0,384},{192,576},{384,0},{576,192},{1,385},{193,577},{385,1},{577... | collective-permute-start | bytes 1327112 | tf_op jit(solution)/shard_map/ppermute | solution.py:87
  148.1 3.1 %collective-permute-start.13 = (f32[96,1152]{1,0:T(8,128)}, f32[96,1152]{1,0:T(8,128)}, u32[]{:S(2)}, u32[]{:S(2)}) collective-permute-start(f32[96,1152]{1,0:T(8,128)} %get-tuple-element.21), channel_id=1, source_target_pairs={{0,576},{192,0},{384,192},{576,384},{1,577},{193,1},{385,193},{577... | collective-permute-start | bytes 1327112 | tf_op jit(solution)/shard_map/ppermute | solution.py:87
  151.2 10.1 %all-to-all-start.1 = ((f32[32,1,32]{2,1,0:T(1,128)}), f32[32,1,32]{2,1,0:T(1,128)S(1)}, u32[]{:S(2)}, u32[]{:S(2)}) async-start(f32[32,1,32]{2,1,0:T(1,128)} %bitcast.8), calls=%async_computation.1 | async-start | bytes 32768 | tf_op jit(solution)/shard_map/all_to_all | solution.py:237
  161.3 8.9 %all-to-all-done.1 = f32[32,1,32]{2,1,0:T(1,128)S(1)} async-done(((f32[32,1,32]{2,1,0:T(1,128)}), f32[32,1,32]{2,1,0:T(1,128)S(1)}, u32[]{:S(2)}, u32[]{:S(2)}) %all-to-all-start.1) | async-done | bytes 4128 | tf_op jit(solution)/shard_map/all_to_all | solution.py:237
  171.5 1.5 fusion.19
  173.7 2.3 %collective-permute-start.14 = (f32[32,1152]{1,0:T(8,128)}, f32[32,1152]{1,0:T(8,128)S(1)}, u32[]{:S(2)}, u32[]{:S(2)}) collective-permute-start(f32[32,1152]{1,0:T(8,128)} %get-tuple-element.23), channel_id=1, source_target_pairs={{0,64},{64,128},{128,0},{1,65},{65,129},{129,1},{2,66},{66,130},{1... | collective-permute-start | bytes 442376 | tf_op jit(solution)/shard_map/ppermute | solution.py:87
  175.9 6.9 %collective-permute-start.15 = (f32[32,1152]{1,0:T(8,128)S(1)}, f32[32,1152]{1,0:T(8,128)}, u32[]{:S(2)}, u32[]{:S(2)}) collective-permute-start(f32[32,1152]{1,0:T(8,128)S(1)} %get-tuple-element.24), channel_id=1, source_target_pairs={{0,128},{64,0},{128,64},{1,129},{65,1},{129,65},{2,130},{66,2},{13... | collective-permute-start | bytes 442376 | tf_op jit(solution)/shard_map/ppermute | solution.py:87
  182.9 8.8 %collective-permute-done.14 = f32[32,1152]{1,0:T(8,128)S(1)} collective-permute-done((f32[32,1152]{1,0:T(8,128)}, f32[32,1152]{1,0:T(8,128)S(1)}, u32[]{:S(2)}, u32[]{:S(2)}) %collective-permute-start.14) | collective-permute-done | bytes 147488 | tf_op jit(solution)/shard_map/ppermute | solution.py:87
  191.6 5.4 %collective-permute-done.15 = f32[32,1152]{1,0:T(8,128)} collective-permute-done((f32[32,1152]{1,0:T(8,128)S(1)}, f32[32,1152]{1,0:T(8,128)}, u32[]{:S(2)}, u32[]{:S(2)}) %collective-permute-start.15) | collective-permute-done | bytes 147488 | tf_op jit(solution)/shard_map/ppermute | solution.py:87
  197.0 1.1 fusion.29
  198.1 0.8 fusion.31
  (68 shorter events, 9.9 us)
Async XLA Ops:
  7.2 22.4 %copy-start = (bf16[1152,1152]{1,0:T(8,128)(2,1)S(1)}, bf16[1152,1152]{1,0:T(8,128)(2,1)}, u32[]{:S(2)}) copy-start(bf16[1152,1152]{1,0:T(8,128)(2,1)} %param.13) | copy-start | bytes 7962628
  7.2 100.5 %all-gather.2.cloned.1.call-start = ((), (), s32[]{:S(2)}) async-start(), calls=%async_computation.2 | async-start | bytes 1843200 | tf_op jit(solution)/shard_map/all_gather | solution.py:151
  10.0 39.5 %collective-permute-start = (bf16[32,1152]{1,0:T(8,128)(2,1)S(1)}, bf16[32,1152]{1,0:T(8,128)(2,1)S(1)}, u32[]{:S(2)}, u32[]{:S(2)}) collective-permute-start(bf16[32,1152]{1,0:T(8,128)(2,1)S(1)} %get-tuple-element.17), channel_id=1, source_target_pairs={{0,3},{1,0},{2,1},{3,2},{4,7},{5,4},{6,5},{7,6},{8,11},{9,8},{10,9... | collective-permute-start | bytes 221192 | tf_op jit(solution)/shard_map/ppermute | solution.py:87
  18.4 31.0 %collective-permute-start.1 = (bf16[32,1152]{1,0:T(8,128)(2,1)S(1)}, bf16[32,1152]{1,0:T(8,128)(2,1)S(1)}, u32[]{:S(2)}, u32[]{:S(2)}) collective-permute-start(bf16[32,1152]{1,0:T(8,128)(2,1)S(1)} %get-tuple-element.17), channel_id=1, source_target_pairs={{0,2},{1,3},{2,0},{3,1},{4,6},{5,7},{6,4},{7,5},{8,10},{9,11},{10,... | collective-permute-start | bytes 221192 | tf_op jit(solution)/shard_map/ppermute | solution.py:87
  20.4 29.1 %collective-permute-start.2 = (bf16[32,1152]{1,0:T(8,128)(2,1)S(1)}, bf16[32,1152]{1,0:T(8,128)(2,1)S(1)}, u32[]{:S(2)}, u32[]{:S(2)}) collective-permute-start(bf16[32,1152]{1,0:T(8,128)(2,1)S(1)} %get-tuple-element.17), channel_id=1, source_target_pairs={{0,1},{1,2},{2,3},{3,0},{4,5},{5,6},{6,7},{7,4},{8,9},{9,10},{10,1... | collective-permute-start | bytes 221192 | tf_op jit(solution)/shard_map/ppermute | solution.py:87
  38.1 35.8 %all-to-all-start = ((bf16[32,2,576]{2,1,0:T(2,128)(2,1)}), bf16[32,2,576]{2,1,0:T(2,128)(2,1)S(1)}, u32[]{:S(2)}, u32[]{:S(2)}) async-start(bf16[32,2,576]{2,1,0:T(2,128)(2,1)} %reshape.168), calls=%async_computation | async-start | bytes 163840 | tf_op jit(solution)/shard_map/all_to_all | solution.py:173
  50.2 11.4 %collective-permute-start.6 = (bf16[128,1152]{1,0:T(8,128)(2,1)}, bf16[128,1152]{1,0:T(8,128)(2,1)S(1)}, u32[]{:S(2)}, u32[]{:S(2)}) collective-permute-start(bf16[128,1152]{1,0:T(8,128)(2,1)} %pad_maximum_fusion), channel_id=1, source_target_pairs={{0,4},{4,8},{8,12},{12,16},{16,20},{20,24},{24,28},{28,0},{1,5},{5... | collective-permute-start | bytes 884744 | tf_op jit(solution)/shard_map/ppermute | solution.py:87
  54.8 9.3 %collective-permute-start.3 = (bf16[128,1152]{1,0:T(8,128)(2,1)}, bf16[128,1152]{1,0:T(8,128)(2,1)}, u32[]{:S(2)}, u32[]{:S(2)}) collective-permute-start(bf16[128,1152]{1,0:T(8,128)(2,1)} %pad_maximum_fusion), channel_id=1, source_target_pairs={{0,28},{4,0},{8,4},{12,8},{16,12},{20,16},{24,20},{28,24},{1,29},{... | collective-permute-start | bytes 884744 | tf_op jit(solution)/shard_map/ppermute | solution.py:87
  61.6 9.8 %collective-permute-start.7 = (bf16[128,1152]{1,0:T(8,128)(2,1)S(1)}, bf16[128,1152]{1,0:T(8,128)(2,1)}, u32[]{:S(2)}, u32[]{:S(2)}) collective-permute-start(bf16[128,1152]{1,0:T(8,128)(2,1)S(1)} %collective-permute-done.6), channel_id=1, source_target_pairs={{0,4},{4,8},{8,12},{12,16},{16,20},{20,24},{24,28},{28,0},{1,5},{5... | collective-permute-start | bytes 884744 | tf_op jit(solution)/shard_map/ppermute | solution.py:87
  64.1 10.0 %collective-permute-start.4 = (bf16[128,1152]{1,0:T(8,128)(2,1)}, bf16[128,1152]{1,0:T(8,128)(2,1)}, u32[]{:S(2)}, u32[]{:S(2)}) collective-permute-start(bf16[128,1152]{1,0:T(8,128)(2,1)} %collective-permute-done.3), channel_id=1, source_target_pairs={{0,28},{4,0},{8,4},{12,8},{16,12},{20,16},{24,20},{28,24},{1,29},{... | collective-permute-start | bytes 884744 | tf_op jit(solution)/shard_map/ppermute | solution.py:87
  71.4 9.0 %collective-permute-start.8 = (bf16[128,1152]{1,0:T(8,128)(2,1)}, bf16[128,1152]{1,0:T(8,128)(2,1)}, u32[]{:S(2)}, u32[]{:S(2)}) collective-permute-start(bf16[128,1152]{1,0:T(8,128)(2,1)} %collective-permute-done.7), channel_id=1, source_target_pairs={{0,4},{4,8},{8,12},{12,16},{16,20},{20,24},{24,28},{28,0},{1,5},{5... | collective-permute-start | bytes 884744 | tf_op jit(solution)/shard_map/ppermute | solution.py:87
  74.1 37.4 %collective-permute-start.5 = (bf16[128,1152]{1,0:T(8,128)(2,1)}, bf16[128,1152]{1,0:T(8,128)(2,1)S(1)}, u32[]{:S(2)}, u32[]{:S(2)}) collective-permute-start(bf16[128,1152]{1,0:T(8,128)(2,1)} %collective-permute-done.4), channel_id=1, source_target_pairs={{0,28},{4,0},{8,4},{12,8},{16,12},{20,16},{24,20},{28,24},{1,29},{... | collective-permute-start | bytes 884744 | tf_op jit(solution)/shard_map/ppermute | solution.py:87
  107.6 11.7 %collective-permute-start.9 = (bf16[128,1152]{1,0:T(8,128)(2,1)}, bf16[128,1152]{1,0:T(8,128)(2,1)S(1)}, u32[]{:S(2)}, u32[]{:S(2)}) collective-permute-start(bf16[128,1152]{1,0:T(8,128)(2,1)} %collective-permute-done.8), channel_id=1, source_target_pairs={{0,4},{4,8},{8,12},{12,16},{16,20},{20,24},{24,28},{28,0},{1,5},{5... | collective-permute-start | bytes 884744 | tf_op jit(solution)/shard_map/ppermute | solution.py:87
  112.3 7.1 %copy-start.1 = (bf16[1056,1152]{1,0:T(8,128)(2,1)S(1)}, bf16[1056,1152]{1,0:T(8,128)(2,1)}, u32[]{:S(2)}) copy-start(bf16[1056,1152]{1,0:T(8,128)(2,1)} %constant_dynamic-update-slice_fusion.4) | copy-start | bytes 7299076
  121.4 4.6 %copy-start.2 = (bf16[1056,1152]{1,0:T(8,128)(2,1)}, bf16[1056,1152]{1,0:T(8,128)(2,1)S(1)}, u32[]{:S(2)}) copy-start(bf16[1056,1152]{1,0:T(8,128)(2,1)S(1)} %bitcast_dynamic-update-slice_fusion) | copy-start | bytes 7299076
  126.0 2.7 %copy-start.4 = (bf16[1056,768]{1,0:T(8,128)(2,1)}, bf16[1056,768]{1,0:T(8,128)(2,1)S(1)}, u32[]{:S(2)}) copy-start(bf16[1056,768]{1,0:T(8,128)(2,1)S(1)} %get-tuple-element.18) | copy-start | bytes 4866052
  128.7 6.6 %collective-permute-start.10 = (f32[384,1152]{1,0:T(8,128)}, f32[384,1152]{1,0:T(8,128)}, u32[]{:S(2)}, u32[]{:S(2)}) collective-permute-start(f32[384,1152]{1,0:T(8,128)} %fusion.14), channel_id=1, source_target_pairs={{0,32},{32,0},{1,33},{33,1},{2,34},{34,2},{3,35},{35,3},{4,36},{36... | collective-permute-start | bytes 5308424 | tf_op jit(solution)/shard_map/ppermute | solution.py:87
  139.3 1.2 copy-start.3
  140.5 56.5 %copy-start.5 = (bf16[32,1152]{1,0:T(8,128)(2,1)S(1)}, bf16[32,1152]{1,0:T(8,128)(2,1)}, u32[]{:S(2)}) copy-start(bf16[32,1152]{1,0:T(8,128)(2,1)} %param.16) | copy-start | bytes 221188
  141.6 29.1 %collective-permute-start.11 = (f32[96,1152]{1,0:T(8,128)}, f32[96,1152]{1,0:T(8,128)S(1)}, u32[]{:S(2)}, u32[]{:S(2)}) collective-permute-start(f32[96,1152]{1,0:T(8,128)} %get-tuple-element.20), channel_id=1, source_target_pairs={{0,192},{192,384},{384,576},{576,0},{1,193},{193,385},{385,577},{5... | collective-permute-start | bytes 1327112 | tf_op jit(solution)/shard_map/ppermute | solution.py:87
  143.8 27.0 %collective-permute-start.12 = (f32[96,1152]{1,0:T(8,128)}, f32[96,1152]{1,0:T(8,128)}, u32[]{:S(2)}, u32[]{:S(2)}) collective-permute-start(f32[96,1152]{1,0:T(8,128)} %get-tuple-element.22), channel_id=1, source_target_pairs={{0,384},{192,576},{384,0},{576,192},{1,385},{193,577},{385,1},{577... | collective-permute-start | bytes 1327112 | tf_op jit(solution)/shard_map/ppermute | solution.py:87
  148.1 23.4 %collective-permute-start.13 = (f32[96,1152]{1,0:T(8,128)}, f32[96,1152]{1,0:T(8,128)}, u32[]{:S(2)}, u32[]{:S(2)}) collective-permute-start(f32[96,1152]{1,0:T(8,128)} %get-tuple-element.21), channel_id=1, source_target_pairs={{0,576},{192,0},{384,192},{576,384},{1,577},{193,1},{385,193},{577... | collective-permute-start | bytes 1327112 | tf_op jit(solution)/shard_map/ppermute | solution.py:87
  151.2 19.0 %all-to-all-start.1 = ((f32[32,1,32]{2,1,0:T(1,128)}), f32[32,1,32]{2,1,0:T(1,128)S(1)}, u32[]{:S(2)}, u32[]{:S(2)}) async-start(f32[32,1,32]{2,1,0:T(1,128)} %bitcast.8), calls=%async_computation.1 | async-start | bytes 32768 | tf_op jit(solution)/shard_map/all_to_all | solution.py:237
  170.7 0.8 copy-start.6
  173.7 17.9 %collective-permute-start.14 = (f32[32,1152]{1,0:T(8,128)}, f32[32,1152]{1,0:T(8,128)S(1)}, u32[]{:S(2)}, u32[]{:S(2)}) collective-permute-start(f32[32,1152]{1,0:T(8,128)} %get-tuple-element.23), channel_id=1, source_target_pairs={{0,64},{64,128},{128,0},{1,65},{65,129},{129,1},{2,66},{66,130},{1... | collective-permute-start | bytes 442376 | tf_op jit(solution)/shard_map/ppermute | solution.py:87
  175.9 21.1 %collective-permute-start.15 = (f32[32,1152]{1,0:T(8,128)S(1)}, f32[32,1152]{1,0:T(8,128)}, u32[]{:S(2)}, u32[]{:S(2)}) collective-permute-start(f32[32,1152]{1,0:T(8,128)S(1)} %get-tuple-element.24), channel_id=1, source_target_pairs={{0,128},{64,0},{128,64},{1,129},{65,1},{129,65},{2,130},{66,2},{13... | collective-permute-start | bytes 442376 | tf_op jit(solution)/shard_map/ppermute | solution.py:87
Sparse Core Ops, SparseCore 0:
  25.3 82.2 all-gather.1

commit v6 on v4

--- a/solution.py
+++ b/solution.py
@@ -217,11 +217,15 @@
     )
     core_terms = direct_scatter(grad_terms, "core", core_size)
     loss_parts, core_terms = lax.optimization_barrier((loss_parts, core_terms))
-    own_losses = jnp.sum(
-        lax.all_to_all(loss_parts, ("section", "mp"), 0, 0, tiled=True), axis=0
+    section_losses = jnp.sum(
+        lax.all_to_all(
+            loss_parts.reshape(section_size, mp_size, row_count), "mp", 1, 1, tiled=True
+        ),
+        axis=1,
     )
     x_terms = direct_scatter(core_terms, "x", x_size)
-    own_losses, x_terms = lax.optimization_barrier((own_losses, x_terms))
+    section_losses, x_terms = lax.optimization_barrier((section_losses, x_terms))
+    own_losses = jnp.sum(lax.all_to_all(section_losses, "section", 0, 0, tiled=True), axis=0)
     own_terms = direct_scatter(x_terms, "zh", zh_size)
     along = jnp.sum(text_unit * own_terms, axis=1, keepdims=True)
     text_grad = (own_terms - text_unit * along) * text_inverse

time: 204 us -> 203 us (level)
  waiting for transfers between devices: 60.1 us -> 57.4 us
    ppermute x16, waiting for transfers between devices: 30 us -> 24.4 us  [shift_ring(): return lax.ppermute(x, axis, [(i, (i + step) % size) for i in range(size)])]
    all_to_all x1 -> x2, waiting for transfers between devices: 8.86 us -> 11.8 us  [the longest x1 6.93 us: local(): lax.all_to_all(section_losses, 'section', 0, 0, tiled=True)]
    all_to_all x1 -> x2, starting transfers between devices: 10.1 us -> 10.3 us  [the longest x1 5.53 us: local(): lax.all_to_all(section_losses, 'section', 0, 0, tiled=True)]
    unnamed x24 -> x26, local copies, waits for them, and re-layouts: 12.7 us -> 12.7 us
  transfers between devices with their start and end apart: 19 -> 20, of which waited for: 11 -> 13; matrix products, arithmetic and copies ran while one was open for 13% -> 14% of each run, Pallas kernels for 0% -> 0%
where the time goes in v6:
time: 203 us; the launch traced here: 202 us
  starting transfers between devices  75.9 us (37%)
  waiting for transfers between devices  57.4 us (28%)
  local copies, waits for them, and re-layouts  20.4 us (10%)
  between operations  16.5 us (8%)
  other arithmetic  15.9 us (8%)
  matrix products  15.4 us (8%)
    ppermute x16, starting transfers between devices, shift_ring(): return lax.ppermute(x, axis, [(i, (i + step) % size) for i in range(size)])  57.2 us
    ppermute x16, waiting for transfers between devices, shift_ring(): return lax.ppermute(x, axis, [(i, (i + step) % size) for i in range(size)])  24.4 us
    all_gather x1, waiting for transfers between devices, local(): lax.all_gather(caption_magnitude, ('x', 'zh', 'core'), axis=0, tiled=True)  21.3 us
    unnamed x26, local copies, waits for them, and re-layouts  12.7 us
    all_to_all x1, starting transfers between devices, local(): lax.all_to_all(jnp.broadcast_to(pooled_norm, (inner_size, pooled_norm.sha...  8.38 us
    all_to_all x1, waiting for transfers between devices, local(): lax.all_to_all(section_losses, 'section', 0, 0, tiled=True)  6.93 us
    all_to_all x1, starting transfers between devices, local(): lax.all_to_all(section_losses, 'section', 0, 0, tiled=True)  5.53 us
    all_to_all x1, waiting for transfers between devices, local(): lax.all_to_all(loss_parts.reshape(section_size, mp_size, row_count), 'mp'...  4.82 us
  transfers between devices with their start and end apart: 20, of which 13 were waited for; matrix products, arithmetic and copies ran while one was open for 14% of the time, Pallas kernels for 0%

profile of v6, /device:TPU:1, one launch (start us, length us, event | category | flops | bytes accessed | tf_op | source)
XLA Modules:
  0.0 201.5 jit_solution(6175932648599158431)
XLA Ops:
  7.2 1.2 fusion.27
  8.4 1.6 constant_dynamic-update-slice_fusion.10
  10.0 4.8 %collective-permute-start.1 = (bf16[32,1152]{1,0:T(8,128)(2,1)S(1)}, bf16[32,1152]{1,0:T(8,128)(2,1)S(1)}, u32[]{:S(2)}, u32[]{:S(2)}) collective-permute-start(bf16[32,1152]{1,0:T(8,128)(2,1)S(1)} %get-tuple-element.17), channel_id=1, source_target_pairs={{0,1},{1,2},{2,3},{3,0},{4,5},{5,6},{6,7},{7,4},{8,9},{9,10},{10,1... | collective-permute-start | bytes 221192 | tf_op jit(solution)/shard_map/ppermute | solution.py:84
  14.8 5.5 %collective-permute-start = (bf16[32,1152]{1,0:T(8,128)(2,1)S(1)}, bf16[32,1152]{1,0:T(8,128)(2,1)S(1)}, u32[]{:S(2)}, u32[]{:S(2)}) collective-permute-start(bf16[32,1152]{1,0:T(8,128)(2,1)S(1)} %get-tuple-element.17), channel_id=1, source_target_pairs={{0,3},{1,0},{2,1},{3,2},{4,7},{5,4},{6,5},{7,6},{8,11},{9,8},{10,9... | collective-permute-start | bytes 221192 | tf_op jit(solution)/shard_map/ppermute | solution.py:84
  21.4 1.6 fusion.26
  23.0 4.1 %fusion.68 = (f32[16]{0:T(128)S(1)}, f32[16,729]{1,0:T(8,128)S(1)}) fusion(bf16[1,729,1152]{2,1,0:T(8,128)(2,1)} %param.10, bf16[1152,1152]{1,0:T(8,128)(2,1)} %param.12, s32[1152]{0:T(1024)S(1)} %add_select_fusion, bf16[1152]{0:T(1024)(128)(2,1)} %param.11), kind=kOutput, calls=%fused_computation.126 | convolution fusion | flops 69426560 | bytes 4387456 | tf_op jit(solution)/shard_map/dot_general | solution.py:24
  27.4 2.2 %fusion.15 = f32[16,1152]{1,0:T(8,128)S(1)} fusion(bf16[1152,1152]{1,0:T(8,128)(2,1)S(1)} %copy-done, bf16[1,729,1152]{2,1,0:T(8,128)(2,1)} %param.10, f32[16,729]{1,0:T(8,128)S(1)} %get-tuple-element.24, f32[16]{0:T(128)S(1)} %fusion.38, f32[16]{0:T(128)S(1)} %get-tuple-element.23), kind=kOutput, calls=%fused_computation.22 | convolution fusion | flops 69394608 | bytes 4454336 | tf_op jit(solution)/shard_map/dot_general | solution.py:31
  30.0 2.2 %convolution_reduce_fusion = bf16[1152]{0:T(1024)(128)(2,1)S(1)} fusion(bf16[1152,1]{0,1:T(2,128)(2,1)S(1)} %reshape.171, bf16[1152,1152]{1,0:T(8,128)(2,1)} %param.14), kind=kOutput, calls=%fused_computation.23 | convolution fusion | flops 2654208 | bytes 2658816 | tf_op jit(solution)/shard_map/dot_general | solution.py:38
  34.1 1.1 reduce.9
  35.9 8.4 %all-to-all-start = ((bf16[32,2,576]{2,1,0:T(2,128)(2,1)}), bf16[32,2,576]{2,1,0:T(2,128)(2,1)S(1)}, u32[]{:S(2)}, u32[]{:S(2)}) async-start(bf16[32,2,576]{2,1,0:T(2,128)(2,1)} %reshape.176), calls=%async_computation | async-start | bytes 163840 | tf_op jit(solution)/shard_map/all_to_all | solution.py:164
  45.7 3.1 %collective-permute-start.2 = (bf16[32,1152]{1,0:T(8,128)(2,1)S(1)}, bf16[32,1152]{1,0:T(8,128)(2,1)S(1)}, u32[]{:S(2)}, u32[]{:S(2)}) collective-permute-start(bf16[32,1152]{1,0:T(8,128)(2,1)S(1)} %collective-permute-done.1), channel_id=1, source_target_pairs={{0,1},{1,2},{2,3},{3,0},{4,5},{5,6},{6,7},{7,4},{8,9},{9,10},{10,1... | collective-permute-start | bytes 221192 | tf_op jit(solution)/shard_map/ppermute | solution.py:84
  48.9 5.4 %collective-permute-done.2 = bf16[32,1152]{1,0:T(8,128)(2,1)S(1)} collective-permute-done((bf16[32,1152]{1,0:T(8,128)(2,1)S(1)}, bf16[32,1152]{1,0:T(8,128)(2,1)S(1)}, u32[]{:S(2)}, u32[]{:S(2)}) %collective-permute-start.2) | collective-permute-done | bytes 73760 | tf_op jit(solution)/shard_map/ppermute | solution.py:84
  55.0 3.1 %collective-permute-start.6 = (bf16[128,1152]{1,0:T(8,128)(2,1)}, bf16[128,1152]{1,0:T(8,128)(2,1)S(1)}, u32[]{:S(2)}, u32[]{:S(2)}) collective-permute-start(bf16[128,1152]{1,0:T(8,128)(2,1)} %pad_maximum_fusion), channel_id=1, source_target_pairs={{0,4},{4,8},{8,12},{12,16},{16,20},{20,24},{24,28},{28,0},{1,5},{5... | collective-permute-start | bytes 884744 | tf_op jit(solution)/shard_map/ppermute | solution.py:84
  59.6 3.4 %collective-permute-start.3 = (bf16[128,1152]{1,0:T(8,128)(2,1)}, bf16[128,1152]{1,0:T(8,128)(2,1)}, u32[]{:S(2)}, u32[]{:S(2)}) collective-permute-start(bf16[128,1152]{1,0:T(8,128)(2,1)} %pad_maximum_fusion), channel_id=1, source_target_pairs={{0,28},{4,0},{8,4},{12,8},{16,12},{20,16},{24,20},{28,24},{1,29},{... | collective-permute-start | bytes 884744 | tf_op jit(solution)/shard_map/ppermute | solution.py:84
  63.9 1.9 collective-permute-start.7
  66.5 1.1 collective-permute-done.3
  67.5 4.4 %collective-permute-start.4 = (bf16[128,1152]{1,0:T(8,128)(2,1)}, bf16[128,1152]{1,0:T(8,128)(2,1)}, u32[]{:S(2)}, u32[]{:S(2)}) collective-permute-start(bf16[128,1152]{1,0:T(8,128)(2,1)} %collective-permute-done.3), channel_id=1, source_target_pairs={{0,28},{4,0},{8,4},{12,8},{16,12},{20,16},{24,20},{28,24},{1,29},{... | collective-permute-start | bytes 884744 | tf_op jit(solution)/shard_map/ppermute | solution.py:84
  72.7 1.9 collective-permute-start.8
  75.9 5.0 %collective-permute-start.5 = (bf16[128,1152]{1,0:T(8,128)(2,1)}, bf16[128,1152]{1,0:T(8,128)(2,1)S(1)}, u32[]{:S(2)}, u32[]{:S(2)}) collective-permute-start(bf16[128,1152]{1,0:T(8,128)(2,1)} %collective-permute-done.4), channel_id=1, source_target_pairs={{0,28},{4,0},{8,4},{12,8},{16,12},{20,16},{24,20},{28,24},{1,29},{... | collective-permute-start | bytes 884744 | tf_op jit(solution)/shard_map/ppermute | solution.py:84
  81.0 1.7 constant_dynamic-update-slice_fusion.6
  82.6 21.3 %all-gather.2.cloned.1.call-done = bf16[768,1152]{1,0:T(8,128)(2,1)} async-done(((bf16[32,1152]{1,0:T(8,128)(2,1)}), bf16[768,1152]{1,0:T(8,128)(2,1)}) %all-gather.2.cloned.1.call-update) | async-done | bytes 1769488 | tf_op jit(solution)/shard_map/all_gather | solution.py:142
  103.9 2.3 %collective-permute-start.9 = (bf16[128,1152]{1,0:T(8,128)(2,1)}, bf16[128,1152]{1,0:T(8,128)(2,1)S(1)}, u32[]{:S(2)}, u32[]{:S(2)}) collective-permute-start(bf16[128,1152]{1,0:T(8,128)(2,1)} %collective-permute-done.8), channel_id=1, source_target_pairs={{0,4},{4,8},{8,12},{12,16},{16,20},{20,24},{24,28},{28,0},{1,5},{5... | collective-permute-start | bytes 884744 | tf_op jit(solution)/shard_map/ppermute | solution.py:84
  106.2 1.7 constant_dynamic-update-slice_fusion.5
  108.7 1.8 copy.18
  110.4 5.2 %collective-permute-done.9 = bf16[128,1152]{1,0:T(8,128)(2,1)S(1)} collective-permute-done((bf16[128,1152]{1,0:T(8,128)(2,1)}, bf16[128,1152]{1,0:T(8,128)(2,1)S(1)}, u32[]{:S(2)}, u32[]{:S(2)}) %collective-permute-start.9) | collective-permute-done | bytes 294944 | tf_op jit(solution)/shard_map/ppermute | solution.py:84
  117.7 3.8 %fusion.6 = (f32[1056]{0:T(1024)S(1)}, f32[1056,768]{1,0:T(8,128)S(1)}) fusion(s32[768]{0:T(1024)S(1)} %add.265, s32[1056]{0:T(1024)S(1)} %pad_add_fusion, f32[]{:T(128)} %bitcast.65, bf16[1056,1152]{1,0:T(8,128)(2,1)S(1)} %bitcast_dynamic-update-slice_fusion, bf16[768,1152]{1,0:T(8,128)(2,1)S(1)} %bitcast.71, f32[]{:T(128)} %bitcast.63), kind=kOutput, calls=%fused_computation.11 | convolution fusion | flops 1878293504 | bytes 7458056 | tf_op jit(solution)/shard_map/dot_general | solution.py:59
  121.6 3.0 %fusion.11 = f32[768,1152]{1,0:T(8,128)S(1)} fusion(bf16[1056,1152]{1,0:T(8,128)(2,1)S(1)} %bitcast_dynamic-update-slice_fusion, f32[1056,768]{1,0:T(8,128)S(1)} %get-tuple-element.26, f32[]{:T(128)} %bitcast.64, s32[768]{0:T(1024)S(1)} %add.265, s32[1056]{0:T(1024)S(1)} %pad_add_fusion), kind=kOutput, calls=%fused_computation.20 | convolution fusion | flops 1875050496 | bytes 9223300 | tf_op jit(solution)/shard_map/dot_general | solution.py:74
  124.6 1.7 copy-done.2
  126.3 1.4 dynamic-slice_bitcast_fusion
  127.7 3.0 %collective-permute-start.10 = (f32[384,1152]{1,0:T(8,128)}, f32[384,1152]{1,0:T(8,128)}, u32[]{:S(2)}, u32[]{:S(2)}) collective-permute-start(f32[384,1152]{1,0:T(8,128)} %dynamic-slice_bitcast_fusion), channel_id=1, source_target_pairs={{0,32},{32,0},{1,33},{33,1},{2,34},{34,2},{3,35},{35,3},{4,36},{36... | collective-permute-start | bytes 5308424 | tf_op jit(solution)/shard_map/ppermute | solution.py:84
  131.0 3.2 %collective-permute-done.10 = f32[384,1152]{1,0:T(8,128)} collective-permute-done((f32[384,1152]{1,0:T(8,128)}, f32[384,1152]{1,0:T(8,128)}, u32[]{:S(2)}, u32[]{:S(2)}) %collective-permute-start.10) | collective-permute-done | bytes 1769504 | tf_op jit(solution)/shard_map/ppermute | solution.py:84
  134.3 2.2 %bitcast_add_fusion = f32[384,1152]{1,0:T(8,128)S(1)} fusion(f32[384,1152]{1,0:T(8,128)} %collective-permute-done.10, f32[2,384,1152]{2,1,0:T(8,128)} %bitcast.69, s32[]{:T(128)S(6)} %select_n.174), kind=kLoop, calls=%fused_computation.15 | loop fusion | flops 442368 | bytes 5308420 | tf_op jit(solution)/shard_map/add | solution.py:110
  136.5 1.2 copy-done.1
  137.7 1.1 dynamic-slice_bitcast_fusion.3
  138.8 2.1 %collective-permute-start.11 = (f32[96,1152]{1,0:T(8,128)}, f32[96,1152]{1,0:T(8,128)S(1)}, u32[]{:S(2)}, u32[]{:S(2)}) collective-permute-start(f32[96,1152]{1,0:T(8,128)} %get-tuple-element.18), channel_id=1, source_target_pairs={{0,192},{192,384},{384,576},{576,0},{1,193},{193,385},{385,577},{5... | collective-permute-start | bytes 1327112 | tf_op jit(solution)/shard_map/ppermute | solution.py:84
  140.9 4.3 %collective-permute-start.12 = (f32[96,1152]{1,0:T(8,128)}, f32[96,1152]{1,0:T(8,128)}, u32[]{:S(2)}, u32[]{:S(2)}) collective-permute-start(f32[96,1152]{1,0:T(8,128)} %get-tuple-element.20), channel_id=1, source_target_pairs={{0,384},{192,576},{384,0},{576,192},{1,385},{193,577},{385,1},{577... | collective-permute-start | bytes 1327112 | tf_op jit(solution)/shard_map/ppermute | solution.py:84
  145.3 3.1 %collective-permute-start.13 = (f32[96,1152]{1,0:T(8,128)}, f32[96,1152]{1,0:T(8,128)}, u32[]{:S(2)}, u32[]{:S(2)}) collective-permute-start(f32[96,1152]{1,0:T(8,128)} %get-tuple-element.19), channel_id=1, source_target_pairs={{0,576},{192,0},{384,192},{576,384},{1,577},{193,1},{385,193},{577... | collective-permute-start | bytes 1327112 | tf_op jit(solution)/shard_map/ppermute | solution.py:84
  149.0 4.8 %all-to-all-start.1 = ((f32[4,1,256]{2,1,0:T(1,128)}), f32[4,1,256]{2,1,0:T(1,128)S(1)}, u32[]{:S(2)}, u32[]{:S(2)}) async-start(f32[4,1,256]{2,1,0:T(1,128)} %reshape.178), calls=%async_computation.1 | async-start | bytes 8192 | tf_op jit(solution)/shard_map/all_to_all | solution.py:221
  153.8 4.8 %all-to-all-done.1 = f32[4,1,256]{2,1,0:T(1,128)S(1)} async-done(((f32[4,1,256]{2,1,0:T(1,128)}), f32[4,1,256]{2,1,0:T(1,128)S(1)}, u32[]{:S(2)}, u32[]{:S(2)}) %all-to-all-start.1) | async-done | bytes 4128 | tf_op jit(solution)/shard_map/all_to_all | solution.py:221
  160.5 2.6 %collective-permute-done.12 = f32[96,1152]{1,0:T(8,128)} collective-permute-done((f32[96,1152]{1,0:T(8,128)}, f32[96,1152]{1,0:T(8,128)}, u32[]{:S(2)}, u32[]{:S(2)}) %collective-permute-start.12) | collective-permute-done | bytes 442400 | tf_op jit(solution)/shard_map/ppermute | solution.py:84
  163.0 2.2 %collective-permute-done.13 = f32[96,1152]{1,0:T(8,128)} collective-permute-done((f32[96,1152]{1,0:T(8,128)}, f32[96,1152]{1,0:T(8,128)}, u32[]{:S(2)}, u32[]{:S(2)}) %collective-permute-start.13) | collective-permute-done | bytes 442400 | tf_op jit(solution)/shard_map/ppermute | solution.py:84
  165.3 1.5 fusion.19
  167.5 4.8 %collective-permute-start.14 = (f32[32,1152]{1,0:T(8,128)}, f32[32,1152]{1,0:T(8,128)S(1)}, u32[]{:S(2)}, u32[]{:S(2)}) collective-permute-start(f32[32,1152]{1,0:T(8,128)} %get-tuple-element.21), channel_id=1, source_target_pairs={{0,64},{64,128},{128,0},{1,65},{65,129},{129,1},{2,66},{66,130},{1... | collective-permute-start | bytes 442376 | tf_op jit(solution)/shard_map/ppermute | solution.py:84
  172.2 4.4 %collective-permute-start.15 = (f32[32,1152]{1,0:T(8,128)S(1)}, f32[32,1152]{1,0:T(8,128)}, u32[]{:S(2)}, u32[]{:S(2)}) collective-permute-start(f32[32,1152]{1,0:T(8,128)S(1)} %get-tuple-element.22), channel_id=1, source_target_pairs={{0,128},{64,0},{128,64},{1,129},{65,1},{129,65},{2,130},{66,2},{13... | collective-permute-start | bytes 442376 | tf_op jit(solution)/shard_map/ppermute | solution.py:84
  176.6 5.5 %all-to-all-start.2 = ((f32[8,1,32]{2,1,0:T(1,128)}), f32[8,1,32]{2,1,0:T(1,128)S(1)}, u32[]{:S(2)}, u32[]{:S(2)}) async-start(f32[8,1,32]{2,1,0:T(1,128)} %bitcast.17), calls=%async_computation.2 | async-start | bytes 8192 | tf_op jit(solution)/shard_map/all_to_all | solution.py:228
  182.2 6.9 %all-to-all-done.2 = f32[8,1,32]{2,1,0:T(1,128)S(1)} async-done(((f32[8,1,32]{2,1,0:T(1,128)}), f32[8,1,32]{2,1,0:T(1,128)S(1)}, u32[]{:S(2)}, u32[]{:S(2)}) %all-to-all-start.2) | async-done | bytes 1056 | tf_op jit(solution)/shard_map/all_to_all | solution.py:228
  189.7 3.2 %collective-permute-done.15 = f32[32,1152]{1,0:T(8,128)} collective-permute-done((f32[32,1152]{1,0:T(8,128)S(1)}, f32[32,1152]{1,0:T(8,128)}, u32[]{:S(2)}, u32[]{:S(2)}) %collective-permute-start.15) | collective-permute-done | bytes 147488 | tf_op jit(solution)/shard_map/ppermute | solution.py:84
  192.8 1.1 fusion.29
  (75 shorter events, 17.1 us)
Async XLA Ops:
  7.2 20.2 %copy-start = (bf16[1152,1152]{1,0:T(8,128)(2,1)S(1)}, bf16[1152,1152]{1,0:T(8,128)(2,1)}, u32[]{:S(2)}) copy-start(bf16[1152,1152]{1,0:T(8,128)(2,1)} %param.13) | copy-start | bytes 7962628
  7.2 96.8 %all-gather.2.cloned.1.call-start = ((), (), s32[]{:S(2)}) async-start(), calls=%async_computation.3 | async-start | bytes 1843200 | tf_op jit(solution)/shard_map/all_gather | solution.py:142
  10.0 35.7 %collective-permute-start.1 = (bf16[32,1152]{1,0:T(8,128)(2,1)S(1)}, bf16[32,1152]{1,0:T(8,128)(2,1)S(1)}, u32[]{:S(2)}, u32[]{:S(2)}) collective-permute-start(bf16[32,1152]{1,0:T(8,128)(2,1)S(1)} %get-tuple-element.17), channel_id=1, source_target_pairs={{0,1},{1,2},{2,3},{3,0},{4,5},{5,6},{6,7},{7,4},{8,9},{9,10},{10,1... | collective-permute-start | bytes 221192 | tf_op jit(solution)/shard_map/ppermute | solution.py:84
  14.8 34.1 %collective-permute-start = (bf16[32,1152]{1,0:T(8,128)(2,1)S(1)}, bf16[32,1152]{1,0:T(8,128)(2,1)S(1)}, u32[]{:S(2)}, u32[]{:S(2)}) collective-permute-start(bf16[32,1152]{1,0:T(8,128)(2,1)S(1)} %get-tuple-element.17), channel_id=1, source_target_pairs={{0,3},{1,0},{2,1},{3,2},{4,7},{5,4},{6,5},{7,6},{8,11},{9,8},{10,9... | collective-permute-start | bytes 221192 | tf_op jit(solution)/shard_map/ppermute | solution.py:84
  35.9 39.3 %all-to-all-start = ((bf16[32,2,576]{2,1,0:T(2,128)(2,1)}), bf16[32,2,576]{2,1,0:T(2,128)(2,1)S(1)}, u32[]{:S(2)}, u32[]{:S(2)}) async-start(bf16[32,2,576]{2,1,0:T(2,128)(2,1)} %reshape.176), calls=%async_computation | async-start | bytes 163840 | tf_op jit(solution)/shard_map/all_to_all | solution.py:164
  45.7 8.6 %collective-permute-start.2 = (bf16[32,1152]{1,0:T(8,128)(2,1)S(1)}, bf16[32,1152]{1,0:T(8,128)(2,1)S(1)}, u32[]{:S(2)}, u32[]{:S(2)}) collective-permute-start(bf16[32,1152]{1,0:T(8,128)(2,1)S(1)} %collective-permute-done.1), channel_id=1, source_target_pairs={{0,1},{1,2},{2,3},{3,0},{4,5},{5,6},{6,7},{7,4},{8,9},{9,10},{10,1... | collective-permute-start | bytes 221192 | tf_op jit(solution)/shard_map/ppermute | solution.py:84
  55.0 8.9 %collective-permute-start.6 = (bf16[128,1152]{1,0:T(8,128)(2,1)}, bf16[128,1152]{1,0:T(8,128)(2,1)S(1)}, u32[]{:S(2)}, u32[]{:S(2)}) collective-permute-start(bf16[128,1152]{1,0:T(8,128)(2,1)} %pad_maximum_fusion), channel_id=1, source_target_pairs={{0,4},{4,8},{8,12},{12,16},{16,20},{20,24},{24,28},{28,0},{1,5},{5... | collective-permute-start | bytes 884744 | tf_op jit(solution)/shard_map/ppermute | solution.py:84
  59.6 7.9 %collective-permute-start.3 = (bf16[128,1152]{1,0:T(8,128)(2,1)}, bf16[128,1152]{1,0:T(8,128)(2,1)}, u32[]{:S(2)}, u32[]{:S(2)}) collective-permute-start(bf16[128,1152]{1,0:T(8,128)(2,1)} %pad_maximum_fusion), channel_id=1, source_target_pairs={{0,28},{4,0},{8,4},{12,8},{16,12},{20,16},{24,20},{28,24},{1,29},{... | collective-permute-start | bytes 884744 | tf_op jit(solution)/shard_map/ppermute | solution.py:84
  63.9 8.8 %collective-permute-start.7 = (bf16[128,1152]{1,0:T(8,128)(2,1)S(1)}, bf16[128,1152]{1,0:T(8,128)(2,1)}, u32[]{:S(2)}, u32[]{:S(2)}) collective-permute-start(bf16[128,1152]{1,0:T(8,128)(2,1)S(1)} %collective-permute-done.6), channel_id=1, source_target_pairs={{0,4},{4,8},{8,12},{12,16},{16,20},{20,24},{24,28},{28,0},{1,5},{5... | collective-permute-start | bytes 884744 | tf_op jit(solution)/shard_map/ppermute | solution.py:84
  67.5 8.4 %collective-permute-start.4 = (bf16[128,1152]{1,0:T(8,128)(2,1)}, bf16[128,1152]{1,0:T(8,128)(2,1)}, u32[]{:S(2)}, u32[]{:S(2)}) collective-permute-start(bf16[128,1152]{1,0:T(8,128)(2,1)} %collective-permute-done.3), channel_id=1, source_target_pairs={{0,28},{4,0},{8,4},{12,8},{16,12},{20,16},{24,20},{28,24},{1,29},{... | collective-permute-start | bytes 884744 | tf_op jit(solution)/shard_map/ppermute | solution.py:84
  72.7 10.0 %collective-permute-start.8 = (bf16[128,1152]{1,0:T(8,128)(2,1)}, bf16[128,1152]{1,0:T(8,128)(2,1)}, u32[]{:S(2)}, u32[]{:S(2)}) collective-permute-start(bf16[128,1152]{1,0:T(8,128)(2,1)} %collective-permute-done.7), channel_id=1, source_target_pairs={{0,4},{4,8},{8,12},{12,16},{16,20},{20,24},{24,28},{28,0},{1,5},{5... | collective-permute-start | bytes 884744 | tf_op jit(solution)/shard_map/ppermute | solution.py:84
  75.9 32.0 %collective-permute-start.5 = (bf16[128,1152]{1,0:T(8,128)(2,1)}, bf16[128,1152]{1,0:T(8,128)(2,1)S(1)}, u32[]{:S(2)}, u32[]{:S(2)}) collective-permute-start(bf16[128,1152]{1,0:T(8,128)(2,1)} %collective-permute-done.4), channel_id=1, source_target_pairs={{0,28},{4,0},{8,4},{12,8},{16,12},{20,16},{24,20},{28,24},{1,29},{... | collective-permute-start | bytes 884744 | tf_op jit(solution)/shard_map/ppermute | solution.py:84
  103.9 11.7 %collective-permute-start.9 = (bf16[128,1152]{1,0:T(8,128)(2,1)}, bf16[128,1152]{1,0:T(8,128)(2,1)S(1)}, u32[]{:S(2)}, u32[]{:S(2)}) collective-permute-start(bf16[128,1152]{1,0:T(8,128)(2,1)} %collective-permute-done.8), channel_id=1, source_target_pairs={{0,4},{4,8},{8,12},{12,16},{16,20},{20,24},{24,28},{28,0},{1,5},{5... | collective-permute-start | bytes 884744 | tf_op jit(solution)/shard_map/ppermute | solution.py:84
  108.7 7.0 %copy-start.5 = (bf16[1056,1152]{1,0:T(8,128)(2,1)S(1)}, bf16[1056,1152]{1,0:T(8,128)(2,1)}, u32[]{:S(2)}) copy-start(bf16[1056,1152]{1,0:T(8,128)(2,1)} %constant_dynamic-update-slice_fusion.4) | copy-start | bytes 7299076
  124.5 1.8 copy-start.2
  127.7 6.6 %collective-permute-start.10 = (f32[384,1152]{1,0:T(8,128)}, f32[384,1152]{1,0:T(8,128)}, u32[]{:S(2)}, u32[]{:S(2)}) collective-permute-start(f32[384,1152]{1,0:T(8,128)} %dynamic-slice_bitcast_fusion), channel_id=1, source_target_pairs={{0,32},{32,0},{1,33},{33,1},{2,34},{34,2},{3,35},{35,3},{4,36},{36... | collective-permute-start | bytes 5308424 | tf_op jit(solution)/shard_map/ppermute | solution.py:84
  136.5 1.2 copy-start.1
  137.7 55.1 %copy-start.3 = (bf16[32,1152]{1,0:T(8,128)(2,1)S(1)}, bf16[32,1152]{1,0:T(8,128)(2,1)}, u32[]{:S(2)}) copy-start(bf16[32,1152]{1,0:T(8,128)(2,1)} %param.16) | copy-start | bytes 221188
  138.8 21.7 %collective-permute-start.11 = (f32[96,1152]{1,0:T(8,128)}, f32[96,1152]{1,0:T(8,128)S(1)}, u32[]{:S(2)}, u32[]{:S(2)}) collective-permute-start(f32[96,1152]{1,0:T(8,128)} %get-tuple-element.18), channel_id=1, source_target_pairs={{0,192},{192,384},{384,576},{576,0},{1,193},{193,385},{385,577},{5... | collective-permute-start | bytes 1327112 | tf_op jit(solution)/shard_map/ppermute | solution.py:84
  140.9 22.1 %collective-permute-start.12 = (f32[96,1152]{1,0:T(8,128)}, f32[96,1152]{1,0:T(8,128)}, u32[]{:S(2)}, u32[]{:S(2)}) collective-permute-start(f32[96,1152]{1,0:T(8,128)} %get-tuple-element.20), channel_id=1, source_target_pairs={{0,384},{192,576},{384,0},{576,192},{1,385},{193,577},{385,1},{577... | collective-permute-start | bytes 1327112 | tf_op jit(solution)/shard_map/ppermute | solution.py:84
  145.3 20.0 %collective-permute-start.13 = (f32[96,1152]{1,0:T(8,128)}, f32[96,1152]{1,0:T(8,128)}, u32[]{:S(2)}, u32[]{:S(2)}) collective-permute-start(f32[96,1152]{1,0:T(8,128)} %get-tuple-element.19), channel_id=1, source_target_pairs={{0,576},{192,0},{384,192},{576,384},{1,577},{193,1},{385,193},{577... | collective-permute-start | bytes 1327112 | tf_op jit(solution)/shard_map/ppermute | solution.py:84
  149.0 9.6 %all-to-all-start.1 = ((f32[4,1,256]{2,1,0:T(1,128)}), f32[4,1,256]{2,1,0:T(1,128)S(1)}, u32[]{:S(2)}, u32[]{:S(2)}) async-start(f32[4,1,256]{2,1,0:T(1,128)} %reshape.178), calls=%async_computation.1 | async-start | bytes 8192 | tf_op jit(solution)/shard_map/all_to_all | solution.py:221
  160.5 2.6 %copy-start.4 = (f32[96,1152]{1,0:T(8,128)}, f32[96,1152]{1,0:T(8,128)S(1)}, u32[]{:S(2)}) copy-start(f32[96,1152]{1,0:T(8,128)S(1)} %collective-permute-done.11) | copy-start | bytes 1327108
  167.5 22.2 %collective-permute-start.14 = (f32[32,1152]{1,0:T(8,128)}, f32[32,1152]{1,0:T(8,128)S(1)}, u32[]{:S(2)}, u32[]{:S(2)}) collective-permute-start(f32[32,1152]{1,0:T(8,128)} %get-tuple-element.21), channel_id=1, source_target_pairs={{0,64},{64,128},{128,0},{1,65},{65,129},{129,1},{2,66},{66,130},{1... | collective-permute-start | bytes 442376 | tf_op jit(solution)/shard_map/ppermute | solution.py:84
  172.2 20.6 %collective-permute-start.15 = (f32[32,1152]{1,0:T(8,128)S(1)}, f32[32,1152]{1,0:T(8,128)}, u32[]{:S(2)}, u32[]{:S(2)}) collective-permute-start(f32[32,1152]{1,0:T(8,128)S(1)} %get-tuple-element.22), channel_id=1, source_target_pairs={{0,128},{64,0},{128,64},{1,129},{65,1},{129,65},{2,130},{66,2},{13... | collective-permute-start | bytes 442376 | tf_op jit(solution)/shard_map/ppermute | solution.py:84
  176.6 12.5 %all-to-all-start.2 = ((f32[8,1,32]{2,1,0:T(1,128)}), f32[8,1,32]{2,1,0:T(1,128)S(1)}, u32[]{:S(2)}, u32[]{:S(2)}) async-start(f32[8,1,32]{2,1,0:T(1,128)} %bitcast.17), calls=%async_computation.2 | async-start | bytes 8192 | tf_op jit(solution)/shard_map/all_to_all | solution.py:228
Sparse Core Ops, SparseCore 0:
  23.1 80.7 all-gather.1

commit v7 on v6

--- a/solution.py
+++ b/solution.py
@@ -138,8 +138,7 @@
     starting_position = score_shift[0]
 
     text_unit, text_inverse = normalize_rows(caption_features)
-    caption_magnitude = text_unit.astype(jnp.bfloat16)
-    device_portion_count = lax.all_gather(caption_magnitude, ("x", "zh", "core"), axis=0, tiled=True)
+    device_portion_count = lax.all_gather(caption_features, ("x", "zh", "core"), axis=0, tiled=True)
 
     chunk_rows = row_count
     prior_norm = normalize_rows(
@@ -200,6 +199,7 @@
         + jnp.arange(row_count, dtype=jnp.int32)[None, :]
     ).reshape(-1)
 
+    device_portion_count = normalize_rows(device_portion_count)[0].astype(jnp.bfloat16)
     row_losses, grad_terms = block_contributions(
         picture_tile,
         target_tile,

time: 203 us -> 207 us (1.020)
  the two profiles are of different devices: /device:TPU:1 before, /device:TPU:14 now
where the time goes in v7:
time: 207 us; the launch traced here: 206 us
  starting transfers between devices  77.8 us (38%)
  waiting for transfers between devices  58.9 us (28%)
  local copies, waits for them, and re-layouts  20.1 us (10%)
  other arithmetic  16.9 us (8%)
  between operations  16.6 us (8%)
  matrix products  15.4 us (7%)
    ppermute x16, starting transfers between devices, shift_ring(): return lax.ppermute(x, axis, [(i, (i + step) % size) for i in range(size)])  55.1 us
    ppermute x16, waiting for transfers between devices, shift_ring(): return lax.ppermute(x, axis, [(i, (i + step) % size) for i in range(size)])  41.1 us
    all_gather x1, waiting for transfers between devices, local(): lax.all_gather(caption_features, ('x', 'zh', 'core'), axis=0, tiled=True)  12.4 us
    unnamed x28, local copies, waits for them, and re-layouts  11.7 us
    all_to_all x1, starting transfers between devices, local(): lax.all_to_all(jnp.broadcast_to(pooled_norm, (inner_size, pooled_norm.sha...  9.15 us
    all_to_all x1, starting transfers between devices, local(): lax.all_to_all(section_losses, 'section', 0, 0, tiled=True)  8.48 us
    all_to_all x1, waiting for transfers between devices, local(): lax.all_to_all(loss_parts.reshape(section_size, mp_size, row_count), 'mp'...  5.41 us
    all_to_all x1, starting transfers between devices, local(): lax.all_to_all(loss_parts.reshape(section_size, mp_size, row_count), 'mp'...  5.05 us
  transfers between devices with their start and end apart: 20, of which 11 were waited for; matrix products, arithmetic and copies ran while one was open for 13% of the time, Pallas kernels for 0%

profile of v7, /device:TPU:14, one launch (start us, length us, event | category | flops | bytes accessed | tf_op | source)
XLA Modules:
  0.0 205.8 jit_solution(17945547603181253124)
XLA Ops:
  7.2 1.2 fusion.30
  8.4 1.6 constant_dynamic-update-slice_fusion.10
  10.0 4.3 %collective-permute-start.1 = (bf16[32,1152]{1,0:T(8,128)(2,1)S(1)}, bf16[32,1152]{1,0:T(8,128)(2,1)S(1)}, u32[]{:S(2)}, u32[]{:S(2)}) collective-permute-start(bf16[32,1152]{1,0:T(8,128)(2,1)S(1)} %get-tuple-element.17), channel_id=1, source_target_pairs={{0,1},{1,2},{2,3},{3,0},{4,5},{5,6},{6,7},{7,4},{8,9},{9,10},{10,1... | collective-permute-start | bytes 221192 | tf_op jit(solution)/shard_map/ppermute | solution.py:84
  14.3 5.5 %collective-permute-start = (bf16[32,1152]{1,0:T(8,128)(2,1)S(1)}, bf16[32,1152]{1,0:T(8,128)(2,1)S(1)}, u32[]{:S(2)}, u32[]{:S(2)}) collective-permute-start(bf16[32,1152]{1,0:T(8,128)(2,1)S(1)} %get-tuple-element.17), channel_id=1, source_target_pairs={{0,3},{1,0},{2,1},{3,2},{4,7},{5,4},{6,5},{7,6},{8,11},{9,8},{10,9... | collective-permute-start | bytes 221192 | tf_op jit(solution)/shard_map/ppermute | solution.py:84
  19.9 4.1 %fusion.68 = (f32[16]{0:T(128)S(1)}, f32[16,729]{1,0:T(8,128)S(1)}) fusion(bf16[1,729,1152]{2,1,0:T(8,128)(2,1)} %param.10, bf16[1152,1152]{1,0:T(8,128)(2,1)} %param.12, s32[1152]{0:T(1024)S(1)} %add_select_fusion, bf16[1152]{0:T(1024)(128)(2,1)} %param.11), kind=kOutput, calls=%fused_computation.129 | convolution fusion | flops 69426560 | bytes 4387456 | tf_op jit(solution)/shard_map/dot_general | solution.py:24
  24.2 2.2 %fusion.16 = f32[16,1152]{1,0:T(8,128)S(1)} fusion(bf16[1152,1152]{1,0:T(8,128)(2,1)S(1)} %copy-done, bf16[1,729,1152]{2,1,0:T(8,128)(2,1)} %param.10, f32[16,729]{1,0:T(8,128)S(1)} %get-tuple-element.24, f32[16]{0:T(128)S(1)} %fusion.38, f32[16]{0:T(128)S(1)} %get-tuple-element.23), kind=kOutput, calls=%fused_computation.25 | convolution fusion | flops 69394608 | bytes 4454336 | tf_op jit(solution)/shard_map/dot_general | solution.py:31
  26.8 2.2 %convolution_reduce_fusion = bf16[1152]{0:T(1024)(128)(2,1)S(1)} fusion(bf16[1152,1]{0,1:T(2,128)(2,1)S(1)} %reshape.190, bf16[1152,1152]{1,0:T(8,128)(2,1)} %param.14), kind=kOutput, calls=%fused_computation.26 | convolution fusion | flops 2654208 | bytes 2658816 | tf_op jit(solution)/shard_map/dot_general | solution.py:38
  32.8 9.2 %all-to-all-start = ((bf16[32,2,576]{2,1,0:T(2,128)(2,1)}), bf16[32,2,576]{2,1,0:T(2,128)(2,1)S(1)}, u32[]{:S(2)}, u32[]{:S(2)}) async-start(bf16[32,2,576]{2,1,0:T(2,128)(2,1)} %reshape.195), calls=%async_computation | async-start | bytes 163840 | tf_op jit(solution)/shard_map/all_to_all | solution.py:163
  44.6 3.4 %collective-permute-start.2 = (bf16[32,1152]{1,0:T(8,128)(2,1)S(1)}, bf16[32,1152]{1,0:T(8,128)(2,1)S(1)}, u32[]{:S(2)}, u32[]{:S(2)}) collective-permute-start(bf16[32,1152]{1,0:T(8,128)(2,1)S(1)} %collective-permute-done.1), channel_id=1, source_target_pairs={{0,1},{1,2},{2,3},{3,0},{4,5},{5,6},{6,7},{7,4},{8,9},{9,10},{10,1... | collective-permute-start | bytes 221192 | tf_op jit(solution)/shard_map/ppermute | solution.py:84
  48.2 4.5 %collective-permute-done.2 = bf16[32,1152]{1,0:T(8,128)(2,1)S(1)} collective-permute-done((bf16[32,1152]{1,0:T(8,128)(2,1)S(1)}, bf16[32,1152]{1,0:T(8,128)(2,1)S(1)}, u32[]{:S(2)}, u32[]{:S(2)}) %collective-permute-start.2) | collective-permute-done | bytes 73760 | tf_op jit(solution)/shard_map/ppermute | solution.py:84
  52.8 2.2 %collective-permute-start.3 = (bf16[128,1152]{1,0:T(8,128)(2,1)S(1)}, bf16[128,1152]{1,0:T(8,128)(2,1)}, u32[]{:S(2)}, u32[]{:S(2)}) collective-permute-start(bf16[128,1152]{1,0:T(8,128)(2,1)S(1)} %pad_maximum_fusion), channel_id=1, source_target_pairs={{0,28},{4,0},{8,4},{12,8},{16,12},{20,16},{24,20},{28,24},{1,29},{... | collective-permute-start | bytes 884744 | tf_op jit(solution)/shard_map/ppermute | solution.py:84
  55.0 3.7 %collective-permute-start.6 = (bf16[128,1152]{1,0:T(8,128)(2,1)S(1)}, bf16[128,1152]{1,0:T(8,128)(2,1)S(1)}, u32[]{:S(2)}, u32[]{:S(2)}) collective-permute-start(bf16[128,1152]{1,0:T(8,128)(2,1)S(1)} %pad_maximum_fusion), channel_id=1, source_target_pairs={{0,4},{4,8},{8,12},{12,16},{16,20},{20,24},{24,28},{28,0},{1,5},{5... | collective-permute-start | bytes 884744 | tf_op jit(solution)/shard_map/ppermute | solution.py:84
  59.3 2.6 %collective-permute-done.3 = bf16[128,1152]{1,0:T(8,128)(2,1)} collective-permute-done((bf16[128,1152]{1,0:T(8,128)(2,1)S(1)}, bf16[128,1152]{1,0:T(8,128)(2,1)}, u32[]{:S(2)}, u32[]{:S(2)}) %collective-permute-start.3) | collective-permute-done | bytes 294944 | tf_op jit(solution)/shard_map/ppermute | solution.py:84
  61.9 2.4 %collective-permute-start.4 = (bf16[128,1152]{1,0:T(8,128)(2,1)}, bf16[128,1152]{1,0:T(8,128)(2,1)}, u32[]{:S(2)}, u32[]{:S(2)}) collective-permute-start(bf16[128,1152]{1,0:T(8,128)(2,1)} %collective-permute-done.3), channel_id=1, source_target_pairs={{0,28},{4,0},{8,4},{12,8},{16,12},{20,16},{24,20},{28,24},{1,29},{... | collective-permute-start | bytes 884744 | tf_op jit(solution)/shard_map/ppermute | solution.py:84
  65.0 3.4 %collective-permute-start.7 = (bf16[128,1152]{1,0:T(8,128)(2,1)S(1)}, bf16[128,1152]{1,0:T(8,128)(2,1)}, u32[]{:S(2)}, u32[]{:S(2)}) collective-permute-start(bf16[128,1152]{1,0:T(8,128)(2,1)S(1)} %collective-permute-done.6), channel_id=1, source_target_pairs={{0,4},{4,8},{8,12},{12,16},{16,20},{20,24},{24,28},{28,0},{1,5},{5... | collective-permute-start | bytes 884744 | tf_op jit(solution)/shard_map/ppermute | solution.py:84
  69.2 1.7 collective-permute-done.4
  70.8 3.6 %collective-permute-start.5 = (bf16[128,1152]{1,0:T(8,128)(2,1)}, bf16[128,1152]{1,0:T(8,128)(2,1)S(1)}, u32[]{:S(2)}, u32[]{:S(2)}) collective-permute-start(bf16[128,1152]{1,0:T(8,128)(2,1)} %collective-permute-done.4), channel_id=1, source_target_pairs={{0,28},{4,0},{8,4},{12,8},{16,12},{20,16},{24,20},{28,24},{1,29},{... | collective-permute-start | bytes 884744 | tf_op jit(solution)/shard_map/ppermute | solution.py:84
  74.5 1.7 constant_dynamic-update-slice_fusion.6
  76.2 2.2 %collective-permute-start.8 = (bf16[128,1152]{1,0:T(8,128)(2,1)}, bf16[128,1152]{1,0:T(8,128)(2,1)S(1)}, u32[]{:S(2)}, u32[]{:S(2)}) collective-permute-start(bf16[128,1152]{1,0:T(8,128)(2,1)} %collective-permute-done.7), channel_id=1, source_target_pairs={{0,4},{4,8},{8,12},{12,16},{16,20},{20,24},{24,28},{28,0},{1,5},{5... | collective-permute-start | bytes 884744 | tf_op jit(solution)/shard_map/ppermute | solution.py:84
  78.4 1.7 constant_dynamic-update-slice_fusion.5
  80.8 5.9 %collective-permute-done.8 = bf16[128,1152]{1,0:T(8,128)(2,1)S(1)} collective-permute-done((bf16[128,1152]{1,0:T(8,128)(2,1)}, bf16[128,1152]{1,0:T(8,128)(2,1)S(1)}, u32[]{:S(2)}, u32[]{:S(2)}) %collective-permute-start.8) | collective-permute-done | bytes 294944 | tf_op jit(solution)/shard_map/ppermute | solution.py:84
  86.7 12.4 %all-gather.2.cloned.1.call-done = bf16[768,1152]{1,0:T(8,128)(2,1)} async-done(((bf16[32,1152]{1,0:T(8,128)(2,1)}), bf16[768,1152]{1,0:T(8,128)(2,1)}) %all-gather.2.cloned.1.call-update) | async-done | bytes 1769488 | tf_op jit(solution)/shard_map/all_gather | solution.py:141
  99.1 2.0 multiply_reduce_fusion
  101.1 2.0 convert_element_type.97
  103.3 3.6 %collective-permute-start.9 = (bf16[128,1152]{1,0:T(8,128)(2,1)S(1)}, bf16[128,1152]{1,0:T(8,128)(2,1)S(1)}, u32[]{:S(2)}, u32[]{:S(2)}) collective-permute-start(bf16[128,1152]{1,0:T(8,128)(2,1)S(1)} %collective-permute-done.8), channel_id=1, source_target_pairs={{0,4},{4,8},{8,12},{12,16},{16,20},{20,24},{24,28},{28,0},{1,5},{5... | collective-permute-start | bytes 884744 | tf_op jit(solution)/shard_map/ppermute | solution.py:84
  106.8 2.2 %copy.20 = f32[2,4,3,32,1152]{4,3,2,1,0:T(8,128)S(1)} copy(f32[2,4,3,32,1152]{4,3,0,2,1:T(8,128)} %bitcast.70) | data formatting | bytes 7077888 | tf_op jit(solution)/shard_map/convert_element_type | solution.py:44
  109.4 5.0 %collective-permute-done.9 = bf16[128,1152]{1,0:T(8,128)(2,1)S(1)} collective-permute-done((bf16[128,1152]{1,0:T(8,128)(2,1)S(1)}, bf16[128,1152]{1,0:T(8,128)(2,1)S(1)}, u32[]{:S(2)}, u32[]{:S(2)}) %collective-permute-start.9) | collective-permute-done | bytes 294944 | tf_op jit(solution)/shard_map/ppermute | solution.py:84
  115.5 3.9 %fusion.7 = (f32[1056]{0:T(1024)S(1)}, f32[1056,768]{1,0:T(8,128)S(1)}) fusion(s32[768]{0:T(1024)S(1)} %add.280, s32[1056]{0:T(1024)S(1)} %pad_add_fusion, f32[]{:T(128)} %bitcast.69, bf16[1056,1152]{1,0:T(8,128)(2,1)S(1)} %bitcast_dynamic-update-slice_fusion, bf16[768,1152]{1,0:T(8,128)(2,1)S(1)} %fusion.1, f32[]{:T(128)} %bitcast.67), kind=kOutput, calls=%fused_computation.14 | convolution fusion | flops 1878293504 | bytes 7458056 | tf_op jit(solution)/shard_map/dot_general | solution.py:59
  119.3 3.0 %fusion.12 = f32[768,1152]{1,0:T(8,128)S(1)} fusion(bf16[1056,1152]{1,0:T(8,128)(2,1)S(1)} %bitcast_dynamic-update-slice_fusion, f32[1056,768]{1,0:T(8,128)S(1)} %get-tuple-element.26, f32[]{:T(128)} %bitcast.68, s32[768]{0:T(1024)S(1)} %add.280, s32[1056]{0:T(1024)S(1)} %pad_add_fusion), kind=kOutput, calls=%fused_computation.23 | convolution fusion | flops 1875050496 | bytes 9223300 | tf_op jit(solution)/shard_map/dot_general | solution.py:74
  122.4 1.7 copy-done.3
  124.1 1.4 dynamic-slice_bitcast_fusion
  125.5 1.9 collective-permute-start.10
  127.8 3.6 %collective-permute-done.10 = f32[384,1152]{1,0:T(8,128)} collective-permute-done((f32[384,1152]{1,0:T(8,128)}, f32[384,1152]{1,0:T(8,128)}, u32[]{:S(2)}, u32[]{:S(2)}) %collective-permute-start.10) | collective-permute-done | bytes 1769504 | tf_op jit(solution)/shard_map/ppermute | solution.py:84
  131.4 2.2 %bitcast_add_fusion = f32[384,1152]{1,0:T(8,128)S(1)} fusion(f32[384,1152]{1,0:T(8,128)} %collective-permute-done.10, f32[2,384,1152]{2,1,0:T(8,128)} %bitcast.74, s32[]{:T(128)S(6)} %select_n.174), kind=kLoop, calls=%fused_computation.18 | loop fusion | flops 442368 | bytes 5308420 | tf_op jit(solution)/shard_map/add | solution.py:110
  133.6 1.2 copy-done.1
  135.9 2.5 %collective-permute-start.11 = (f32[96,1152]{1,0:T(8,128)}, f32[96,1152]{1,0:T(8,128)S(1)}, u32[]{:S(2)}, u32[]{:S(2)}) collective-permute-start(f32[96,1152]{1,0:T(8,128)} %get-tuple-element.18), channel_id=1, source_target_pairs={{0,192},{192,384},{384,576},{576,0},{1,193},{193,385},{385,577},{5... | collective-permute-start | bytes 1327112 | tf_op jit(solution)/shard_map/ppermute | solution.py:84
  138.4 3.4 %collective-permute-start.13 = (f32[96,1152]{1,0:T(8,128)}, f32[96,1152]{1,0:T(8,128)}, u32[]{:S(2)}, u32[]{:S(2)}) collective-permute-start(f32[96,1152]{1,0:T(8,128)} %get-tuple-element.19), channel_id=1, source_target_pairs={{0,576},{192,0},{384,192},{576,384},{1,577},{193,1},{385,193},{577... | collective-permute-start | bytes 1327112 | tf_op jit(solution)/shard_map/ppermute | solution.py:84
  141.8 3.4 %collective-permute-start.12 = (f32[96,1152]{1,0:T(8,128)}, f32[96,1152]{1,0:T(8,128)}, u32[]{:S(2)}, u32[]{:S(2)}) collective-permute-start(f32[96,1152]{1,0:T(8,128)} %get-tuple-element.20), channel_id=1, source_target_pairs={{0,384},{192,576},{384,0},{576,192},{1,385},{193,577},{385,1},{577... | collective-permute-start | bytes 1327112 | tf_op jit(solution)/shard_map/ppermute | solution.py:84
  145.8 5.0 %all-to-all-start.1 = ((f32[4,1,256]{2,1,0:T(1,128)}), f32[4,1,256]{2,1,0:T(1,128)S(1)}, u32[]{:S(2)}, u32[]{:S(2)}) async-start(f32[4,1,256]{2,1,0:T(1,128)} %reshape.197), calls=%async_computation.1 | async-start | bytes 8192 | tf_op jit(solution)/shard_map/all_to_all | solution.py:221
  151.0 5.4 %all-to-all-done.1 = f32[4,1,256]{2,1,0:T(1,128)S(1)} async-done(((f32[4,1,256]{2,1,0:T(1,128)}), f32[4,1,256]{2,1,0:T(1,128)S(1)}, u32[]{:S(2)}, u32[]{:S(2)}) %all-to-all-start.1) | async-done | bytes 4128 | tf_op jit(solution)/shard_map/all_to_all | solution.py:221
  158.3 4.9 %collective-permute-done.13 = f32[96,1152]{1,0:T(8,128)} collective-permute-done((f32[96,1152]{1,0:T(8,128)}, f32[96,1152]{1,0:T(8,128)}, u32[]{:S(2)}, u32[]{:S(2)}) %collective-permute-start.13) | collective-permute-done | bytes 442400 | tf_op jit(solution)/shard_map/ppermute | solution.py:84
  163.2 1.5 fusion.20
  164.7 8.5 %all-to-all-start.2 = ((f32[8,1,32]{2,1,0:T(1,128)}), f32[8,1,32]{2,1,0:T(1,128)S(1)}, u32[]{:S(2)}, u32[]{:S(2)}) async-start(f32[8,1,32]{2,1,0:T(1,128)} %bitcast.18), calls=%async_computation.2 | async-start | bytes 8192 | tf_op jit(solution)/shard_map/all_to_all | solution.py:228
  173.9 6.0 %collective-permute-start.14 = (f32[32,1152]{1,0:T(8,128)}, f32[32,1152]{1,0:T(8,128)S(1)}, u32[]{:S(2)}, u32[]{:S(2)}) collective-permute-start(f32[32,1152]{1,0:T(8,128)} %get-tuple-element.21), channel_id=1, source_target_pairs={{0,64},{64,128},{128,0},{1,65},{65,129},{129,1},{2,66},{66,130},{1... | collective-permute-start | bytes 442376 | tf_op jit(solution)/shard_map/ppermute | solution.py:84
  179.9 3.7 %collective-permute-start.15 = (f32[32,1152]{1,0:T(8,128)S(1)}, f32[32,1152]{1,0:T(8,128)}, u32[]{:S(2)}, u32[]{:S(2)}) collective-permute-start(f32[32,1152]{1,0:T(8,128)S(1)} %get-tuple-element.22), channel_id=1, source_target_pairs={{0,128},{64,0},{128,64},{1,129},{65,1},{129,65},{2,130},{66,2},{13... | collective-permute-start | bytes 442376 | tf_op jit(solution)/shard_map/ppermute | solution.py:84
  184.2 8.0 %collective-permute-done.14 = f32[32,1152]{1,0:T(8,128)S(1)} collective-permute-done((f32[32,1152]{1,0:T(8,128)}, f32[32,1152]{1,0:T(8,128)S(1)}, u32[]{:S(2)}, u32[]{:S(2)}) %collective-permute-start.14) | collective-permute-done | bytes 147488 | tf_op jit(solution)/shard_map/ppermute | solution.py:84
  192.2 4.8 %collective-permute-done.15 = f32[32,1152]{1,0:T(8,128)} collective-permute-done((f32[32,1152]{1,0:T(8,128)S(1)}, f32[32,1152]{1,0:T(8,128)}, u32[]{:S(2)}, u32[]{:S(2)}) %collective-permute-start.15) | collective-permute-done | bytes 147488 | tf_op jit(solution)/shard_map/ppermute | solution.py:84
  197.0 1.1 fusion.27
  (83 shorter events, 15.6 us)
Async XLA Ops:
  7.2 17.1 %copy-start = (bf16[1152,1152]{1,0:T(8,128)(2,1)S(1)}, bf16[1152,1152]{1,0:T(8,128)(2,1)}, u32[]{:S(2)}) copy-start(bf16[1152,1152]{1,0:T(8,128)(2,1)} %param.13) | copy-start | bytes 7962628
  7.2 91.9 %all-gather.2.cloned.1.call-start = ((), (), s32[]{:S(2)}) async-start(), calls=%async_computation.3 | async-start | bytes 1843200 | tf_op jit(solution)/shard_map/all_gather | solution.py:141
  10.0 34.6 %collective-permute-start.1 = (bf16[32,1152]{1,0:T(8,128)(2,1)S(1)}, bf16[32,1152]{1,0:T(8,128)(2,1)S(1)}, u32[]{:S(2)}, u32[]{:S(2)}) collective-permute-start(bf16[32,1152]{1,0:T(8,128)(2,1)S(1)} %get-tuple-element.17), channel_id=1, source_target_pairs={{0,1},{1,2},{2,3},{3,0},{4,5},{5,6},{6,7},{7,4},{8,9},{9,10},{10,1... | collective-permute-start | bytes 221192 | tf_op jit(solution)/shard_map/ppermute | solution.py:84
  14.3 33.9 %collective-permute-start = (bf16[32,1152]{1,0:T(8,128)(2,1)S(1)}, bf16[32,1152]{1,0:T(8,128)(2,1)S(1)}, u32[]{:S(2)}, u32[]{:S(2)}) collective-permute-start(bf16[32,1152]{1,0:T(8,128)(2,1)S(1)} %get-tuple-element.17), channel_id=1, source_target_pairs={{0,3},{1,0},{2,1},{3,2},{4,7},{5,4},{6,5},{7,6},{8,11},{9,8},{10,9... | collective-permute-start | bytes 221192 | tf_op jit(solution)/shard_map/ppermute | solution.py:84
  32.8 36.2 %all-to-all-start = ((bf16[32,2,576]{2,1,0:T(2,128)(2,1)}), bf16[32,2,576]{2,1,0:T(2,128)(2,1)S(1)}, u32[]{:S(2)}, u32[]{:S(2)}) async-start(bf16[32,2,576]{2,1,0:T(2,128)(2,1)} %reshape.195), calls=%async_computation | async-start | bytes 163840 | tf_op jit(solution)/shard_map/all_to_all | solution.py:163
  44.6 8.1 %collective-permute-start.2 = (bf16[32,1152]{1,0:T(8,128)(2,1)S(1)}, bf16[32,1152]{1,0:T(8,128)(2,1)S(1)}, u32[]{:S(2)}, u32[]{:S(2)}) collective-permute-start(bf16[32,1152]{1,0:T(8,128)(2,1)S(1)} %collective-permute-done.1), channel_id=1, source_target_pairs={{0,1},{1,2},{2,3},{3,0},{4,5},{5,6},{6,7},{7,4},{8,9},{9,10},{10,1... | collective-permute-start | bytes 221192 | tf_op jit(solution)/shard_map/ppermute | solution.py:84
  52.8 9.1 %collective-permute-start.3 = (bf16[128,1152]{1,0:T(8,128)(2,1)S(1)}, bf16[128,1152]{1,0:T(8,128)(2,1)}, u32[]{:S(2)}, u32[]{:S(2)}) collective-permute-start(bf16[128,1152]{1,0:T(8,128)(2,1)S(1)} %pad_maximum_fusion), channel_id=1, source_target_pairs={{0,28},{4,0},{8,4},{12,8},{16,12},{20,16},{24,20},{28,24},{1,29},{... | collective-permute-start | bytes 884744 | tf_op jit(solution)/shard_map/ppermute | solution.py:84
  55.0 10.0 %collective-permute-start.6 = (bf16[128,1152]{1,0:T(8,128)(2,1)S(1)}, bf16[128,1152]{1,0:T(8,128)(2,1)S(1)}, u32[]{:S(2)}, u32[]{:S(2)}) collective-permute-start(bf16[128,1152]{1,0:T(8,128)(2,1)S(1)} %pad_maximum_fusion), channel_id=1, source_target_pairs={{0,4},{4,8},{8,12},{12,16},{16,20},{20,24},{24,28},{28,0},{1,5},{5... | collective-permute-start | bytes 884744 | tf_op jit(solution)/shard_map/ppermute | solution.py:84
  61.9 8.9 %collective-permute-start.4 = (bf16[128,1152]{1,0:T(8,128)(2,1)}, bf16[128,1152]{1,0:T(8,128)(2,1)}, u32[]{:S(2)}, u32[]{:S(2)}) collective-permute-start(bf16[128,1152]{1,0:T(8,128)(2,1)} %collective-permute-done.3), channel_id=1, source_target_pairs={{0,28},{4,0},{8,4},{12,8},{16,12},{20,16},{24,20},{28,24},{1,29},{... | collective-permute-start | bytes 884744 | tf_op jit(solution)/shard_map/ppermute | solution.py:84
  65.0 11.2 %collective-permute-start.7 = (bf16[128,1152]{1,0:T(8,128)(2,1)S(1)}, bf16[128,1152]{1,0:T(8,128)(2,1)}, u32[]{:S(2)}, u32[]{:S(2)}) collective-permute-start(bf16[128,1152]{1,0:T(8,128)(2,1)S(1)} %collective-permute-done.6), channel_id=1, source_target_pairs={{0,4},{4,8},{8,12},{12,16},{16,20},{20,24},{24,28},{28,0},{1,5},{5... | collective-permute-start | bytes 884744 | tf_op jit(solution)/shard_map/ppermute | solution.py:84
  70.8 9.2 %collective-permute-start.5 = (bf16[128,1152]{1,0:T(8,128)(2,1)}, bf16[128,1152]{1,0:T(8,128)(2,1)S(1)}, u32[]{:S(2)}, u32[]{:S(2)}) collective-permute-start(bf16[128,1152]{1,0:T(8,128)(2,1)} %collective-permute-done.4), channel_id=1, source_target_pairs={{0,28},{4,0},{8,4},{12,8},{16,12},{20,16},{24,20},{28,24},{1,29},{... | collective-permute-start | bytes 884744 | tf_op jit(solution)/shard_map/ppermute | solution.py:84
  76.2 10.5 %collective-permute-start.8 = (bf16[128,1152]{1,0:T(8,128)(2,1)}, bf16[128,1152]{1,0:T(8,128)(2,1)S(1)}, u32[]{:S(2)}, u32[]{:S(2)}) collective-permute-start(bf16[128,1152]{1,0:T(8,128)(2,1)} %collective-permute-done.7), channel_id=1, source_target_pairs={{0,4},{4,8},{8,12},{12,16},{16,20},{20,24},{24,28},{28,0},{1,5},{5... | collective-permute-start | bytes 884744 | tf_op jit(solution)/shard_map/ppermute | solution.py:84
  99.1 2.0 copy-start.2
  103.3 11.1 %collective-permute-start.9 = (bf16[128,1152]{1,0:T(8,128)(2,1)S(1)}, bf16[128,1152]{1,0:T(8,128)(2,1)S(1)}, u32[]{:S(2)}, u32[]{:S(2)}) collective-permute-start(bf16[128,1152]{1,0:T(8,128)(2,1)S(1)} %collective-permute-done.8), channel_id=1, source_target_pairs={{0,4},{4,8},{8,12},{12,16},{16,20},{20,24},{24,28},{28,0},{1,5},{5... | collective-permute-start | bytes 884744 | tf_op jit(solution)/shard_map/ppermute | solution.py:84
  109.1 5.3 %copy-start.6 = (bf16[1056,1152]{1,0:T(8,128)(2,1)S(1)}, bf16[1056,1152]{1,0:T(8,128)(2,1)}, u32[]{:S(2)}) copy-start(bf16[1056,1152]{1,0:T(8,128)(2,1)} %constant_dynamic-update-slice_fusion.4) | copy-start | bytes 7299076
  122.4 1.8 copy-start.3
  125.5 5.9 %collective-permute-start.10 = (f32[384,1152]{1,0:T(8,128)}, f32[384,1152]{1,0:T(8,128)}, u32[]{:S(2)}, u32[]{:S(2)}) collective-permute-start(f32[384,1152]{1,0:T(8,128)} %dynamic-slice_bitcast_fusion), channel_id=1, source_target_pairs={{0,32},{32,0},{1,33},{33,1},{2,34},{34,2},{3,35},{35,3},{4,36},{36... | collective-permute-start | bytes 5308424 | tf_op jit(solution)/shard_map/ppermute | solution.py:84
  133.6 1.2 copy-start.1
  133.6 17.3 %copy-start.4 = (bf16[32,1152]{1,0:T(8,128)(2,1)S(1)}, bf16[32,1152]{1,0:T(8,128)(2,1)}, u32[]{:S(2)}) copy-start(bf16[32,1152]{1,0:T(8,128)(2,1)} %param.16) | copy-start | bytes 221188
  135.9 22.4 %collective-permute-start.11 = (f32[96,1152]{1,0:T(8,128)}, f32[96,1152]{1,0:T(8,128)S(1)}, u32[]{:S(2)}, u32[]{:S(2)}) collective-permute-start(f32[96,1152]{1,0:T(8,128)} %get-tuple-element.18), channel_id=1, source_target_pairs={{0,192},{192,384},{384,576},{576,0},{1,193},{193,385},{385,577},{5... | collective-permute-start | bytes 1327112 | tf_op jit(solution)/shard_map/ppermute | solution.py:84
  138.4 24.8 %collective-permute-start.13 = (f32[96,1152]{1,0:T(8,128)}, f32[96,1152]{1,0:T(8,128)}, u32[]{:S(2)}, u32[]{:S(2)}) collective-permute-start(f32[96,1152]{1,0:T(8,128)} %get-tuple-element.19), channel_id=1, source_target_pairs={{0,576},{192,0},{384,192},{576,384},{1,577},{193,1},{385,193},{577... | collective-permute-start | bytes 1327112 | tf_op jit(solution)/shard_map/ppermute | solution.py:84
  141.8 21.5 %collective-permute-start.12 = (f32[96,1152]{1,0:T(8,128)}, f32[96,1152]{1,0:T(8,128)}, u32[]{:S(2)}, u32[]{:S(2)}) collective-permute-start(f32[96,1152]{1,0:T(8,128)} %get-tuple-element.20), channel_id=1, source_target_pairs={{0,384},{192,576},{384,0},{576,192},{1,385},{193,577},{385,1},{577... | collective-permute-start | bytes 1327112 | tf_op jit(solution)/shard_map/ppermute | solution.py:84
  145.8 10.6 %all-to-all-start.1 = ((f32[4,1,256]{2,1,0:T(1,128)}), f32[4,1,256]{2,1,0:T(1,128)S(1)}, u32[]{:S(2)}, u32[]{:S(2)}) async-start(f32[4,1,256]{2,1,0:T(1,128)} %reshape.197), calls=%async_computation.1 | async-start | bytes 8192 | tf_op jit(solution)/shard_map/all_to_all | solution.py:221
  158.3 4.9 %copy-start.5 = (f32[96,1152]{1,0:T(8,128)}, f32[96,1152]{1,0:T(8,128)S(1)}, u32[]{:S(2)}) copy-start(f32[96,1152]{1,0:T(8,128)S(1)} %collective-permute-done.11) | copy-start | bytes 1327108
  164.7 18.9 %all-to-all-start.2 = ((f32[8,1,32]{2,1,0:T(1,128)}), f32[8,1,32]{2,1,0:T(1,128)S(1)}, u32[]{:S(2)}, u32[]{:S(2)}) async-start(f32[8,1,32]{2,1,0:T(1,128)} %bitcast.18), calls=%async_computation.2 | async-start | bytes 8192 | tf_op jit(solution)/shard_map/all_to_all | solution.py:228
  173.9 18.3 %collective-permute-start.14 = (f32[32,1152]{1,0:T(8,128)}, f32[32,1152]{1,0:T(8,128)S(1)}, u32[]{:S(2)}, u32[]{:S(2)}) collective-permute-start(f32[32,1152]{1,0:T(8,128)} %get-tuple-element.21), channel_id=1, source_target_pairs={{0,64},{64,128},{128,0},{1,65},{65,129},{129,1},{2,66},{66,130},{1... | collective-permute-start | bytes 442376 | tf_op jit(solution)/shard_map/ppermute | solution.py:84
  179.9 17.1 %collective-permute-start.15 = (f32[32,1152]{1,0:T(8,128)S(1)}, f32[32,1152]{1,0:T(8,128)}, u32[]{:S(2)}, u32[]{:S(2)}) collective-permute-start(f32[32,1152]{1,0:T(8,128)S(1)} %get-tuple-element.22), channel_id=1, source_target_pairs={{0,128},{64,0},{128,64},{1,129},{65,1},{129,65},{2,130},{66,2},{13... | collective-permute-start | bytes 442376 | tf_op jit(solution)/shard_map/ppermute | solution.py:84
Sparse Core Ops, SparseCore 0:
  20.0 79.0 all-gather.1

commit v8 on v6

--- a/solution.py
+++ b/solution.py
@@ -139,7 +139,7 @@
 
     text_unit, text_inverse = normalize_rows(caption_features)
     caption_magnitude = text_unit.astype(jnp.bfloat16)
-    device_portion_count = lax.all_gather(caption_magnitude, ("x", "zh", "core"), axis=0, tiled=True)
+    device_portion_count = lax.all_gather(caption_magnitude, ("core", "x", "zh"), axis=0, tiled=True)
 
     chunk_rows = row_count
     prior_norm = normalize_rows(
@@ -184,12 +184,6 @@
     pooled_labels = group_labels[:, :, 0].reshape(-1)
     target_tile = jnp.concatenate([prior_labels, pooled_labels])
 
-    width = device_portion_count.shape[1]
-    device_portion_count = (
-        device_portion_count.reshape(x_size, zh_size, core_size, row_count, width)
-        .transpose(2, 0, 1, 3, 4)
-        .reshape(outer_size * row_count, width)
-    )
     blocks = jnp.arange(outer_size, dtype=jnp.int32)
     block_core = blocks // (x_size * zh_size)
     block_x = blocks // zh_size % x_size

time: 203 us -> 209 us (1.030)
  waiting for transfers between devices: 57.4 us -> 59.6 us
    unnamed x26 -> x28, local copies, waits for them, and re-layouts: 12.7 us -> 15.6 us
  transfers between devices with their start and end apart: 20 -> 20, of which waited for: 13 -> 13; matrix products, arithmetic and copies ran while one was open for 14% -> 13% of each run, Pallas kernels for 0% -> 0%
where the time goes in v8:
time: 209 us; the launch traced here: 207 us
  starting transfers between devices  75.9 us (36%)
  waiting for transfers between devices  59.6 us (29%)
  local copies, waits for them, and re-layouts  22.1 us (11%)
  matrix products  17.2 us (8%)
  between operations  16.5 us (8%)
  other arithmetic  15.9 us (8%)
    ppermute x16, starting transfers between devices, shift_ring(): return lax.ppermute(x, axis, [(i, (i + step) % size) for i in range(size)])  57.2 us
    ppermute x16, waiting for transfers between devices, shift_ring(): return lax.ppermute(x, axis, [(i, (i + step) % size) for i in range(size)])  26.3 us
    all_gather x1, waiting for transfers between devices, local(): lax.all_gather(caption_magnitude, ('core', 'x', 'zh'), axis=0, tiled=True)  21.6 us
    unnamed x28, local copies, waits for them, and re-layouts  15.6 us
    all_to_all x1, starting transfers between devices, local(): lax.all_to_all(jnp.broadcast_to(pooled_norm, (inner_size, pooled_norm.sha...  8.38 us
    all_to_all x1, waiting for transfers between devices, local(): lax.all_to_all(section_losses, 'section', 0, 0, tiled=True)  6.93 us
    dot_general x1, matrix products, block_contributions(): lax.dot_general(picture_tile, device_portion_count, (((1,), (1,)), ((), (...  5.68 us
    all_to_all x1, starting transfers between devices, local(): lax.all_to_all(section_losses, 'section', 0, 0, tiled=True)  5.53 us
  transfers between devices with their start and end apart: 20, of which 13 were waited for; matrix products, arithmetic and copies ran while one was open for 13% of the time, Pallas kernels for 0%

profile of v8, /device:TPU:1, one launch (start us, length us, event | category | flops | bytes accessed | tf_op | source)
XLA Modules:
  0.0 207.3 jit_solution(2631651248264556840)
XLA Ops:
  7.2 1.2 fusion.27
  8.4 1.6 constant_dynamic-update-slice_fusion.10
  10.0 4.8 %collective-permute-start.1 = (bf16[32,1152]{1,0:T(8,128)(2,1)S(1)}, bf16[32,1152]{1,0:T(8,128)(2,1)S(1)}, u32[]{:S(2)}, u32[]{:S(2)}) collective-permute-start(bf16[32,1152]{1,0:T(8,128)(2,1)S(1)} %get-tuple-element.17), channel_id=1, source_target_pairs={{0,1},{1,2},{2,3},{3,0},{4,5},{5,6},{6,7},{7,4},{8,9},{9,10},{10,1... | collective-permute-start | bytes 221192 | tf_op jit(solution)/shard_map/ppermute | solution.py:84
  14.8 5.5 %collective-permute-start = (bf16[32,1152]{1,0:T(8,128)(2,1)S(1)}, bf16[32,1152]{1,0:T(8,128)(2,1)S(1)}, u32[]{:S(2)}, u32[]{:S(2)}) collective-permute-start(bf16[32,1152]{1,0:T(8,128)(2,1)S(1)} %get-tuple-element.17), channel_id=1, source_target_pairs={{0,3},{1,0},{2,1},{3,2},{4,7},{5,4},{6,5},{7,6},{8,11},{9,8},{10,9... | collective-permute-start | bytes 221192 | tf_op jit(solution)/shard_map/ppermute | solution.py:84
  21.4 1.6 fusion.26
  23.0 4.1 %fusion.68 = (f32[16]{0:T(128)S(1)}, f32[16,729]{1,0:T(8,128)S(1)}) fusion(bf16[1,729,1152]{2,1,0:T(8,128)(2,1)} %param.10, bf16[1152,1152]{1,0:T(8,128)(2,1)} %param.12, s32[1152]{0:T(1024)S(1)} %add_select_fusion, bf16[1152]{0:T(1024)(128)(2,1)} %param.11), kind=kOutput, calls=%fused_computation.126 | convolution fusion | flops 69426560 | bytes 4387456 | tf_op jit(solution)/shard_map/dot_general | solution.py:24
  27.4 2.2 %fusion.15 = f32[16,1152]{1,0:T(8,128)S(1)} fusion(bf16[1152,1152]{1,0:T(8,128)(2,1)S(1)} %copy-done, bf16[1,729,1152]{2,1,0:T(8,128)(2,1)} %param.10, f32[16,729]{1,0:T(8,128)S(1)} %get-tuple-element.24, f32[16]{0:T(128)S(1)} %fusion.38, f32[16]{0:T(128)S(1)} %get-tuple-element.23), kind=kOutput, calls=%fused_computation.22 | convolution fusion | flops 69394608 | bytes 4454336 | tf_op jit(solution)/shard_map/dot_general | solution.py:31
  30.0 2.2 %convolution_reduce_fusion = bf16[1152]{0:T(1024)(128)(2,1)S(1)} fusion(bf16[1152,1]{0,1:T(2,128)(2,1)S(1)} %reshape.163, bf16[1152,1152]{1,0:T(8,128)(2,1)} %param.14), kind=kOutput, calls=%fused_computation.23 | convolution fusion | flops 2654208 | bytes 2658816 | tf_op jit(solution)/shard_map/dot_general | solution.py:38
  35.9 8.4 %all-to-all-start = ((bf16[32,2,576]{2,1,0:T(2,128)(2,1)}), bf16[32,2,576]{2,1,0:T(2,128)(2,1)S(1)}, u32[]{:S(2)}, u32[]{:S(2)}) async-start(bf16[32,2,576]{2,1,0:T(2,128)(2,1)} %reshape.168), calls=%async_computation | async-start | bytes 163840 | tf_op jit(solution)/shard_map/all_to_all | solution.py:164
  45.7 3.1 %collective-permute-start.2 = (bf16[32,1152]{1,0:T(8,128)(2,1)S(1)}, bf16[32,1152]{1,0:T(8,128)(2,1)S(1)}, u32[]{:S(2)}, u32[]{:S(2)}) collective-permute-start(bf16[32,1152]{1,0:T(8,128)(2,1)S(1)} %collective-permute-done.1), channel_id=1, source_target_pairs={{0,1},{1,2},{2,3},{3,0},{4,5},{5,6},{6,7},{7,4},{8,9},{9,10},{10,1... | collective-permute-start | bytes 221192 | tf_op jit(solution)/shard_map/ppermute | solution.py:84
  48.9 5.4 %collective-permute-done.2 = bf16[32,1152]{1,0:T(8,128)(2,1)S(1)} collective-permute-done((bf16[32,1152]{1,0:T(8,128)(2,1)S(1)}, bf16[32,1152]{1,0:T(8,128)(2,1)S(1)}, u32[]{:S(2)}, u32[]{:S(2)}) %collective-permute-start.2) | collective-permute-done | bytes 73760 | tf_op jit(solution)/shard_map/ppermute | solution.py:84
  55.0 3.1 %collective-permute-start.6 = (bf16[128,1152]{1,0:T(8,128)(2,1)}, bf16[128,1152]{1,0:T(8,128)(2,1)S(1)}, u32[]{:S(2)}, u32[]{:S(2)}) collective-permute-start(bf16[128,1152]{1,0:T(8,128)(2,1)} %pad_maximum_fusion), channel_id=1, source_target_pairs={{0,4},{4,8},{8,12},{12,16},{16,20},{20,24},{24,28},{28,0},{1,5},{5... | collective-permute-start | bytes 884744 | tf_op jit(solution)/shard_map/ppermute | solution.py:84
  59.6 3.4 %collective-permute-start.3 = (bf16[128,1152]{1,0:T(8,128)(2,1)}, bf16[128,1152]{1,0:T(8,128)(2,1)}, u32[]{:S(2)}, u32[]{:S(2)}) collective-permute-start(bf16[128,1152]{1,0:T(8,128)(2,1)} %pad_maximum_fusion), channel_id=1, source_target_pairs={{0,28},{4,0},{8,4},{12,8},{16,12},{20,16},{24,20},{28,24},{1,29},{... | collective-permute-start | bytes 884744 | tf_op jit(solution)/shard_map/ppermute | solution.py:84
  63.9 1.9 collective-permute-start.7
  66.5 1.1 collective-permute-done.3
  67.5 4.4 %collective-permute-start.4 = (bf16[128,1152]{1,0:T(8,128)(2,1)}, bf16[128,1152]{1,0:T(8,128)(2,1)}, u32[]{:S(2)}, u32[]{:S(2)}) collective-permute-start(bf16[128,1152]{1,0:T(8,128)(2,1)} %collective-permute-done.3), channel_id=1, source_target_pairs={{0,28},{4,0},{8,4},{12,8},{16,12},{20,16},{24,20},{28,24},{1,29},{... | collective-permute-start | bytes 884744 | tf_op jit(solution)/shard_map/ppermute | solution.py:84
  72.7 1.9 collective-permute-start.8
  75.9 5.0 %collective-permute-start.5 = (bf16[128,1152]{1,0:T(8,128)(2,1)}, bf16[128,1152]{1,0:T(8,128)(2,1)S(1)}, u32[]{:S(2)}, u32[]{:S(2)}) collective-permute-start(bf16[128,1152]{1,0:T(8,128)(2,1)} %collective-permute-done.4), channel_id=1, source_target_pairs={{0,28},{4,0},{8,4},{12,8},{16,12},{20,16},{24,20},{28,24},{1,29},{... | collective-permute-start | bytes 884744 | tf_op jit(solution)/shard_map/ppermute | solution.py:84
  80.9 1.7 constant_dynamic-update-slice_fusion.6
  82.6 21.6 %all-gather.2.cloned.1.call-done = bf16[768,1152]{1,0:T(8,128)(2,1)} async-done(((bf16[32,1152]{1,0:T(8,128)(2,1)}), bf16[768,1152]{1,0:T(8,128)(2,1)}) %all-gather.2.cloned.1.call-update) | async-done | bytes 1769488 | tf_op jit(solution)/shard_map/all_gather | solution.py:142
  104.2 2.3 %collective-permute-start.9 = (bf16[128,1152]{1,0:T(8,128)(2,1)}, bf16[128,1152]{1,0:T(8,128)(2,1)S(1)}, u32[]{:S(2)}, u32[]{:S(2)}) collective-permute-start(bf16[128,1152]{1,0:T(8,128)(2,1)} %collective-permute-done.8), channel_id=1, source_target_pairs={{0,4},{4,8},{8,12},{12,16},{16,20},{20,24},{24,28},{28,0},{1,5},{5... | collective-permute-start | bytes 884744 | tf_op jit(solution)/shard_map/ppermute | solution.py:84
  106.5 1.7 constant_dynamic-update-slice_fusion.5
  109.0 7.1 %collective-permute-done.9 = bf16[128,1152]{1,0:T(8,128)(2,1)S(1)} collective-permute-done((bf16[128,1152]{1,0:T(8,128)(2,1)}, bf16[128,1152]{1,0:T(8,128)(2,1)S(1)}, u32[]{:S(2)}, u32[]{:S(2)}) %collective-permute-start.9) | collective-permute-done | bytes 294944 | tf_op jit(solution)/shard_map/ppermute | solution.py:84
  116.8 1.7 constant_dynamic-update-slice_fusion.2
  118.5 1.7 constant_dynamic-update-slice_fusion.1
  121.6 5.7 %fusion.6 = (f32[1056]{0:T(1024)S(1)}, f32[1056,768]{1,0:T(8,128)S(1)}) fusion(s32[768]{0:T(1024)S(1)} %add.265, s32[1056]{0:T(1024)S(1)} %pad_add_fusion, f32[]{:T(128)} %bitcast.61, bf16[1056,1152]{1,0:T(8,128)(2,1)} %bitcast_dynamic-update-slice_fusion, bf16[768,1152]{1,0:T(8,128)(2,1)S(1)} %copy-done.6, f32[]{:T(128)} %bitcast.59), kind=kOutput, calls=%fused_computation.11 | convolution fusion | flops 1878293504 | bytes 7458056 | tf_op jit(solution)/shard_map/dot_general | solution.py:59
  127.3 3.0 %fusion.11 = f32[768,1152]{1,0:T(8,128)S(1)} fusion(bf16[1056,1152]{1,0:T(8,128)(2,1)S(1)} %copy-done.5, f32[1056,768]{1,0:T(8,128)S(1)} %get-tuple-element.26, f32[]{:T(128)} %bitcast.60, s32[768]{0:T(1024)S(1)} %add.265, s32[1056]{0:T(1024)S(1)} %pad_add_fusion), kind=kOutput, calls=%fused_computation.20 | convolution fusion | flops 1875050496 | bytes 9223300 | tf_op jit(solution)/shard_map/dot_general | solution.py:74
  130.3 1.7 copy-done.2
  132.0 1.4 dynamic-slice_bitcast_fusion
  133.4 2.9 %collective-permute-start.10 = (f32[384,1152]{1,0:T(8,128)}, f32[384,1152]{1,0:T(8,128)}, u32[]{:S(2)}, u32[]{:S(2)}) collective-permute-start(f32[384,1152]{1,0:T(8,128)} %dynamic-slice_bitcast_fusion), channel_id=1, source_target_pairs={{0,32},{32,0},{1,33},{33,1},{2,34},{34,2},{3,35},{35,3},{4,36},{36... | collective-permute-start | bytes 5308424 | tf_op jit(solution)/shard_map/ppermute | solution.py:84
  136.8 3.2 %collective-permute-done.10 = f32[384,1152]{1,0:T(8,128)} collective-permute-done((f32[384,1152]{1,0:T(8,128)}, f32[384,1152]{1,0:T(8,128)}, u32[]{:S(2)}, u32[]{:S(2)}) %collective-permute-start.10) | collective-permute-done | bytes 1769504 | tf_op jit(solution)/shard_map/ppermute | solution.py:84
  140.0 2.2 %bitcast_add_fusion = f32[384,1152]{1,0:T(8,128)S(1)} fusion(f32[384,1152]{1,0:T(8,128)} %collective-permute-done.10, f32[2,384,1152]{2,1,0:T(8,128)} %bitcast.65, s32[]{:T(128)S(6)} %select_n.174), kind=kLoop, calls=%fused_computation.15 | loop fusion | flops 442368 | bytes 5308420 | tf_op jit(solution)/shard_map/add | solution.py:110
  142.2 1.2 copy-done.1
  143.4 1.1 dynamic-slice_bitcast_fusion.3
  144.5 2.1 %collective-permute-start.11 = (f32[96,1152]{1,0:T(8,128)}, f32[96,1152]{1,0:T(8,128)S(1)}, u32[]{:S(2)}, u32[]{:S(2)}) collective-permute-start(f32[96,1152]{1,0:T(8,128)} %get-tuple-element.18), channel_id=1, source_target_pairs={{0,192},{192,384},{384,576},{576,0},{1,193},{193,385},{385,577},{5... | collective-permute-start | bytes 1327112 | tf_op jit(solution)/shard_map/ppermute | solution.py:84
  146.7 4.3 %collective-permute-start.12 = (f32[96,1152]{1,0:T(8,128)}, f32[96,1152]{1,0:T(8,128)}, u32[]{:S(2)}, u32[]{:S(2)}) collective-permute-start(f32[96,1152]{1,0:T(8,128)} %get-tuple-element.20), channel_id=1, source_target_pairs={{0,384},{192,576},{384,0},{576,192},{1,385},{193,577},{385,1},{577... | collective-permute-start | bytes 1327112 | tf_op jit(solution)/shard_map/ppermute | solution.py:84
  151.0 3.1 %collective-permute-start.13 = (f32[96,1152]{1,0:T(8,128)}, f32[96,1152]{1,0:T(8,128)}, u32[]{:S(2)}, u32[]{:S(2)}) collective-permute-start(f32[96,1152]{1,0:T(8,128)} %get-tuple-element.19), channel_id=1, source_target_pairs={{0,576},{192,0},{384,192},{576,384},{1,577},{193,1},{385,193},{577... | collective-permute-start | bytes 1327112 | tf_op jit(solution)/shard_map/ppermute | solution.py:84
  154.7 4.8 %all-to-all-start.1 = ((f32[4,1,256]{2,1,0:T(1,128)}), f32[4,1,256]{2,1,0:T(1,128)S(1)}, u32[]{:S(2)}, u32[]{:S(2)}) async-start(f32[4,1,256]{2,1,0:T(1,128)} %reshape.170), calls=%async_computation.1 | async-start | bytes 8192 | tf_op jit(solution)/shard_map/all_to_all | solution.py:215
  159.5 4.8 %all-to-all-done.1 = f32[4,1,256]{2,1,0:T(1,128)S(1)} async-done(((f32[4,1,256]{2,1,0:T(1,128)}), f32[4,1,256]{2,1,0:T(1,128)S(1)}, u32[]{:S(2)}, u32[]{:S(2)}) %all-to-all-start.1) | async-done | bytes 4128 | tf_op jit(solution)/shard_map/all_to_all | solution.py:215
  166.2 2.5 %collective-permute-done.12 = f32[96,1152]{1,0:T(8,128)} collective-permute-done((f32[96,1152]{1,0:T(8,128)}, f32[96,1152]{1,0:T(8,128)}, u32[]{:S(2)}, u32[]{:S(2)}) %collective-permute-start.12) | collective-permute-done | bytes 442400 | tf_op jit(solution)/shard_map/ppermute | solution.py:84
  168.7 2.2 %collective-permute-done.13 = f32[96,1152]{1,0:T(8,128)} collective-permute-done((f32[96,1152]{1,0:T(8,128)}, f32[96,1152]{1,0:T(8,128)}, u32[]{:S(2)}, u32[]{:S(2)}) %collective-permute-start.13) | collective-permute-done | bytes 442400 | tf_op jit(solution)/shard_map/ppermute | solution.py:84
  171.0 1.5 fusion.19
  173.2 4.8 %collective-permute-start.14 = (f32[32,1152]{1,0:T(8,128)}, f32[32,1152]{1,0:T(8,128)S(1)}, u32[]{:S(2)}, u32[]{:S(2)}) collective-permute-start(f32[32,1152]{1,0:T(8,128)} %get-tuple-element.21), channel_id=1, source_target_pairs={{0,64},{64,128},{128,0},{1,65},{65,129},{129,1},{2,66},{66,130},{1... | collective-permute-start | bytes 442376 | tf_op jit(solution)/shard_map/ppermute | solution.py:84
  178.0 4.4 %collective-permute-start.15 = (f32[32,1152]{1,0:T(8,128)S(1)}, f32[32,1152]{1,0:T(8,128)}, u32[]{:S(2)}, u32[]{:S(2)}) collective-permute-start(f32[32,1152]{1,0:T(8,128)S(1)} %get-tuple-element.22), channel_id=1, source_target_pairs={{0,128},{64,0},{128,64},{1,129},{65,1},{129,65},{2,130},{66,2},{13... | collective-permute-start | bytes 442376 | tf_op jit(solution)/shard_map/ppermute | solution.py:84
  182.4 5.5 %all-to-all-start.2 = ((f32[8,1,32]{2,1,0:T(1,128)}), f32[8,1,32]{2,1,0:T(1,128)S(1)}, u32[]{:S(2)}, u32[]{:S(2)}) async-start(f32[8,1,32]{2,1,0:T(1,128)} %bitcast.14), calls=%async_computation.2 | async-start | bytes 8192 | tf_op jit(solution)/shard_map/all_to_all | solution.py:222
  187.9 6.9 %all-to-all-done.2 = f32[8,1,32]{2,1,0:T(1,128)S(1)} async-done(((f32[8,1,32]{2,1,0:T(1,128)}), f32[8,1,32]{2,1,0:T(1,128)S(1)}, u32[]{:S(2)}, u32[]{:S(2)}) %all-to-all-start.2) | async-done | bytes 1056 | tf_op jit(solution)/shard_map/all_to_all | solution.py:222
  195.4 3.2 %collective-permute-done.15 = f32[32,1152]{1,0:T(8,128)} collective-permute-done((f32[32,1152]{1,0:T(8,128)S(1)}, f32[32,1152]{1,0:T(8,128)}, u32[]{:S(2)}, u32[]{:S(2)}) %collective-permute-start.15) | collective-permute-done | bytes 147488 | tf_op jit(solution)/shard_map/ppermute | solution.py:84
  198.5 1.1 fusion.29
  (76 shorter events, 18.2 us)
Async XLA Ops:
  7.2 20.2 %copy-start = (bf16[1152,1152]{1,0:T(8,128)(2,1)S(1)}, bf16[1152,1152]{1,0:T(8,128)(2,1)}, u32[]{:S(2)}) copy-start(bf16[1152,1152]{1,0:T(8,128)(2,1)} %param.13) | copy-start | bytes 7962628
  7.2 97.1 %all-gather.2.cloned.1.call-start = ((), (), s32[]{:S(2)}) async-start(), calls=%async_computation.3 | async-start | bytes 1843200 | tf_op jit(solution)/shard_map/all_gather | solution.py:142
  10.0 35.7 %collective-permute-start.1 = (bf16[32,1152]{1,0:T(8,128)(2,1)S(1)}, bf16[32,1152]{1,0:T(8,128)(2,1)S(1)}, u32[]{:S(2)}, u32[]{:S(2)}) collective-permute-start(bf16[32,1152]{1,0:T(8,128)(2,1)S(1)} %get-tuple-element.17), channel_id=1, source_target_pairs={{0,1},{1,2},{2,3},{3,0},{4,5},{5,6},{6,7},{7,4},{8,9},{9,10},{10,1... | collective-permute-start | bytes 221192 | tf_op jit(solution)/shard_map/ppermute | solution.py:84
  14.8 34.1 %collective-permute-start = (bf16[32,1152]{1,0:T(8,128)(2,1)S(1)}, bf16[32,1152]{1,0:T(8,128)(2,1)S(1)}, u32[]{:S(2)}, u32[]{:S(2)}) collective-permute-start(bf16[32,1152]{1,0:T(8,128)(2,1)S(1)} %get-tuple-element.17), channel_id=1, source_target_pairs={{0,3},{1,0},{2,1},{3,2},{4,7},{5,4},{6,5},{7,6},{8,11},{9,8},{10,9... | collective-permute-start | bytes 221192 | tf_op jit(solution)/shard_map/ppermute | solution.py:84
  35.9 39.3 %all-to-all-start = ((bf16[32,2,576]{2,1,0:T(2,128)(2,1)}), bf16[32,2,576]{2,1,0:T(2,128)(2,1)S(1)}, u32[]{:S(2)}, u32[]{:S(2)}) async-start(bf16[32,2,576]{2,1,0:T(2,128)(2,1)} %reshape.168), calls=%async_computation | async-start | bytes 163840 | tf_op jit(solution)/shard_map/all_to_all | solution.py:164
  45.7 8.6 %collective-permute-start.2 = (bf16[32,1152]{1,0:T(8,128)(2,1)S(1)}, bf16[32,1152]{1,0:T(8,128)(2,1)S(1)}, u32[]{:S(2)}, u32[]{:S(2)}) collective-permute-start(bf16[32,1152]{1,0:T(8,128)(2,1)S(1)} %collective-permute-done.1), channel_id=1, source_target_pairs={{0,1},{1,2},{2,3},{3,0},{4,5},{5,6},{6,7},{7,4},{8,9},{9,10},{10,1... | collective-permute-start | bytes 221192 | tf_op jit(solution)/shard_map/ppermute | solution.py:84
  55.0 8.9 %collective-permute-start.6 = (bf16[128,1152]{1,0:T(8,128)(2,1)}, bf16[128,1152]{1,0:T(8,128)(2,1)S(1)}, u32[]{:S(2)}, u32[]{:S(2)}) collective-permute-start(bf16[128,1152]{1,0:T(8,128)(2,1)} %pad_maximum_fusion), channel_id=1, source_target_pairs={{0,4},{4,8},{8,12},{12,16},{16,20},{20,24},{24,28},{28,0},{1,5},{5... | collective-permute-start | bytes 884744 | tf_op jit(solution)/shard_map/ppermute | solution.py:84
  59.6 7.9 %collective-permute-start.3 = (bf16[128,1152]{1,0:T(8,128)(2,1)}, bf16[128,1152]{1,0:T(8,128)(2,1)}, u32[]{:S(2)}, u32[]{:S(2)}) collective-permute-start(bf16[128,1152]{1,0:T(8,128)(2,1)} %pad_maximum_fusion), channel_id=1, source_target_pairs={{0,28},{4,0},{8,4},{12,8},{16,12},{20,16},{24,20},{28,24},{1,29},{... | collective-permute-start | bytes 884744 | tf_op jit(solution)/shard_map/ppermute | solution.py:84
  63.9 8.8 %collective-permute-start.7 = (bf16[128,1152]{1,0:T(8,128)(2,1)S(1)}, bf16[128,1152]{1,0:T(8,128)(2,1)}, u32[]{:S(2)}, u32[]{:S(2)}) collective-permute-start(bf16[128,1152]{1,0:T(8,128)(2,1)S(1)} %collective-permute-done.6), channel_id=1, source_target_pairs={{0,4},{4,8},{8,12},{12,16},{16,20},{20,24},{24,28},{28,0},{1,5},{5... | collective-permute-start | bytes 884744 | tf_op jit(solution)/shard_map/ppermute | solution.py:84
  67.5 8.4 %collective-permute-start.4 = (bf16[128,1152]{1,0:T(8,128)(2,1)}, bf16[128,1152]{1,0:T(8,128)(2,1)}, u32[]{:S(2)}, u32[]{:S(2)}) collective-permute-start(bf16[128,1152]{1,0:T(8,128)(2,1)} %collective-permute-done.3), channel_id=1, source_target_pairs={{0,28},{4,0},{8,4},{12,8},{16,12},{20,16},{24,20},{28,24},{1,29},{... | collective-permute-start | bytes 884744 | tf_op jit(solution)/shard_map/ppermute | solution.py:84
  72.7 10.0 %collective-permute-start.8 = (bf16[128,1152]{1,0:T(8,128)(2,1)}, bf16[128,1152]{1,0:T(8,128)(2,1)}, u32[]{:S(2)}, u32[]{:S(2)}) collective-permute-start(bf16[128,1152]{1,0:T(8,128)(2,1)} %collective-permute-done.7), channel_id=1, source_target_pairs={{0,4},{4,8},{8,12},{12,16},{16,20},{20,24},{24,28},{28,0},{1,5},{5... | collective-permute-start | bytes 884744 | tf_op jit(solution)/shard_map/ppermute | solution.py:84
  75.9 32.3 %collective-permute-start.5 = (bf16[128,1152]{1,0:T(8,128)(2,1)}, bf16[128,1152]{1,0:T(8,128)(2,1)S(1)}, u32[]{:S(2)}, u32[]{:S(2)}) collective-permute-start(bf16[128,1152]{1,0:T(8,128)(2,1)} %collective-permute-done.4), channel_id=1, source_target_pairs={{0,28},{4,0},{8,4},{12,8},{16,12},{20,16},{24,20},{28,24},{1,29},{... | collective-permute-start | bytes 884744 | tf_op jit(solution)/shard_map/ppermute | solution.py:84
  104.2 17.3 %copy-start.6 = (bf16[768,1152]{1,0:T(8,128)(2,1)S(1)}, bf16[768,1152]{1,0:T(8,128)(2,1)}, u32[]{:S(2)}) copy-start(bf16[768,1152]{1,0:T(8,128)(2,1)} %all-gather.2.cloned.1.call-done) | copy-start | bytes 5308420
  104.2 11.8 %collective-permute-start.9 = (bf16[128,1152]{1,0:T(8,128)(2,1)}, bf16[128,1152]{1,0:T(8,128)(2,1)S(1)}, u32[]{:S(2)}, u32[]{:S(2)}) collective-permute-start(bf16[128,1152]{1,0:T(8,128)(2,1)} %collective-permute-done.8), channel_id=1, source_target_pairs={{0,4},{4,8},{8,12},{12,16},{16,20},{20,24},{24,28},{28,0},{1,5},{5... | collective-permute-start | bytes 884744 | tf_op jit(solution)/shard_map/ppermute | solution.py:84
  121.6 5.7 %copy-start.5 = (bf16[1056,1152]{1,0:T(8,128)(2,1)S(1)}, bf16[1056,1152]{1,0:T(8,128)(2,1)}, u32[]{:S(2)}) copy-start(bf16[1056,1152]{1,0:T(8,128)(2,1)} %bitcast_dynamic-update-slice_fusion) | copy-start | bytes 7299076
  130.3 1.8 copy-start.2
  133.4 6.6 %collective-permute-start.10 = (f32[384,1152]{1,0:T(8,128)}, f32[384,1152]{1,0:T(8,128)}, u32[]{:S(2)}, u32[]{:S(2)}) collective-permute-start(f32[384,1152]{1,0:T(8,128)} %dynamic-slice_bitcast_fusion), channel_id=1, source_target_pairs={{0,32},{32,0},{1,33},{33,1},{2,34},{34,2},{3,35},{35,3},{4,36},{36... | collective-permute-start | bytes 5308424 | tf_op jit(solution)/shard_map/ppermute | solution.py:84
  142.2 1.2 copy-start.1
  143.4 55.2 %copy-start.3 = (bf16[32,1152]{1,0:T(8,128)(2,1)S(1)}, bf16[32,1152]{1,0:T(8,128)(2,1)}, u32[]{:S(2)}) copy-start(bf16[32,1152]{1,0:T(8,128)(2,1)} %param.16) | copy-start | bytes 221188
  144.5 21.7 %collective-permute-start.11 = (f32[96,1152]{1,0:T(8,128)}, f32[96,1152]{1,0:T(8,128)S(1)}, u32[]{:S(2)}, u32[]{:S(2)}) collective-permute-start(f32[96,1152]{1,0:T(8,128)} %get-tuple-element.18), channel_id=1, source_target_pairs={{0,192},{192,384},{384,576},{576,0},{1,193},{193,385},{385,577},{5... | collective-permute-start | bytes 1327112 | tf_op jit(solution)/shard_map/ppermute | solution.py:84
  146.7 22.1 %collective-permute-start.12 = (f32[96,1152]{1,0:T(8,128)}, f32[96,1152]{1,0:T(8,128)}, u32[]{:S(2)}, u32[]{:S(2)}) collective-permute-start(f32[96,1152]{1,0:T(8,128)} %get-tuple-element.20), channel_id=1, source_target_pairs={{0,384},{192,576},{384,0},{576,192},{1,385},{193,577},{385,1},{577... | collective-permute-start | bytes 1327112 | tf_op jit(solution)/shard_map/ppermute | solution.py:84
  151.0 20.0 %collective-permute-start.13 = (f32[96,1152]{1,0:T(8,128)}, f32[96,1152]{1,0:T(8,128)}, u32[]{:S(2)}, u32[]{:S(2)}) collective-permute-start(f32[96,1152]{1,0:T(8,128)} %get-tuple-element.19), channel_id=1, source_target_pairs={{0,576},{192,0},{384,192},{576,384},{1,577},{193,1},{385,193},{577... | collective-permute-start | bytes 1327112 | tf_op jit(solution)/shard_map/ppermute | solution.py:84
  154.7 9.6 %all-to-all-start.1 = ((f32[4,1,256]{2,1,0:T(1,128)}), f32[4,1,256]{2,1,0:T(1,128)S(1)}, u32[]{:S(2)}, u32[]{:S(2)}) async-start(f32[4,1,256]{2,1,0:T(1,128)} %reshape.170), calls=%async_computation.1 | async-start | bytes 8192 | tf_op jit(solution)/shard_map/all_to_all | solution.py:215
  166.2 2.5 %copy-start.4 = (f32[96,1152]{1,0:T(8,128)}, f32[96,1152]{1,0:T(8,128)S(1)}, u32[]{:S(2)}) copy-start(f32[96,1152]{1,0:T(8,128)S(1)} %collective-permute-done.11) | copy-start | bytes 1327108
  173.2 22.2 %collective-permute-start.14 = (f32[32,1152]{1,0:T(8,128)}, f32[32,1152]{1,0:T(8,128)S(1)}, u32[]{:S(2)}, u32[]{:S(2)}) collective-permute-start(f32[32,1152]{1,0:T(8,128)} %get-tuple-element.21), channel_id=1, source_target_pairs={{0,64},{64,128},{128,0},{1,65},{65,129},{129,1},{2,66},{66,130},{1... | collective-permute-start | bytes 442376 | tf_op jit(solution)/shard_map/ppermute | solution.py:84
  178.0 20.6 %collective-permute-start.15 = (f32[32,1152]{1,0:T(8,128)S(1)}, f32[32,1152]{1,0:T(8,128)}, u32[]{:S(2)}, u32[]{:S(2)}) collective-permute-start(f32[32,1152]{1,0:T(8,128)S(1)} %get-tuple-element.22), channel_id=1, source_target_pairs={{0,128},{64,0},{128,64},{1,129},{65,1},{129,65},{2,130},{66,2},{13... | collective-permute-start | bytes 442376 | tf_op jit(solution)/shard_map/ppermute | solution.py:84
  182.4 12.5 %all-to-all-start.2 = ((f32[8,1,32]{2,1,0:T(1,128)}), f32[8,1,32]{2,1,0:T(1,128)S(1)}, u32[]{:S(2)}, u32[]{:S(2)}) async-start(f32[8,1,32]{2,1,0:T(1,128)} %bitcast.14), calls=%async_computation.2 | async-start | bytes 8192 | tf_op jit(solution)/shard_map/all_to_all | solution.py:222
Sparse Core Ops, SparseCore 0:
  23.1 81.0 all-gather.1

commit v9 on v6

--- a/solution.py
+++ b/solution.py
@@ -90,10 +90,10 @@
     forward_steps = size // 2
     backward_steps = size - 1 - forward_steps
     for step in range(1, forward_steps + 1):
-        if held is not None and step == held_step:
-            forward, held = lax.optimization_barrier((forward, held))
         forward = shift_ring(forward, axis, size, 1)
         arrived[(size - step) % size] = forward
+        if held is not None and step == held_step:
+            arrived[(size - step) % size], held = lax.optimization_barrier((forward, held))
         if step <= backward_steps:
             backward = shift_ring(backward, axis, size, -1)
             arrived[step] = backward
@@ -150,7 +150,7 @@
         "section",
         section_size,
         held=device_portion_count,
-        held_step=section_size // 2,
+        held_step=section_size // 2 - 1,
     )
 
     pooled = pool_image(

time: 203 us -> 193 us (0.951)
  waiting for transfers between devices: 57.4 us -> 47.2 us
    all_gather x1, waiting for transfers between devices: 21.3 us -> 11.3 us  [local(): lax.all_gather(caption_magnitude, ('x', 'zh', 'core'), axis=0, tiled=True)]
where the time goes in v9:
time: 193 us; the launch traced here: 191 us
  starting transfers between devices  74.9 us (39%)
  waiting for transfers between devices  47.2 us (24%)
  local copies, waits for them, and re-layouts  21.6 us (11%)
  between operations  16.5 us (9%)
  other arithmetic  15.9 us (8%)
  matrix products  15.4 us (8%)
    ppermute x16, starting transfers between devices, shift_ring(): return lax.ppermute(x, axis, [(i, (i + step) % size) for i in range(size)])  56.2 us
    ppermute x16, waiting for transfers between devices, shift_ring(): return lax.ppermute(x, axis, [(i, (i + step) % size) for i in range(size)])  24.2 us
    unnamed x26, local copies, waits for them, and re-layouts  13.9 us
    all_gather x1, waiting for transfers between devices, local(): lax.all_gather(caption_magnitude, ('x', 'zh', 'core'), axis=0, tiled=True)  11.3 us
    all_to_all x1, starting transfers between devices, local(): lax.all_to_all(jnp.broadcast_to(pooled_norm, (inner_size, pooled_norm.sha...  8.38 us
    all_to_all x1, waiting for transfers between devices, local(): lax.all_to_all(section_losses, 'section', 0, 0, tiled=True)  6.93 us
    all_to_all x1, starting transfers between devices, local(): lax.all_to_all(section_losses, 'section', 0, 0, tiled=True)  5.5 us
    all_to_all x1, waiting for transfers between devices, local(): lax.all_to_all(loss_parts.reshape(section_size, mp_size, row_count), 'mp'...  4.82 us
  transfers between devices with their start and end apart: 20, of which 13 were waited for; matrix products, arithmetic and copies ran while one was open for 14% of the time, Pallas kernels for 0%

profile of v9, /device:TPU:1, one launch (start us, length us, event | category | flops | bytes accessed | tf_op | source)
XLA Modules:
  0.0 191.4 jit_solution(15780724559553454469)
XLA Ops:
  7.2 1.2 fusion.27
  8.4 1.6 constant_dynamic-update-slice_fusion.10
  10.0 4.8 %collective-permute-start.1 = (bf16[32,1152]{1,0:T(8,128)(2,1)S(1)}, bf16[32,1152]{1,0:T(8,128)(2,1)S(1)}, u32[]{:S(2)}, u32[]{:S(2)}) collective-permute-start(bf16[32,1152]{1,0:T(8,128)(2,1)S(1)} %get-tuple-element.17), channel_id=1, source_target_pairs={{0,1},{1,2},{2,3},{3,0},{4,5},{5,6},{6,7},{7,4},{8,9},{9,10},{10,1... | collective-permute-start | bytes 221192 | tf_op jit(solution)/shard_map/ppermute | solution.py:84
  14.8 5.5 %collective-permute-start = (bf16[32,1152]{1,0:T(8,128)(2,1)S(1)}, bf16[32,1152]{1,0:T(8,128)(2,1)S(1)}, u32[]{:S(2)}, u32[]{:S(2)}) collective-permute-start(bf16[32,1152]{1,0:T(8,128)(2,1)S(1)} %get-tuple-element.17), channel_id=1, source_target_pairs={{0,3},{1,0},{2,1},{3,2},{4,7},{5,4},{6,5},{7,6},{8,11},{9,8},{10,9... | collective-permute-start | bytes 221192 | tf_op jit(solution)/shard_map/ppermute | solution.py:84
  21.4 1.6 fusion.26
  23.0 4.1 %fusion.68 = (f32[16]{0:T(128)S(1)}, f32[16,729]{1,0:T(8,128)S(1)}) fusion(bf16[1,729,1152]{2,1,0:T(8,128)(2,1)} %param.10, bf16[1152,1152]{1,0:T(8,128)(2,1)} %param.12, s32[1152]{0:T(1024)S(1)} %add_select_fusion, bf16[1152]{0:T(1024)(128)(2,1)} %param.11), kind=kOutput, calls=%fused_computation.126 | convolution fusion | flops 69426560 | bytes 4387456 | tf_op jit(solution)/shard_map/dot_general | solution.py:24
  27.4 2.2 %fusion.15 = f32[16,1152]{1,0:T(8,128)S(1)} fusion(bf16[1152,1152]{1,0:T(8,128)(2,1)S(1)} %copy-done, bf16[1,729,1152]{2,1,0:T(8,128)(2,1)} %param.10, f32[16,729]{1,0:T(8,128)S(1)} %get-tuple-element.24, f32[16]{0:T(128)S(1)} %fusion.38, f32[16]{0:T(128)S(1)} %get-tuple-element.23), kind=kOutput, calls=%fused_computation.22 | convolution fusion | flops 69394608 | bytes 4454336 | tf_op jit(solution)/shard_map/dot_general | solution.py:31
  30.0 2.2 %convolution_reduce_fusion = bf16[1152]{0:T(1024)(128)(2,1)S(1)} fusion(bf16[1152,1]{0,1:T(2,128)(2,1)S(1)} %reshape.171, bf16[1152,1152]{1,0:T(8,128)(2,1)} %param.14), kind=kOutput, calls=%fused_computation.23 | convolution fusion | flops 2654208 | bytes 2658816 | tf_op jit(solution)/shard_map/dot_general | solution.py:38
  34.1 1.1 reduce.9
  35.9 8.4 %all-to-all-start = ((bf16[32,2,576]{2,1,0:T(2,128)(2,1)}), bf16[32,2,576]{2,1,0:T(2,128)(2,1)S(1)}, u32[]{:S(2)}, u32[]{:S(2)}) async-start(bf16[32,2,576]{2,1,0:T(2,128)(2,1)} %reshape.176), calls=%async_computation | async-start | bytes 163840 | tf_op jit(solution)/shard_map/all_to_all | solution.py:164
  45.7 3.1 %collective-permute-start.2 = (bf16[32,1152]{1,0:T(8,128)(2,1)S(1)}, bf16[32,1152]{1,0:T(8,128)(2,1)S(1)}, u32[]{:S(2)}, u32[]{:S(2)}) collective-permute-start(bf16[32,1152]{1,0:T(8,128)(2,1)S(1)} %collective-permute-done.1), channel_id=1, source_target_pairs={{0,1},{1,2},{2,3},{3,0},{4,5},{5,6},{6,7},{7,4},{8,9},{9,10},{10,1... | collective-permute-start | bytes 221192 | tf_op jit(solution)/shard_map/ppermute | solution.py:84
  48.9 5.4 %collective-permute-done.2 = bf16[32,1152]{1,0:T(8,128)(2,1)S(1)} collective-permute-done((bf16[32,1152]{1,0:T(8,128)(2,1)S(1)}, bf16[32,1152]{1,0:T(8,128)(2,1)S(1)}, u32[]{:S(2)}, u32[]{:S(2)}) %collective-permute-start.2) | collective-permute-done | bytes 73760 | tf_op jit(solution)/shard_map/ppermute | solution.py:84
  55.0 3.1 %collective-permute-start.6 = (bf16[128,1152]{1,0:T(8,128)(2,1)}, bf16[128,1152]{1,0:T(8,128)(2,1)S(1)}, u32[]{:S(2)}, u32[]{:S(2)}) collective-permute-start(bf16[128,1152]{1,0:T(8,128)(2,1)} %pad_maximum_fusion), channel_id=1, source_target_pairs={{0,4},{4,8},{8,12},{12,16},{16,20},{20,24},{24,28},{28,0},{1,5},{5... | collective-permute-start | bytes 884744 | tf_op jit(solution)/shard_map/ppermute | solution.py:84
  59.6 3.4 %collective-permute-start.3 = (bf16[128,1152]{1,0:T(8,128)(2,1)}, bf16[128,1152]{1,0:T(8,128)(2,1)}, u32[]{:S(2)}, u32[]{:S(2)}) collective-permute-start(bf16[128,1152]{1,0:T(8,128)(2,1)} %pad_maximum_fusion), channel_id=1, source_target_pairs={{0,28},{4,0},{8,4},{12,8},{16,12},{20,16},{24,20},{28,24},{1,29},{... | collective-permute-start | bytes 884744 | tf_op jit(solution)/shard_map/ppermute | solution.py:84
  63.9 1.9 collective-permute-start.7
  66.5 1.1 collective-permute-done.3
  67.5 4.4 %collective-permute-start.4 = (bf16[128,1152]{1,0:T(8,128)(2,1)}, bf16[128,1152]{1,0:T(8,128)(2,1)}, u32[]{:S(2)}, u32[]{:S(2)}) collective-permute-start(bf16[128,1152]{1,0:T(8,128)(2,1)} %collective-permute-done.3), channel_id=1, source_target_pairs={{0,28},{4,0},{8,4},{12,8},{16,12},{20,16},{24,20},{28,24},{1,29},{... | collective-permute-start | bytes 884744 | tf_op jit(solution)/shard_map/ppermute | solution.py:84
  72.7 1.9 collective-permute-start.8
  75.9 5.0 %collective-permute-start.5 = (bf16[128,1152]{1,0:T(8,128)(2,1)}, bf16[128,1152]{1,0:T(8,128)(2,1)S(1)}, u32[]{:S(2)}, u32[]{:S(2)}) collective-permute-start(bf16[128,1152]{1,0:T(8,128)(2,1)} %collective-permute-done.4), channel_id=1, source_target_pairs={{0,28},{4,0},{8,4},{12,8},{16,12},{20,16},{24,20},{28,24},{1,29},{... | collective-permute-start | bytes 884744 | tf_op jit(solution)/shard_map/ppermute | solution.py:84
  80.9 1.7 constant_dynamic-update-slice_fusion.6
  82.6 2.1 %collective-permute-start.9 = (bf16[128,1152]{1,0:T(8,128)(2,1)}, bf16[128,1152]{1,0:T(8,128)(2,1)S(1)}, u32[]{:S(2)}, u32[]{:S(2)}) collective-permute-start(bf16[128,1152]{1,0:T(8,128)(2,1)} %collective-permute-done.8), channel_id=1, source_target_pairs={{0,4},{4,8},{8,12},{12,16},{16,20},{20,24},{24,28},{28,0},{1,5},{5... | collective-permute-start | bytes 884744 | tf_op jit(solution)/shard_map/ppermute | solution.py:84
  84.7 1.7 constant_dynamic-update-slice_fusion.5
  87.2 4.8 %collective-permute-done.9 = bf16[128,1152]{1,0:T(8,128)(2,1)S(1)} collective-permute-done((bf16[128,1152]{1,0:T(8,128)(2,1)}, bf16[128,1152]{1,0:T(8,128)(2,1)S(1)}, u32[]{:S(2)}, u32[]{:S(2)}) %collective-permute-start.9) | collective-permute-done | bytes 294944 | tf_op jit(solution)/shard_map/ppermute | solution.py:84
  92.7 11.3 %all-gather.2.cloned.1.call-done = bf16[768,1152]{1,0:T(8,128)(2,1)} async-done(((bf16[32,1152]{1,0:T(8,128)(2,1)}), bf16[768,1152]{1,0:T(8,128)(2,1)}) %all-gather.2.cloned.1.call-update) | async-done | bytes 1769488 | tf_op jit(solution)/shard_map/all_gather | solution.py:142
  103.9 1.8 copy.18
  108.2 3.9 %fusion.6 = (f32[1056]{0:T(1024)S(1)}, f32[1056,768]{1,0:T(8,128)S(1)}) fusion(s32[768]{0:T(1024)S(1)} %add.265, s32[1056]{0:T(1024)S(1)} %pad_add_fusion, f32[]{:T(128)} %bitcast.65, bf16[1056,1152]{1,0:T(8,128)(2,1)S(1)} %bitcast_dynamic-update-slice_fusion, bf16[768,1152]{1,0:T(8,128)(2,1)S(1)} %bitcast.71, f32[]{:T(128)} %bitcast.63), kind=kOutput, calls=%fused_computation.11 | convolution fusion | flops 1878293504 | bytes 7458056 | tf_op jit(solution)/shard_map/dot_general | solution.py:59
  112.1 3.0 %fusion.11 = f32[768,1152]{1,0:T(8,128)S(1)} fusion(bf16[1056,1152]{1,0:T(8,128)(2,1)S(1)} %bitcast_dynamic-update-slice_fusion, f32[1056,768]{1,0:T(8,128)S(1)} %get-tuple-element.26, f32[]{:T(128)} %bitcast.64, s32[768]{0:T(1024)S(1)} %add.265, s32[1056]{0:T(1024)S(1)} %pad_add_fusion), kind=kOutput, calls=%fused_computation.20 | convolution fusion | flops 1875050496 | bytes 9223300 | tf_op jit(solution)/shard_map/dot_general | solution.py:74
  115.1 1.7 copy-done.2
  116.8 1.4 dynamic-slice_bitcast_fusion
  118.2 2.1 %collective-permute-start.10 = (f32[384,1152]{1,0:T(8,128)}, f32[384,1152]{1,0:T(8,128)}, u32[]{:S(2)}, u32[]{:S(2)}) collective-permute-start(f32[384,1152]{1,0:T(8,128)} %dynamic-slice_bitcast_fusion), channel_id=1, source_target_pairs={{0,32},{32,0},{1,33},{33,1},{2,34},{34,2},{3,35},{35,3},{4,36},{36... | collective-permute-start | bytes 5308424 | tf_op jit(solution)/shard_map/ppermute | solution.py:84
  120.7 3.4 %collective-permute-done.10 = f32[384,1152]{1,0:T(8,128)} collective-permute-done((f32[384,1152]{1,0:T(8,128)}, f32[384,1152]{1,0:T(8,128)}, u32[]{:S(2)}, u32[]{:S(2)}) %collective-permute-start.10) | collective-permute-done | bytes 1769504 | tf_op jit(solution)/shard_map/ppermute | solution.py:84
  124.1 2.2 %bitcast_add_fusion = f32[384,1152]{1,0:T(8,128)S(1)} fusion(f32[384,1152]{1,0:T(8,128)} %collective-permute-done.10, f32[2,384,1152]{2,1,0:T(8,128)} %bitcast.69, s32[]{:T(128)S(6)} %select_n.174), kind=kLoop, calls=%fused_computation.15 | loop fusion | flops 442368 | bytes 5308420 | tf_op jit(solution)/shard_map/add | solution.py:110
  126.3 1.2 copy-done.1
  127.5 1.1 dynamic-slice_bitcast_fusion.3
  128.6 2.1 %collective-permute-start.11 = (f32[96,1152]{1,0:T(8,128)}, f32[96,1152]{1,0:T(8,128)S(1)}, u32[]{:S(2)}, u32[]{:S(2)}) collective-permute-start(f32[96,1152]{1,0:T(8,128)} %get-tuple-element.18), channel_id=1, source_target_pairs={{0,192},{192,384},{384,576},{576,0},{1,193},{193,385},{385,577},{5... | collective-permute-start | bytes 1327112 | tf_op jit(solution)/shard_map/ppermute | solution.py:84
  130.8 4.3 %collective-permute-start.12 = (f32[96,1152]{1,0:T(8,128)}, f32[96,1152]{1,0:T(8,128)}, u32[]{:S(2)}, u32[]{:S(2)}) collective-permute-start(f32[96,1152]{1,0:T(8,128)} %get-tuple-element.20), channel_id=1, source_target_pairs={{0,384},{192,576},{384,0},{576,192},{1,385},{193,577},{385,1},{577... | collective-permute-start | bytes 1327112 | tf_op jit(solution)/shard_map/ppermute | solution.py:84
  135.1 3.1 %collective-permute-start.13 = (f32[96,1152]{1,0:T(8,128)}, f32[96,1152]{1,0:T(8,128)}, u32[]{:S(2)}, u32[]{:S(2)}) collective-permute-start(f32[96,1152]{1,0:T(8,128)} %get-tuple-element.19), channel_id=1, source_target_pairs={{0,576},{192,0},{384,192},{576,384},{1,577},{193,1},{385,193},{577... | collective-permute-start | bytes 1327112 | tf_op jit(solution)/shard_map/ppermute | solution.py:84
  138.9 4.8 %all-to-all-start.1 = ((f32[4,1,256]{2,1,0:T(1,128)}), f32[4,1,256]{2,1,0:T(1,128)S(1)}, u32[]{:S(2)}, u32[]{:S(2)}) async-start(f32[4,1,256]{2,1,0:T(1,128)} %reshape.178), calls=%async_computation.1 | async-start | bytes 8192 | tf_op jit(solution)/shard_map/all_to_all | solution.py:221
  143.6 4.8 %all-to-all-done.1 = f32[4,1,256]{2,1,0:T(1,128)S(1)} async-done(((f32[4,1,256]{2,1,0:T(1,128)}), f32[4,1,256]{2,1,0:T(1,128)S(1)}, u32[]{:S(2)}, u32[]{:S(2)}) %all-to-all-start.1) | async-done | bytes 4128 | tf_op jit(solution)/shard_map/all_to_all | solution.py:221
  150.3 2.7 %collective-permute-done.12 = f32[96,1152]{1,0:T(8,128)} collective-permute-done((f32[96,1152]{1,0:T(8,128)}, f32[96,1152]{1,0:T(8,128)}, u32[]{:S(2)}, u32[]{:S(2)}) %collective-permute-start.12) | collective-permute-done | bytes 442400 | tf_op jit(solution)/shard_map/ppermute | solution.py:84
  153.0 2.3 %collective-permute-done.13 = f32[96,1152]{1,0:T(8,128)} collective-permute-done((f32[96,1152]{1,0:T(8,128)}, f32[96,1152]{1,0:T(8,128)}, u32[]{:S(2)}, u32[]{:S(2)}) %collective-permute-start.13) | collective-permute-done | bytes 442400 | tf_op jit(solution)/shard_map/ppermute | solution.py:84
  155.3 1.5 fusion.19
  157.5 4.8 %collective-permute-start.14 = (f32[32,1152]{1,0:T(8,128)}, f32[32,1152]{1,0:T(8,128)S(1)}, u32[]{:S(2)}, u32[]{:S(2)}) collective-permute-start(f32[32,1152]{1,0:T(8,128)} %get-tuple-element.21), channel_id=1, source_target_pairs={{0,64},{64,128},{128,0},{1,65},{65,129},{129,1},{2,66},{66,130},{1... | collective-permute-start | bytes 442376 | tf_op jit(solution)/shard_map/ppermute | solution.py:84
  162.2 4.4 %collective-permute-start.15 = (f32[32,1152]{1,0:T(8,128)S(1)}, f32[32,1152]{1,0:T(8,128)}, u32[]{:S(2)}, u32[]{:S(2)}) collective-permute-start(f32[32,1152]{1,0:T(8,128)S(1)} %get-tuple-element.22), channel_id=1, source_target_pairs={{0,128},{64,0},{128,64},{1,129},{65,1},{129,65},{2,130},{66,2},{13... | collective-permute-start | bytes 442376 | tf_op jit(solution)/shard_map/ppermute | solution.py:84
  166.6 5.5 %all-to-all-start.2 = ((f32[8,1,32]{2,1,0:T(1,128)}), f32[8,1,32]{2,1,0:T(1,128)S(1)}, u32[]{:S(2)}, u32[]{:S(2)}) async-start(f32[8,1,32]{2,1,0:T(1,128)} %bitcast.17), calls=%async_computation.2 | async-start | bytes 8192 | tf_op jit(solution)/shard_map/all_to_all | solution.py:228
  172.2 6.9 %all-to-all-done.2 = f32[8,1,32]{2,1,0:T(1,128)S(1)} async-done(((f32[8,1,32]{2,1,0:T(1,128)}), f32[8,1,32]{2,1,0:T(1,128)S(1)}, u32[]{:S(2)}, u32[]{:S(2)}) %all-to-all-start.2) | async-done | bytes 1056 | tf_op jit(solution)/shard_map/all_to_all | solution.py:228
  179.6 3.1 %collective-permute-done.15 = f32[32,1152]{1,0:T(8,128)} collective-permute-done((f32[32,1152]{1,0:T(8,128)S(1)}, f32[32,1152]{1,0:T(8,128)}, u32[]{:S(2)}, u32[]{:S(2)}) %collective-permute-start.15) | collective-permute-done | bytes 147488 | tf_op jit(solution)/shard_map/ppermute | solution.py:84
  182.7 1.1 fusion.29
  (75 shorter events, 18.2 us)
Async XLA Ops:
  7.2 20.2 %copy-start = (bf16[1152,1152]{1,0:T(8,128)(2,1)S(1)}, bf16[1152,1152]{1,0:T(8,128)(2,1)}, u32[]{:S(2)}) copy-start(bf16[1152,1152]{1,0:T(8,128)(2,1)} %param.13) | copy-start | bytes 7962628
  7.2 96.8 %all-gather.2.cloned.1.call-start = ((), (), s32[]{:S(2)}) async-start(), calls=%async_computation.3 | async-start | bytes 1843200 | tf_op jit(solution)/shard_map/all_gather | solution.py:142
  10.0 35.7 %collective-permute-start.1 = (bf16[32,1152]{1,0:T(8,128)(2,1)S(1)}, bf16[32,1152]{1,0:T(8,128)(2,1)S(1)}, u32[]{:S(2)}, u32[]{:S(2)}) collective-permute-start(bf16[32,1152]{1,0:T(8,128)(2,1)S(1)} %get-tuple-element.17), channel_id=1, source_target_pairs={{0,1},{1,2},{2,3},{3,0},{4,5},{5,6},{6,7},{7,4},{8,9},{9,10},{10,1... | collective-permute-start | bytes 221192 | tf_op jit(solution)/shard_map/ppermute | solution.py:84
  14.8 34.1 %collective-permute-start = (bf16[32,1152]{1,0:T(8,128)(2,1)S(1)}, bf16[32,1152]{1,0:T(8,128)(2,1)S(1)}, u32[]{:S(2)}, u32[]{:S(2)}) collective-permute-start(bf16[32,1152]{1,0:T(8,128)(2,1)S(1)} %get-tuple-element.17), channel_id=1, source_target_pairs={{0,3},{1,0},{2,1},{3,2},{4,7},{5,4},{6,5},{7,6},{8,11},{9,8},{10,9... | collective-permute-start | bytes 221192 | tf_op jit(solution)/shard_map/ppermute | solution.py:84
  35.9 39.3 %all-to-all-start = ((bf16[32,2,576]{2,1,0:T(2,128)(2,1)}), bf16[32,2,576]{2,1,0:T(2,128)(2,1)S(1)}, u32[]{:S(2)}, u32[]{:S(2)}) async-start(bf16[32,2,576]{2,1,0:T(2,128)(2,1)} %reshape.176), calls=%async_computation | async-start | bytes 163840 | tf_op jit(solution)/shard_map/all_to_all | solution.py:164
  45.7 8.6 %collective-permute-start.2 = (bf16[32,1152]{1,0:T(8,128)(2,1)S(1)}, bf16[32,1152]{1,0:T(8,128)(2,1)S(1)}, u32[]{:S(2)}, u32[]{:S(2)}) collective-permute-start(bf16[32,1152]{1,0:T(8,128)(2,1)S(1)} %collective-permute-done.1), channel_id=1, source_target_pairs={{0,1},{1,2},{2,3},{3,0},{4,5},{5,6},{6,7},{7,4},{8,9},{9,10},{10,1... | collective-permute-start | bytes 221192 | tf_op jit(solution)/shard_map/ppermute | solution.py:84
  55.0 8.9 %collective-permute-start.6 = (bf16[128,1152]{1,0:T(8,128)(2,1)}, bf16[128,1152]{1,0:T(8,128)(2,1)S(1)}, u32[]{:S(2)}, u32[]{:S(2)}) collective-permute-start(bf16[128,1152]{1,0:T(8,128)(2,1)} %pad_maximum_fusion), channel_id=1, source_target_pairs={{0,4},{4,8},{8,12},{12,16},{16,20},{20,24},{24,28},{28,0},{1,5},{5... | collective-permute-start | bytes 884744 | tf_op jit(solution)/shard_map/ppermute | solution.py:84
  59.6 7.9 %collective-permute-start.3 = (bf16[128,1152]{1,0:T(8,128)(2,1)}, bf16[128,1152]{1,0:T(8,128)(2,1)}, u32[]{:S(2)}, u32[]{:S(2)}) collective-permute-start(bf16[128,1152]{1,0:T(8,128)(2,1)} %pad_maximum_fusion), channel_id=1, source_target_pairs={{0,28},{4,0},{8,4},{12,8},{16,12},{20,16},{24,20},{28,24},{1,29},{... | collective-permute-start | bytes 884744 | tf_op jit(solution)/shard_map/ppermute | solution.py:84
  63.9 8.8 %collective-permute-start.7 = (bf16[128,1152]{1,0:T(8,128)(2,1)S(1)}, bf16[128,1152]{1,0:T(8,128)(2,1)}, u32[]{:S(2)}, u32[]{:S(2)}) collective-permute-start(bf16[128,1152]{1,0:T(8,128)(2,1)S(1)} %collective-permute-done.6), channel_id=1, source_target_pairs={{0,4},{4,8},{8,12},{12,16},{16,20},{20,24},{24,28},{28,0},{1,5},{5... | collective-permute-start | bytes 884744 | tf_op jit(solution)/shard_map/ppermute | solution.py:84
  67.5 8.4 %collective-permute-start.4 = (bf16[128,1152]{1,0:T(8,128)(2,1)}, bf16[128,1152]{1,0:T(8,128)(2,1)}, u32[]{:S(2)}, u32[]{:S(2)}) collective-permute-start(bf16[128,1152]{1,0:T(8,128)(2,1)} %collective-permute-done.3), channel_id=1, source_target_pairs={{0,28},{4,0},{8,4},{12,8},{16,12},{20,16},{24,20},{28,24},{1,29},{... | collective-permute-start | bytes 884744 | tf_op jit(solution)/shard_map/ppermute | solution.py:84
  72.7 10.0 %collective-permute-start.8 = (bf16[128,1152]{1,0:T(8,128)(2,1)}, bf16[128,1152]{1,0:T(8,128)(2,1)}, u32[]{:S(2)}, u32[]{:S(2)}) collective-permute-start(bf16[128,1152]{1,0:T(8,128)(2,1)} %collective-permute-done.7), channel_id=1, source_target_pairs={{0,4},{4,8},{8,12},{12,16},{16,20},{20,24},{24,28},{28,0},{1,5},{5... | collective-permute-start | bytes 884744 | tf_op jit(solution)/shard_map/ppermute | solution.py:84
  75.9 10.5 %collective-permute-start.5 = (bf16[128,1152]{1,0:T(8,128)(2,1)}, bf16[128,1152]{1,0:T(8,128)(2,1)S(1)}, u32[]{:S(2)}, u32[]{:S(2)}) collective-permute-start(bf16[128,1152]{1,0:T(8,128)(2,1)} %collective-permute-done.4), channel_id=1, source_target_pairs={{0,28},{4,0},{8,4},{12,8},{16,12},{20,16},{24,20},{28,24},{1,29},{... | collective-permute-start | bytes 884744 | tf_op jit(solution)/shard_map/ppermute | solution.py:84
  82.6 9.3 %collective-permute-start.9 = (bf16[128,1152]{1,0:T(8,128)(2,1)}, bf16[128,1152]{1,0:T(8,128)(2,1)S(1)}, u32[]{:S(2)}, u32[]{:S(2)}) collective-permute-start(bf16[128,1152]{1,0:T(8,128)(2,1)} %collective-permute-done.8), channel_id=1, source_target_pairs={{0,4},{4,8},{8,12},{12,16},{16,20},{20,24},{24,28},{28,0},{1,5},{5... | collective-permute-start | bytes 884744 | tf_op jit(solution)/shard_map/ppermute | solution.py:84
  103.9 2.2 %copy-start.5 = (bf16[1056,1152]{1,0:T(8,128)(2,1)S(1)}, bf16[1056,1152]{1,0:T(8,128)(2,1)}, u32[]{:S(2)}) copy-start(bf16[1056,1152]{1,0:T(8,128)(2,1)} %constant_dynamic-update-slice_fusion.3) | copy-start | bytes 7299076
  115.1 1.8 copy-start.2
  118.2 5.9 %collective-permute-start.10 = (f32[384,1152]{1,0:T(8,128)}, f32[384,1152]{1,0:T(8,128)}, u32[]{:S(2)}, u32[]{:S(2)}) collective-permute-start(f32[384,1152]{1,0:T(8,128)} %dynamic-slice_bitcast_fusion), channel_id=1, source_target_pairs={{0,32},{32,0},{1,33},{33,1},{2,34},{34,2},{3,35},{35,3},{4,36},{36... | collective-permute-start | bytes 5308424 | tf_op jit(solution)/shard_map/ppermute | solution.py:84
  126.3 1.2 copy-start.1
  127.5 55.2 %copy-start.3 = (bf16[32,1152]{1,0:T(8,128)(2,1)S(1)}, bf16[32,1152]{1,0:T(8,128)(2,1)}, u32[]{:S(2)}) copy-start(bf16[32,1152]{1,0:T(8,128)(2,1)} %param.16) | copy-start | bytes 221188
  128.6 21.7 %collective-permute-start.11 = (f32[96,1152]{1,0:T(8,128)}, f32[96,1152]{1,0:T(8,128)S(1)}, u32[]{:S(2)}, u32[]{:S(2)}) collective-permute-start(f32[96,1152]{1,0:T(8,128)} %get-tuple-element.18), channel_id=1, source_target_pairs={{0,192},{192,384},{384,576},{576,0},{1,193},{193,385},{385,577},{5... | collective-permute-start | bytes 1327112 | tf_op jit(solution)/shard_map/ppermute | solution.py:84
  130.8 22.2 %collective-permute-start.12 = (f32[96,1152]{1,0:T(8,128)}, f32[96,1152]{1,0:T(8,128)}, u32[]{:S(2)}, u32[]{:S(2)}) collective-permute-start(f32[96,1152]{1,0:T(8,128)} %get-tuple-element.20), channel_id=1, source_target_pairs={{0,384},{192,576},{384,0},{576,192},{1,385},{193,577},{385,1},{577... | collective-permute-start | bytes 1327112 | tf_op jit(solution)/shard_map/ppermute | solution.py:84
  135.1 20.2 %collective-permute-start.13 = (f32[96,1152]{1,0:T(8,128)}, f32[96,1152]{1,0:T(8,128)}, u32[]{:S(2)}, u32[]{:S(2)}) collective-permute-start(f32[96,1152]{1,0:T(8,128)} %get-tuple-element.19), channel_id=1, source_target_pairs={{0,576},{192,0},{384,192},{576,384},{1,577},{193,1},{385,193},{577... | collective-permute-start | bytes 1327112 | tf_op jit(solution)/shard_map/ppermute | solution.py:84
  138.9 9.6 %all-to-all-start.1 = ((f32[4,1,256]{2,1,0:T(1,128)}), f32[4,1,256]{2,1,0:T(1,128)S(1)}, u32[]{:S(2)}, u32[]{:S(2)}) async-start(f32[4,1,256]{2,1,0:T(1,128)} %reshape.178), calls=%async_computation.1 | async-start | bytes 8192 | tf_op jit(solution)/shard_map/all_to_all | solution.py:221
  150.3 2.7 %copy-start.4 = (f32[96,1152]{1,0:T(8,128)}, f32[96,1152]{1,0:T(8,128)S(1)}, u32[]{:S(2)}) copy-start(f32[96,1152]{1,0:T(8,128)S(1)} %collective-permute-done.11) | copy-start | bytes 1327108
  157.5 22.2 %collective-permute-start.14 = (f32[32,1152]{1,0:T(8,128)}, f32[32,1152]{1,0:T(8,128)S(1)}, u32[]{:S(2)}, u32[]{:S(2)}) collective-permute-start(f32[32,1152]{1,0:T(8,128)} %get-tuple-element.21), channel_id=1, source_target_pairs={{0,64},{64,128},{128,0},{1,65},{65,129},{129,1},{2,66},{66,130},{1... | collective-permute-start | bytes 442376 | tf_op jit(solution)/shard_map/ppermute | solution.py:84
  162.2 20.5 %collective-permute-start.15 = (f32[32,1152]{1,0:T(8,128)S(1)}, f32[32,1152]{1,0:T(8,128)}, u32[]{:S(2)}, u32[]{:S(2)}) collective-permute-start(f32[32,1152]{1,0:T(8,128)S(1)} %get-tuple-element.22), channel_id=1, source_target_pairs={{0,128},{64,0},{128,64},{1,129},{65,1},{129,65},{2,130},{66,2},{13... | collective-permute-start | bytes 442376 | tf_op jit(solution)/shard_map/ppermute | solution.py:84
  166.6 12.4 %all-to-all-start.2 = ((f32[8,1,32]{2,1,0:T(1,128)}), f32[8,1,32]{2,1,0:T(1,128)S(1)}, u32[]{:S(2)}, u32[]{:S(2)}) async-start(f32[8,1,32]{2,1,0:T(1,128)} %bitcast.17), calls=%async_computation.2 | async-start | bytes 8192 | tf_op jit(solution)/shard_map/all_to_all | solution.py:228
Sparse Core Ops, SparseCore 0:
  23.1 80.7 all-gather.1
